TPU v7x, 256 devices: a whole 4x4x8 slice. The times are simulated.
256 devices in a mesh: dp: 32 (over z, x_lo, core), factor: 8 (over y, x_hi).
Axes of the slice: x: 4 (x_hi: 2, x_lo: 2; x = x_hi * 2 + x_lo), y: 4, z: 8, core: 2. Of those that a mesh axis runs over, the one named last changes fastest.
Arguments:
- activations: bfloat16 [65536, 14336], P('dp', 'factor'), may hold values from -6 to 6
- out_grads: bfloat16 [65536, 4096], P('dp', 'factor'), may hold values from -6 to 6
- proj_in: bfloat16 [14336, 256], P('factor'), may hold values from -0.046875 to 0.046875
- proj_out: bfloat16 [4096, 256], P('factor'), may hold values from -0.09375 to 0.09375
- basis_in: bfloat16 [256, 256], replicated, may hold values from -0.375 to 0.375
- basis_out: bfloat16 [256, 256], replicated, may hold values from -0.375 to 0.375
- eigen_values: float32 [256, 256], P('factor'), may hold values from 0.01 to 10
- query_in: bfloat16 [256, 8, 256], P('dp'), may hold values from -3 to 3
- query_out: bfloat16 [256, 8, 256], P('dp'), may hold values from -3 to 3
- lengths: int32 [32, 16], P('dp'), may hold values from 1 to 256, 2048 in all within a row
- continues: int32 [32], replicated, may hold values from 0 to 1, as said below
- owners: int32 [512, 1], replicated, may hold values from 0 to 31; in each aligned block of 512 rows (0 to 511, 512 to 1023, ...) at most 32 rows name the same one
Outputs:
- influence: float32 [1024, 256], P('dp')
Inputs may be any that keep to these rules, and one draw needn't show every extreme that they name: `lengths`: each row sums to 2048. `continues`: the flags of sequences 0, 15, 16 and 30 are 1; the flag of the last sequence is not read. `owners`: no dp index owns more than 32 document numbers, and one owns exactly 32.
All inputs are finite; a program needn't handle non-finite values.
Results may differ from a plain program's by a relative error of at most 0.0027.
Values may be sent and summed in bfloat16 or wider, within the bound.
No kernel may reach another device: no remote copies, remote signals or barrier semaphores. Data moves between devices by JAX's collectives and lax.ppermute only.
A program may use at most 64 MiB of HBM per device.

v0:
```python
import jax
import jax.numpy as jnp
from jax import lax
from jax.sharding import PartitionSpec as P

OWN_CAP = 32


DAMPING = 0.1
EPSILON = 1e-06


def from_behind(block, axis, distance):
    devices = range(lax.axis_size(axis))
    route = [(i - distance, i) for i in devices if i - distance in devices]
    return lax.ppermute(block, axis, route)


def per_device(
    activations,
    out_grads,
    proj_in,
    proj_out,
    basis_in,
    basis_out,
    eigen_values,
    query_in,
    query_out,
    lengths,
    continues,
    owners,
):
    tokens_here = activations.shape[0]
    pieces = lengths.shape[1]
    rank_slice = eigen_values.shape[0]
    rank_in = basis_in.shape[0]
    factor_index = lax.axis_index("factor")
    data_index = lax.axis_index("dp")
    data_count = lax.axis_size("dp")
    highest = lax.Precision.HIGHEST
    in_part = jnp.dot(activations, proj_in, preferred_element_type=jnp.float32)
    out_part = jnp.dot(out_grads, proj_out, preferred_element_type=jnp.float32)
    basis_in_wide = basis_in.astype(jnp.float32)
    basis_out_wide = basis_out.astype(jnp.float32)
    rot_in = lax.psum(jnp.dot(in_part, basis_in_wide, precision=highest), "factor")
    rot_out_rows = lax.psum_scatter(
        lax.dot_general(basis_out_wide, out_part, (((0,), (1,)), ((), ())), precision=highest),
        "factor",
        scatter_dimension=0,
        tiled=True,
    )
    piece_lengths = lengths[0]
    piece_ends = jnp.cumsum(piece_lengths)
    piece_starts = piece_ends - piece_lengths
    position = jnp.arange(tokens_here, dtype=jnp.int32)[:, None]
    member = ((position >= piece_starts[None, :]) & (position < piece_ends[None, :])).astype(
        jnp.float32
    )
    stacked = (member[:, :, None] * rot_out_rows.T[:, None, :]).reshape(
        tokens_here, pieces * rank_slice
    )
    grad_rows = lax.dot_general(stacked, rot_in, (((0,), (0,)), ((), ())), precision=highest)
    grad_rows = grad_rows.reshape(pieces, rank_slice * rank_in)
    preceding = from_behind(grad_rows[pieces - 1].astype(jnp.bfloat16), "dp", 1).astype(jnp.float32)
    joined_next = jnp.where(data_index < data_count - 1, continues[data_index], 0).astype(
        jnp.float32
    )
    joined_prev = jnp.where(data_index > 0, continues[jnp.maximum(data_index - 1, 0)], 0).astype(
        jnp.float32
    )
    grad_rows = grad_rows.at[0].add(joined_prev * preceding)
    grad_rows = grad_rows.at[pieces - 1].multiply(1.0 - joined_next)
    scale = (1.0 / (eigen_values + DAMPING)).reshape(-1)
    self_part = jnp.sum(grad_rows * grad_rows * scale[None, :], axis=1)
    grad_low = grad_rows.astype(jnp.bfloat16)
    basis_cut = lax.dynamic_slice_in_dim(basis_out_wide, factor_index * rank_slice, rank_slice, 1)
    q_out = jnp.einsum("qtk,kl->qtl", query_out.astype(jnp.float32), basis_cut, precision=highest)
    q_in = jnp.einsum("qtk,kl->qtl", query_in.astype(jnp.float32), basis_in_wide, precision=highest)
    outer = jnp.einsum("qti,qtj->qij", q_out, q_in, precision=highest)
    part = lax.dot_general(
        grad_low,
        lax.all_gather(
            (outer.reshape(query_in.shape[0], rank_slice * rank_in) * scale[None, :]).astype(
                jnp.bfloat16
            ),
            "dp",
            axis=0,
            tiled=True,
        ),
        (((1,), (1,)), ((), ())),
        preferred_element_type=jnp.float32,
    )
    own_all = owners[:, 0]
    doc_count = own_all.shape[0]
    mine_ids = data_index * pieces + jnp.arange(pieces, dtype=jnp.int32)
    own_mine = lax.dynamic_slice_in_dim(own_all, data_index * pieces, pieces)
    earlier = (own_all[None, :] == own_mine[:, None]) & (
        jnp.arange(doc_count, dtype=jnp.int32)[None, :] < mine_ids[:, None]
    )
    rank_mine = jnp.sum(earlier.astype(jnp.int32), axis=1)
    slot_index = own_mine * OWN_CAP + rank_mine
    slot_rows = data_count * OWN_CAP
    placing = (jnp.arange(slot_rows, dtype=jnp.int32)[:, None] == slot_index[None, :]).astype(
        jnp.float32
    )
    raw_total, self_total = lax.psum((part, self_part), "factor")
    relative = raw_total / jnp.sqrt(self_total + EPSILON)[:, None]
    placed = jnp.dot(placing, relative, precision=highest)
    return lax.psum_scatter(placed, "dp", scatter_dimension=0, tiled=True)


def solution(mesh):
    placed = (
        P("dp", "factor"),
        P("dp", "factor"),
        P("factor", None),
        P("factor", None),
        P(),
        P(),
        P("factor", None),
        P("dp", None, None),
        P("dp", None, None),
        P("dp", None),
        P(),
        P(),
    )
    return jax.shard_map(
        per_device, mesh=mesh, in_specs=placed, out_specs=P("dp", None), check_vma=False
    )
```

profile of v0, /device:TPU:1, one launch (start us, length us, event | category | flops | bytes accessed | tf_op | source)
XLA Modules:
  0.0 391.8 jit_solution(14859609049050436812)
XLA Ops:
  7.4 1.6 copy-done
  9.0 1.7 fusion.17
  10.6 2.4 convolution_bitcast_fusion
  13.1 2.9 copy.22
  16.1 1.1 copy-done.8
  17.2 5.3 %fusion.18 = f32[2048,256]{1,0:T(8,128)S(1)} fusion(bf16[2048,1792]{1,0:T(8,128)(2,1)} %param.16, bf16[1792,256]{1,0:T(8,128)(2,1)S(1)} %copy-done.8), kind=kOutput, calls=%fused_computation.39 | convolution fusion | flops 1879048192 | bytes 10354688 | tf_op jit(solution)/shard_map/dot_general | solution.py:41
  22.5 2.4 fusion.19
  25.0 0.6 copy-done.4
  25.7 0.1 fusion.4
  25.8 0.2 convolution_bitcast_fusion.2
  26.0 0.5 convolution_bitcast_fusion.1
  26.5 0.2 copy.28
  26.7 0.7 multiply_convert_fusion
  27.5 0.7 fusion.16
  28.8 0.1 copy.19
  28.9 0.1 reduce.4
  29.8 0.2 convert_reduce_fusion
  30.0 0.1 fusion.7
  30.1 69.6 %reduce-scatter.7.cloned.1.call-done = f32[32,2048]{1,0:T(8,128)} async-done(((f32[256,2048]{1,0:T(8,128)}), f32[32,2048]{1,0:T(8,128)}) %reduce-scatter.7.cloned.1.call-update) | async-done | bytes 262160
  99.7 3.4 broadcast_multiply_fusion
  103.1 111.1 %all-reduce.3.cloned.1.call-done = f32[2048,256]{1,0:T(8,128)} async-done(((f32[2048,256]{1,0:T(8,128)}), f32[2048,256]{1,0:T(8,128)}) %all-reduce.3.cloned.1.call-update) | async-done | bytes 2097168 | tf_op jit(solution)/shard_map/psum | solution.py:45
  214.2 6.0 %fusion.20 = f32[512,256]{1,0:T(8,128)S(1)} fusion(f32[2048,512]{0,1:T(8,128)} %bitcast.57, f32[2048,256]{1,0:T(8,128)} %all-reduce.3.cloned.1.call-done), kind=kOutput, calls=%fused_computation.41 | convolution fusion | flops 3221225472 | bytes 6815744 | tf_op jit(solution)/shard_map/dot_general | solution.py:62
  220.3 3.6 collective-permute-start
  223.8 0.1 reshape.133
  224.0 0.7 collective-permute-done
  224.7 0.1 scatter-add.4
  224.9 0.2 scatter-mul.4
  225.0 0.2 multiply_reduce_fusion
  225.3 3.4 fusion.1
  228.6 32.8 %all-reduce = (f32[16,256]{1,0:T(8,128)S(1)}, f32[16]{0:T(128)S(1)}) all-reduce(f32[16,256]{1,0:T(8,128)S(1)} %fusion.1, f32[16]{0:T(128)S(1)} %multiply_reduce_fusion), channel_id=1, replica_groups=mesh['dp'=32,'factor'=8] {'factor'}, use_global_device_ids=true, to_apply=%region_4.5 | all-reduce | flops 4112 | bytes 32896 | tf_op jit(solution)/shard_map/psum | solution.py:106
  261.4 1.6 fusion
  263.1 121.3 %reduce-scatter.5.cloned.1.call-done = f32[32,256]{1,0:T(8,128)} async-done(((f32[1024,256]{1,0:T(8,128)}), f32[32,256]{1,0:T(8,128)}) %reduce-scatter.5.cloned.1.call-update) | async-done | bytes 32784 | tf_op jit(solution)/shard_map/reduce_scatter | solution.py:109
  (40 shorter events, 0.6 us)
Async XLA Ops:
  7.4 1.6 copy-start
  7.4 3.3 copy-start.2
  7.4 92.3 %reduce-scatter.7.cloned.1.call-start = ((), (), s32[]{:S(2)}) async-start(), calls=%async_computation.5 | async-start | bytes 2359296
  16.0 1.2 copy-start.8
  16.0 6.5 %copy-start.1 = (bf16[256,256]{1,0:T(8,128)(2,1)S(1)}, bf16[256,256]{1,0:T(8,128)(2,1)}, u32[]{:S(2)}) copy-start(bf16[256,256]{1,0:T(8,128)(2,1)} %param.20) | copy-start | bytes 393220
  16.0 198.2 %all-reduce.3.cloned.1.call-start = ((), (), s32[]{:S(2)}) async-start(), calls=%async_computation.2 | async-start | bytes 4194304 | tf_op jit(solution)/shard_map/psum | solution.py:45
  24.9 0.8 copy-start.4
  24.9 0.8 copy-start.3
  24.9 1.0 copy-start.9
  24.9 2.6 copy-start.6
  24.9 3.9 copy-start.7
  24.9 4.8 %copy-start.5 = (s32[512,1]{0,1:T(1,128)S(1)}, s32[512,1]{0,1:T(1,128)}, u32[]{:S(2)}) copy-start(s32[512,1]{0,1:T(1,128)} %param.27) | copy-start | bytes 6148
  24.9 200.3 %all-gather.2.cloned.1.call-start = ((), (), s32[]{:S(2)}) async-start(), calls=%async_computation.3 | async-start | bytes 4325376 | tf_op jit(solution)/shard_map/all_gather | solution.py:82
  27.4 357.0 %reduce-scatter.5.cloned.1.call-start = ((), (), s32[]{:S(2)}) async-start(), calls=%async_computation.4 | async-start | bytes 1081344 | tf_op jit(solution)/shard_map/reduce_scatter | solution.py:109
  220.3 4.4 %collective-permute-start = (bf16[8192]{0:T(1024)(128)(2,1)S(1)}, bf16[8192]{0:T(1024)(128)(2,1)S(1)}, u32[]{:S(2)}, u32[]{:S(2)}) collective-permute-start(bf16[8192]{0:T(1024)(128)(2,1)S(1)} %bitcast.64), channel_id=1, source_target_pairs={{0,8},{8,16},{16,24},{24,32},{32,40},{40,48},{48,56},{56,64},{64,7... | collective-permute-start | bytes 49160 | tf_op jit(solution)/shard_map/ppermute | solution.py:16
Sparse Core Ops, SparseCore 0:
  16.1 83.5 reduce-scatter.6
  102.3 111.8 all-reduce.2
Sparse Core Ops, SparseCore 1:
  27.5 71.3 all-gather.1
  263.2 121.2 reduce-scatter.4
where the time goes:
time: 395 us; the launch traced here: 392 us
  waiting for transfers between devices  303 us (77%)
  blocking collectives  32.8 us (8%)
  matrix products  23.6 us (6%)
  between operations  16.4 us (4%)
  local copies, waits for them, and re-layouts  7.7 us (2%)
  other arithmetic  4.89 us (1%)
    reduce_scatter x1, waiting for transfers between devices, per_device(): return lax.psum_scatter(placed, 'dp', scatter_dimension=0, tiled=True)  121 us
    psum x1, waiting for transfers between devices, per_device(): lax.psum(jnp.dot(in_part, basis_in_wide, precision=highest), 'factor')  111 us
    unnamed x5, waiting for transfers between devices  69.6 us
    psum x1, blocking collectives, per_device(): raw_total, self_total = lax.psum((part, self_part), 'factor')  32.8 us
  transfers between devices with their start and end apart: 5, of which 4 were waited for; matrix products, arithmetic and copies ran while one was open for 5% of the time, Pallas kernels for 0%

commit v1 on v0

v1 whole, which is shorter than its diff:
```python
import jax
import jax.numpy as jnp
from jax import lax
from jax.sharding import PartitionSpec as P

OWN_CAP = 32


DAMPING = 0.1
EPSILON = 1e-06


def from_behind(block, axis, distance):
    devices = range(lax.axis_size(axis))
    route = [(i - distance, i) for i in devices if i - distance in devices]
    return lax.ppermute(block, axis, route)


def butterfly_sum(block, axis):
    size = lax.axis_size(axis)
    step = 1
    while step < size:
        block = block + lax.ppermute(block, axis, [(i, i ^ step) for i in range(size)])
        step *= 2
    return block


def butterfly_gather(block, axis):
    size = lax.axis_size(axis)
    me = lax.axis_index(axis)
    step = 1
    while step < size:
        other = lax.ppermute(block, axis, [(i, i ^ step) for i in range(size)])
        upper = (me // step) % 2 == 1
        block = jnp.where(
            upper,
            jnp.concatenate([other, block], axis=0),
            jnp.concatenate([block, other], axis=0),
        )
        step *= 2
    return block


def per_device(
    activations,
    out_grads,
    proj_in,
    proj_out,
    basis_in,
    basis_out,
    eigen_values,
    query_in,
    query_out,
    lengths,
    continues,
    owners,
):
    tokens_here = activations.shape[0]
    pieces = lengths.shape[1]
    rank_slice = eigen_values.shape[0]
    rank_in = basis_in.shape[0]
    rank_out = basis_out.shape[0]
    factor_index = lax.axis_index("factor")
    factor_count = lax.axis_size("factor")
    data_index = lax.axis_index("dp")
    data_count = lax.axis_size("dp")
    highest = lax.Precision.HIGHEST
    chunk = tokens_here // factor_count

    queries = lax.all_gather(jnp.concatenate([query_in, query_out], axis=2), "dp", axis=0, tiled=True)

    in_part = jnp.dot(activations, proj_in, preferred_element_type=jnp.float32)
    out_part = jnp.dot(out_grads, proj_out, preferred_element_type=jnp.float32)
    stacked_parts = jnp.concatenate([in_part, out_part], axis=1)
    gathered_parts = lax.all_to_all(stacked_parts, "factor", 0, 0, tiled=True)
    chunk_sums = jnp.sum(gathered_parts.reshape(factor_count, chunk, rank_in + rank_out), axis=0)
    basis_in_wide = basis_in.astype(jnp.float32)
    basis_out_wide = basis_out.astype(jnp.float32)
    rot_in_chunk = jnp.dot(chunk_sums[:, :rank_in], basis_in_wide, precision=highest)
    rot_out_chunk = jnp.dot(chunk_sums[:, rank_in:], basis_out_wide, precision=highest)
    out_blocks = rot_out_chunk.reshape(chunk, factor_count, rank_slice).transpose(1, 0, 2)
    sending = jnp.concatenate(
        [jnp.broadcast_to(rot_in_chunk[None], (factor_count, chunk, rank_in)), out_blocks], axis=2
    ).reshape(factor_count * chunk, rank_in + rank_slice)
    received = lax.all_to_all(sending, "factor", 0, 0, tiled=True)
    rot_in = received[:, :rank_in]
    rot_out_rows = received[:, rank_in:]

    piece_lengths = lengths[0]
    piece_ends = jnp.cumsum(piece_lengths)
    piece_starts = piece_ends - piece_lengths
    position = jnp.arange(tokens_here, dtype=jnp.int32)[:, None]
    member = ((position >= piece_starts[None, :]) & (position < piece_ends[None, :])).astype(
        jnp.float32
    )
    stacked = (member[:, :, None] * rot_out_rows[:, None, :]).reshape(
        tokens_here, pieces * rank_slice
    )
    grad_rows = lax.dot_general(stacked, rot_in, (((0,), (0,)), ((), ())), precision=highest)
    grad_rows = grad_rows.reshape(pieces, rank_slice * rank_in)
    preceding = from_behind(grad_rows[pieces - 1], "dp", 1)
    joined_next = jnp.where(data_index < data_count - 1, continues[data_index], 0).astype(
        jnp.float32
    )
    joined_prev = jnp.where(data_index > 0, continues[jnp.maximum(data_index - 1, 0)], 0).astype(
        jnp.float32
    )
    grad_rows = grad_rows.at[0].add(joined_prev * preceding)
    grad_rows = grad_rows.at[pieces - 1].multiply(1.0 - joined_next)
    scale = (1.0 / (eigen_values + DAMPING)).reshape(-1)
    self_part = jnp.sum(grad_rows * grad_rows * scale[None, :], axis=1)
    grad_low = grad_rows.astype(jnp.bfloat16)

    basis_cut = lax.dynamic_slice_in_dim(basis_out_wide, factor_index * rank_slice, rank_slice, 1)
    q_in = jnp.einsum(
        "qtk,kl->qtl", queries[:, :, :rank_in].astype(jnp.float32), basis_in_wide, precision=highest
    )
    q_out = jnp.einsum(
        "qtk,kl->qtl", queries[:, :, rank_in:].astype(jnp.float32), basis_cut, precision=highest
    )
    outer = jnp.einsum("qti,qtj->qij", q_out, q_in, precision=highest)
    query_grad = (outer.reshape(queries.shape[0], rank_slice * rank_in) * scale[None, :]).astype(
        jnp.bfloat16
    )
    part = lax.dot_general(
        grad_low, query_grad, (((1,), (1,)), ((), ())), preferred_element_type=jnp.float32
    )

    totals = butterfly_sum(jnp.concatenate([part, self_part[:, None]], axis=1), "factor")
    relative = totals[:, :-1] / jnp.sqrt(totals[:, -1:] + EPSILON)
    relative_all = butterfly_gather(relative, "dp")

    own_all = owners[:, 0]
    doc_count = own_all.shape[0]
    numbers = jnp.arange(doc_count, dtype=jnp.int32)
    earlier = (own_all[None, :] == own_all[:, None]) & (numbers[None, :] < numbers[:, None])
    rank_all = jnp.sum(earlier.astype(jnp.int32), axis=1)
    slots = jnp.arange(OWN_CAP, dtype=jnp.int32)[:, None]
    placing = ((own_all[None, :] == data_index) & (rank_all[None, :] == slots)).astype(jnp.float32)
    return jnp.dot(placing, relative_all, precision=highest)


def solution(mesh):
    placed = (
        P("dp", "factor"),
        P("dp", "factor"),
        P("factor", None),
        P("factor", None),
        P(),
        P(),
        P("factor", None),
        P("dp", None, None),
        P("dp", None, None),
        P("dp", None),
        P(),
        P(),
    )
    return jax.shard_map(
        per_device, mesh=mesh, in_specs=placed, out_specs=P("dp", None), check_vma=False
    )
```

time: 395 us -> 215 us (0.54)
  the two profiles are of different devices: /device:TPU:1 before, /device:TPU:96 now
where the time goes in v1:
time: 215 us
  waiting for transfers between devices  109 us (51%)
  starting transfers between devices  42 us (20%)
  matrix products  25.4 us (12%)
  local copies, waits for them, and re-layouts  16.8 us (8%)
  between operations  15.1 us (7%)
  other arithmetic  6.76 us (3%)
    all_to_all x1, waiting for transfers between devices, per_device(): gathered_parts = lax.all_to_all(stacked_parts, 'factor', 0, 0, tiled=True)  50.3 us
    ppermute x5, starting transfers between devices, butterfly_gather(): other = lax.ppermute(block, axis, [(i, i ^ step) for i in range(size)])  26.7 us
    all_to_all x1, waiting for transfers between devices, per_device(): received = lax.all_to_all(sending, 'factor', 0, 0, tiled=True)  20.7 us
    ppermute x5, waiting for transfers between devices, butterfly_gather(): other = lax.ppermute(block, axis, [(i, i ^ step) for i in range(size)])  19.9 us
    ppermute x3, waiting for transfers between devices, butterfly_sum(): lax.ppermute(block, axis, [(i, i ^ step) for i in range(size)])  12.9 us
    unnamed x35, local copies, waits for them, and re-layouts  11.2 us
    dot_general x1, matrix products, per_device(): outer = jnp.einsum('qti,qtj->qij', q_out, q_in, precision=highest)  7.07 us
    all_to_all x1, starting transfers between devices, per_device(): gathered_parts = lax.all_to_all(stacked_parts, 'factor', 0, 0, tiled=True)  7.06 us
  transfers between devices with their start and end apart: 12, of which 11 were waited for; matrix products, arithmetic and copies ran while one was open for 13% of the time, Pallas kernels for 0%

profile of v1, /device:TPU:96, one launch (start us, length us, event | category | flops | bytes accessed | tf_op | source)
XLA Modules:
  0.0 214.9 jit_solution(14173243660565642719)
XLA Ops:
  6.5 5.5 %fusion.37 = f32[2048,256]{0,1:T(8,128)S(1)} fusion(bf16[2048,1792]{1,0:T(8,128)(2,1)} %param.16, bf16[1792,256]{1,0:T(8,128)(2,1)} %param.18), kind=kOutput, calls=%fused_computation.63 | convolution fusion | flops 1879048192 | bytes 10354688 | tf_op jit(solution)/shard_map/dot_general | solution.py:72
  12.1 0.8 fusion.38
  13.3 2.3 %copy.52 = f32[64,8,8,256]{3,2,0,1:T(8,128)} copy(f32[64,8,8,256]{3,2,1,0:T(8,128)S(1)} %bitcast.52) | data formatting | bytes 8388608 | tf_op jit(solution)/shard_map/all_to_all | solution.py:75
  15.7 7.1 %all-to-all-start = ((f32[8,256,512]{1,2,0:T(8,128)}), f32[8,256,512]{1,2,0:T(8,128)}, u32[]{:S(2)}, u32[]{:S(2)}) async-start(f32[8,256,512]{1,2,0:T(8,128)} %bitcast.51), calls=%async_computation | async-start | bytes 8388608 | tf_op jit(solution)/shard_map/all_to_all | solution.py:75
  22.8 0.6 pad_maximum_fusion.2
  23.5 50.3 %all-to-all-done = f32[8,256,512]{1,2,0:T(8,128)} async-done(((f32[8,256,512]{1,2,0:T(8,128)}), f32[8,256,512]{1,2,0:T(8,128)}, u32[]{:S(2)}, u32[]{:S(2)}) %all-to-all-start) | async-done | bytes 4194336 | tf_op jit(solution)/shard_map/all_to_all | solution.py:75
  73.8 2.5 %reduce_sum.28 = f32[256,512]{0,1:T(8,128)S(1)} reduce(f32[8,256,512]{1,2,0:T(8,128)} %all-to-all-done, f32[]{:T(128)} %constant.156.clone.1), dimensions={0}, to_apply=%region_2.3 | reduce | flops 917504 | bytes 4718596 | tf_op jit(solution)/shard_map/reduce_sum | solution.py:76
  77.2 1.6 pad_maximum_fusion.1
  78.8 4.5 %all-to-all-start.1 = ((f32[8,256,288]{1,2,0:T(8,128)}), f32[8,256,288]{1,2,0:T(8,128)}, u32[]{:S(2)}, u32[]{:S(2)}) async-start(f32[8,256,288]{1,2,0:T(8,128)} %pad_maximum_fusion.1), calls=%async_computation.1 | async-start | bytes 4718592 | tf_op jit(solution)/shard_map/all_to_all | solution.py:85
  85.6 5.1 %all-gather.2.cloned.1.call-done = bf16[256,8,512]{2,1,0:T(8,128)(2,1)} async-done(((bf16[8,8,512]{2,1,0:T(8,128)(2,1)}), bf16[256,8,512]{2,1,0:T(8,128)(2,1)}) %all-gather.2.cloned.1.call-update) | async-done | bytes 2097168 | tf_op jit(solution)/shard_map/all_gather | solution.py:70
  90.6 1.9 fusion.6
  93.0 20.7 %all-to-all-done.1 = f32[8,256,288]{1,2,0:T(8,128)} async-done(((f32[8,256,288]{1,2,0:T(8,128)}), f32[8,256,288]{1,2,0:T(8,128)}, u32[]{:S(2)}, u32[]{:S(2)}) %all-to-all-start.1) | async-done | bytes 2359328 | tf_op jit(solution)/shard_map/all_to_all | solution.py:85
  113.7 1.9 copy.46
  116.2 3.5 %fusion.2 = f32[512,256]{1,0:T(8,128)S(1)} fusion(f32[2048,512]{0,1:T(8,128)S(1)} %bitcast.53, f32[2048,288]{0,1:T(8,128)S(1)} %bitcast.55), kind=kOutput, calls=%fused_computation.6 | convolution fusion | flops 3221225472 | bytes 6815744 | tf_op jit(solution)/shard_map/dot_general | solution.py:99
  119.7 2.1 collective-permute-start
  121.8 7.1 %fusion.39 = f32[256,32,256]{2,1,0:T(8,128)S(1)} fusion(f32[256,8,32]{2,1,0:T(8,128)S(1)} %fusion.6, f32[256,8,256]{2,1,0:T(8,128)S(1)} %fusion.4), kind=kOutput, calls=%fused_computation.65 | convolution fusion | flops 201326592 | bytes 10747904 | tf_op jit(solution)/shard_map/qti,qtj->qij/dot_general | solution.py:121
  128.9 11.0 %copy.49 = f32[32,8,32,256]{3,1,2,0:T(8,128)} copy(f32[32,8,32,256]{3,2,1,0:T(8,128)S(1)} %bitcast.50) | data formatting | bytes 16777216
  140.7 4.7 %fusion = f32[16,256]{1,0:T(8,128)S(1)} fusion(f32[256,8192]{1,0:T(8,128)} %bitcast.49, f32[8192]{0:T(1024)S(1)} %bitcast.58, f32[16,8192]{1,0:T(8,128)S(1)} %scatter-mul.4), kind=kOutput, calls=%fused_computation.1 | convolution fusion | flops 71434240 | bytes 8962048 | tf_op jit(solution)/shard_map/dot_general | solution.py:125
  145.5 0.8 collective-permute-start.1
  146.3 4.5 %collective-permute-done.1 = f32[16,257]{1,0:T(8,128)S(1)} collective-permute-done((f32[16,257]{1,0:T(8,128)S(1)}, f32[16,257]{1,0:T(8,128)S(1)}, u32[]{:S(2)}, u32[]{:S(2)}) %collective-permute-start.1) | collective-permute-done | bytes 16480 | tf_op jit(solution)/shard_map/ppermute | solution.py:23
  150.8 3.8 %collective-permute-done.2 = f32[16,257]{1,0:T(8,128)S(1)} collective-permute-done((f32[16,257]{1,0:T(8,128)S(1)}, f32[16,257]{1,0:T(8,128)S(1)}, u32[]{:S(2)}, u32[]{:S(2)}) %collective-permute-start.2) | collective-permute-done | bytes 16480 | tf_op jit(solution)/shard_map/ppermute | solution.py:23
  154.7 0.8 collective-permute-start.3
  155.5 4.5 %collective-permute-done.3 = f32[16,257]{1,0:T(8,128)S(1)} collective-permute-done((f32[16,257]{1,0:T(8,128)S(1)}, f32[16,257]{1,0:T(8,128)S(1)}, u32[]{:S(2)}, u32[]{:S(2)}) %collective-permute-start.3) | collective-permute-done | bytes 16480 | tf_op jit(solution)/shard_map/ppermute | solution.py:23
  160.3 1.2 collective-permute-done.4
  161.4 0.9 collective-permute-start.5
  162.3 3.0 %collective-permute-done.5 = f32[32,256]{1,0:T(8,128)S(1)} collective-permute-done((f32[32,256]{1,0:T(8,128)S(1)}, f32[32,256]{1,0:T(8,128)S(1)}, u32[]{:S(2)}, u32[]{:S(2)}) %collective-permute-start.5) | collective-permute-done | bytes 32800 | tf_op jit(solution)/shard_map/ppermute | solution.py:33
  165.5 4.2 %collective-permute-done.6 = f32[64,256]{1,0:T(8,128)S(1)} collective-permute-done((f32[64,256]{1,0:T(8,128)S(1)}, f32[64,256]{1,0:T(8,128)S(1)}, u32[]{:S(2)}, u32[]{:S(2)}) %collective-permute-start.6) | collective-permute-done | bytes 65568 | tf_op jit(solution)/shard_map/ppermute | solution.py:33
  169.7 5.2 %collective-permute-start.7 = (f32[128,256]{1,0:T(8,128)S(1)}, f32[128,256]{1,0:T(8,128)S(1)}, u32[]{:S(2)}, u32[]{:S(2)}) collective-permute-start(f32[128,256]{1,0:T(8,128)S(1)} %maximum_select_fusion.3), channel_id=1, source_target_pairs={{0,64},{8,72},{16,80},{24,88},{32,96},{40,104},{48,112},{56,120},{... | collective-permute-start | bytes 393224 | tf_op jit(solution)/shard_map/ppermute | solution.py:33
  174.9 4.6 %collective-permute-done.7 = f32[128,256]{1,0:T(8,128)S(1)} collective-permute-done((f32[128,256]{1,0:T(8,128)S(1)}, f32[128,256]{1,0:T(8,128)S(1)}, u32[]{:S(2)}, u32[]{:S(2)}) %collective-permute-start.7) | collective-permute-done | bytes 131104 | tf_op jit(solution)/shard_map/ppermute | solution.py:33
  179.6 20.4 %collective-permute-start.8 = (f32[256,256]{1,0:T(8,128)S(1)}, f32[256,256]{1,0:T(8,128)S(1)}, u32[]{:S(2)}, u32[]{:S(2)}) collective-permute-start(f32[256,256]{1,0:T(8,128)S(1)} %maximum_select_fusion.2), channel_id=1, source_target_pairs={{0,128},{8,136},{16,144},{24,152},{32,160},{40,168},{48,176},{56,1... | collective-permute-start | bytes 786440 | tf_op jit(solution)/shard_map/ppermute | solution.py:33
  200.2 6.9 %collective-permute-done.8 = f32[256,256]{1,0:T(8,128)S(1)} collective-permute-done((f32[256,256]{1,0:T(8,128)S(1)}, f32[256,256]{1,0:T(8,128)S(1)}, u32[]{:S(2)}, u32[]{:S(2)}) %collective-permute-start.8) | collective-permute-done | bytes 262176 | tf_op jit(solution)/shard_map/ppermute | solution.py:33
  207.1 0.9 fusion.9
  (73 shorter events, 4.9 us)
Async XLA Ops:
  6.5 5.5 %copy-start = (bf16[2048,512]{1,0:T(8,128)(2,1)S(1)}, bf16[2048,512]{1,0:T(8,128)(2,1)}, u32[]{:S(2)}) copy-start(bf16[2048,512]{1,0:T(8,128)(2,1)} %param.17) | copy-start | bytes 6291460
  6.5 5.5 %copy-start.8 = (bf16[512,256]{1,0:T(8,128)(2,1)S(1)}, bf16[512,256]{1,0:T(8,128)(2,1)}, u32[]{:S(2)}) copy-start(bf16[512,256]{1,0:T(8,128)(2,1)} %param.19) | copy-start | bytes 786436
  15.7 7.1 %copy-start.10 = (bf16[8,8,256]{2,1,0:T(8,128)(2,1)S(1)}, bf16[8,8,256]{2,1,0:T(8,128)(2,1)}, u32[]{:S(2)}) copy-start(bf16[8,8,256]{2,1,0:T(8,128)(2,1)} %param.24) | copy-start | bytes 98308
  15.7 7.1 %copy-start.11 = (bf16[8,8,256]{2,1,0:T(8,128)(2,1)S(1)}, bf16[8,8,256]{2,1,0:T(8,128)(2,1)}, u32[]{:S(2)}) copy-start(bf16[8,8,256]{2,1,0:T(8,128)(2,1)} %param.23) | copy-start | bytes 98308
  15.7 58.1 %all-to-all-start = ((f32[8,256,512]{1,2,0:T(8,128)}), f32[8,256,512]{1,2,0:T(8,128)}, u32[]{:S(2)}, u32[]{:S(2)}) async-start(f32[8,256,512]{1,2,0:T(8,128)} %bitcast.51), calls=%async_computation | async-start | bytes 8388608 | tf_op jit(solution)/shard_map/all_to_all | solution.py:75
  22.7 67.9 %all-gather.2.cloned.1.call-start = ((), (), s32[]{:S(2)}) async-start(), calls=%async_computation.2 | async-start | bytes 2162688 | tf_op jit(solution)/shard_map/all_gather | solution.py:70
  23.5 52.9 %copy-start.5 = (bf16[256,256]{1,0:T(8,128)(2,1)S(1)}, bf16[256,256]{1,0:T(8,128)(2,1)}, u32[]{:S(2)}) copy-start(bf16[256,256]{1,0:T(8,128)(2,1)} %param.20) | copy-start | bytes 393220
  23.5 53.2 %copy-start.6 = (bf16[256,256]{1,0:T(8,128)(2,1)S(1)}, bf16[256,256]{1,0:T(8,128)(2,1)}, u32[]{:S(2)}) copy-start(bf16[256,256]{1,0:T(8,128)(2,1)} %param.21) | copy-start | bytes 393220
  78.7 4.5 %copy-start.13 = (s32[32]{0:T(128)S(1)}, s32[32]{0:T(128)}, u32[]{:S(2)}) copy-start(s32[32]{0:T(128)} %param.26) | copy-start | bytes 388
  78.7 5.8 %copy-start.14 = (s32[1,16]{1,0:T(1,128)S(1)}, s32[1,16]{1,0:T(1,128)}, u32[]{:S(2)}) copy-start(s32[1,16]{1,0:T(1,128)} %param.25) | copy-start | bytes 196
  78.7 6.7 %copy-start.9 = (f32[32,256]{1,0:T(8,128)S(1)}, f32[32,256]{1,0:T(8,128)}, u32[]{:S(2)}) copy-start(f32[32,256]{1,0:T(8,128)} %param.22) | copy-start | bytes 98308
  78.7 11.9 %copy-start.7 = (bf16[256,256]{1,0:T(8,128)(2,1)S(1)}, bf16[256,256]{1,0:T(8,128)(2,1)}, u32[]{:S(2)}) copy-start(bf16[256,256]{1,0:T(8,128)(2,1)} %param.21) | copy-start | bytes 393220
  78.8 34.9 %all-to-all-start.1 = ((f32[8,256,288]{1,2,0:T(8,128)}), f32[8,256,288]{1,2,0:T(8,128)}, u32[]{:S(2)}, u32[]{:S(2)}) async-start(f32[8,256,288]{1,2,0:T(8,128)} %pad_maximum_fusion.1), calls=%async_computation.1 | async-start | bytes 4718592 | tf_op jit(solution)/shard_map/all_to_all | solution.py:85
  90.6 1.9 copy-start.4
  119.7 9.2 %copy-start.2 = (f32[512,256]{1,0:T(8,128)}, f32[512,256]{1,0:T(8,128)S(1)}, u32[]{:S(2)}) copy-start(f32[512,256]{1,0:T(8,128)S(1)} %fusion.2) | copy-start | bytes 1572868
  119.7 20.4 %collective-permute-start = (f32[8192]{0:T(1024)S(1)}, f32[8192]{0:T(1024)S(1)}, u32[]{:S(2)}, u32[]{:S(2)}) collective-permute-start(f32[8192]{0:T(1024)S(1)} %bitcast.61), channel_id=1, source_target_pairs={{0,8},{8,16},{16,24},{24,32},{32,40},{40,48},{48,56},{56,64},{64,7... | collective-permute-start | bytes 98312 | tf_op jit(solution)/shard_map/ppermute | solution.py:16
  128.9 11.0 %copy-start.3 = (f32[512,256]{1,0:T(8,128)S(1)}, f32[512,256]{1,0:T(8,128)}, u32[]{:S(2)}) copy-start(f32[512,256]{1,0:T(8,128)} %copy-done.2) | copy-start | bytes 1572868
  140.6 59.3 %copy-start.12 = (s32[512,1]{0,1:T(1,128)S(1)}, s32[512,1]{0,1:T(1,128)}, u32[]{:S(2)}) copy-start(s32[512,1]{0,1:T(1,128)} %param.27) | copy-start | bytes 6148
  140.6 67.4 %copy-start.1 = (bf16[2048,512]{1,0:T(8,128)(2,1)S(1)}, bf16[2048,512]{1,0:T(8,128)(2,1)}, u32[]{:S(2)}) copy-start(bf16[2048,512]{1,0:T(8,128)(2,1)} %param.17) | copy-start | bytes 6291460
  145.5 5.4 %collective-permute-start.1 = (f32[16,257]{1,0:T(8,128)S(1)}, f32[16,257]{1,0:T(8,128)S(1)}, u32[]{:S(2)}, u32[]{:S(2)}) collective-permute-start(f32[16,257]{1,0:T(8,128)S(1)} %pad_maximum_fusion.3), channel_id=1, source_target_pairs={{0,1},{1,0},{2,3},{3,2},{4,5},{5,4},{6,7},{7,6},{8,9},{9,8},{10,11... | collective-permute-start | bytes 49352 | tf_op jit(solution)/shard_map/ppermute | solution.py:23
  150.8 3.8 %collective-permute-start.2 = (f32[16,257]{1,0:T(8,128)S(1)}, f32[16,257]{1,0:T(8,128)S(1)}, u32[]{:S(2)}, u32[]{:S(2)}) collective-permute-start(f32[16,257]{1,0:T(8,128)S(1)} %fusion.35), channel_id=1, source_target_pairs={{0,2},{1,3},{2,0},{3,1},{4,6},{5,7},{6,4},{7,5},{8,10},{9,11},{10,... | collective-permute-start | bytes 49352 | tf_op jit(solution)/shard_map/ppermute | solution.py:23
  154.7 5.3 %collective-permute-start.3 = (f32[16,257]{1,0:T(8,128)S(1)}, f32[16,257]{1,0:T(8,128)S(1)}, u32[]{:S(2)}, u32[]{:S(2)}) collective-permute-start(f32[16,257]{1,0:T(8,128)S(1)} %add.71), channel_id=1, source_target_pairs={{0,4},{1,5},{2,6},{3,7},{4,0},{5,1},{6,2},{7,3},{8,12},{9,13},{10,... | collective-permute-start | bytes 49352 | tf_op jit(solution)/shard_map/ppermute | solution.py:23
  160.2 1.2 collective-permute-start.4
  161.4 3.9 %collective-permute-start.5 = (f32[32,256]{1,0:T(8,128)S(1)}, f32[32,256]{1,0:T(8,128)S(1)}, u32[]{:S(2)}, u32[]{:S(2)}) collective-permute-start(f32[32,256]{1,0:T(8,128)S(1)} %maximum_select_fusion.5), channel_id=1, source_target_pairs={{0,16},{8,24},{16,0},{24,8},{32,48},{40,56},{48,32},{56,40},{64,80... | collective-permute-start | bytes 98312 | tf_op jit(solution)/shard_map/ppermute | solution.py:33
  165.3 4.4 %collective-permute-start.6 = (f32[64,256]{1,0:T(8,128)S(1)}, f32[64,256]{1,0:T(8,128)S(1)}, u32[]{:S(2)}, u32[]{:S(2)}) collective-permute-start(f32[64,256]{1,0:T(8,128)S(1)} %maximum_select_fusion.4), channel_id=1, source_target_pairs={{0,32},{8,40},{16,48},{24,56},{32,0},{40,8},{48,16},{56,24},{64,96... | collective-permute-start | bytes 196616 | tf_op jit(solution)/shard_map/ppermute | solution.py:33
  169.7 9.8 %collective-permute-start.7 = (f32[128,256]{1,0:T(8,128)S(1)}, f32[128,256]{1,0:T(8,128)S(1)}, u32[]{:S(2)}, u32[]{:S(2)}) collective-permute-start(f32[128,256]{1,0:T(8,128)S(1)} %maximum_select_fusion.3), channel_id=1, source_target_pairs={{0,64},{8,72},{16,80},{24,88},{32,96},{40,104},{48,112},{56,120},{... | collective-permute-start | bytes 393224 | tf_op jit(solution)/shard_map/ppermute | solution.py:33
  179.6 27.5 %collective-permute-start.8 = (f32[256,256]{1,0:T(8,128)S(1)}, f32[256,256]{1,0:T(8,128)S(1)}, u32[]{:S(2)}, u32[]{:S(2)}) collective-permute-start(f32[256,256]{1,0:T(8,128)S(1)} %maximum_select_fusion.2), channel_id=1, source_target_pairs={{0,128},{8,136},{16,144},{24,152},{32,160},{40,168},{48,176},{56,1... | collective-permute-start | bytes 786440 | tf_op jit(solution)/shard_map/ppermute | solution.py:33
Sparse Core Ops, SparseCore 0:
  25.4 65.1 all-gather.1

commit v2 on v1

--- a/solution.py
+++ b/solution.py
@@ -28,8 +28,8 @@
 def butterfly_gather(block, axis):
     size = lax.axis_size(axis)
     me = lax.axis_index(axis)
-    step = 1
-    while step < size:
+    step = size // 2
+    while step >= 1:
         other = lax.ppermute(block, axis, [(i, i ^ step) for i in range(size)])
         upper = (me // step) % 2 == 1
         block = jnp.where(
@@ -37,8 +37,13 @@
             jnp.concatenate([other, block], axis=0),
             jnp.concatenate([block, other], axis=0),
         )
-        step *= 2
+        step //= 2
     return block
+
+
+def bit_reversed(count):
+    width = count.bit_length() - 1
+    return [int(format(i, f"0{width}b")[::-1], 2) for i in range(count)]
 
 
 def per_device(
@@ -67,7 +72,6 @@
     highest = lax.Precision.HIGHEST
     chunk = tokens_here // factor_count
 
-    queries = lax.all_gather(jnp.concatenate([query_in, query_out], axis=2), "dp", axis=0, tiled=True)
 
     in_part = jnp.dot(activations, proj_in, preferred_element_type=jnp.float32)
     out_part = jnp.dot(out_grads, proj_out, preferred_element_type=jnp.float32)
@@ -112,15 +116,14 @@
     grad_low = grad_rows.astype(jnp.bfloat16)
 
     basis_cut = lax.dynamic_slice_in_dim(basis_out_wide, factor_index * rank_slice, rank_slice, 1)
-    q_in = jnp.einsum(
-        "qtk,kl->qtl", queries[:, :, :rank_in].astype(jnp.float32), basis_in_wide, precision=highest
-    )
-    q_out = jnp.einsum(
-        "qtk,kl->qtl", queries[:, :, rank_in:].astype(jnp.float32), basis_cut, precision=highest
-    )
+    q_out = jnp.einsum("qtk,kl->qtl", query_out.astype(jnp.float32), basis_cut, precision=highest)
+    q_in = jnp.einsum("qtk,kl->qtl", query_in.astype(jnp.float32), basis_in_wide, precision=highest)
     outer = jnp.einsum("qti,qtj->qij", q_out, q_in, precision=highest)
-    query_grad = (outer.reshape(queries.shape[0], rank_slice * rank_in) * scale[None, :]).astype(
-        jnp.bfloat16
+    query_grad = lax.all_gather(
+        (outer.reshape(query_in.shape[0], rank_slice * rank_in) * scale[None, :]).astype(jnp.bfloat16),
+        "dp",
+        axis=0,
+        tiled=True,
     )
     part = lax.dot_general(
         grad_low, query_grad, (((1,), (1,)), ((), ())), preferred_element_type=jnp.float32
@@ -136,7 +139,11 @@
     earlier = (own_all[None, :] == own_all[:, None]) & (numbers[None, :] < numbers[:, None])
     rank_all = jnp.sum(earlier.astype(jnp.int32), axis=1)
     slots = jnp.arange(OWN_CAP, dtype=jnp.int32)[:, None]
-    placing = ((own_all[None, :] == data_index) & (rank_all[None, :] == slots)).astype(jnp.float32)
+    arrival = jnp.asarray(bit_reversed(data_count), jnp.int32)
+    order = (arrival[:, None] * pieces + jnp.arange(pieces, dtype=jnp.int32)[None, :]).reshape(-1)
+    placing = ((own_all[order][None, :] == data_index) & (rank_all[order][None, :] == slots)).astype(
+        jnp.float32
+    )
     return jnp.dot(placing, relative_all, precision=highest)
 
 

time: 215 us -> 206 us (0.958)
  the two profiles are of different devices: /device:TPU:96 before, /device:TPU:1 now
where the time goes in v2:
time: 206 us; the launch traced here: 205 us
  waiting for transfers between devices  120 us (58%)
  starting transfers between devices  32.6 us (16%)
  matrix products  16.2 us (8%)
  between operations  15 us (7%)
  local copies, waits for them, and re-layouts  14.6 us (7%)
  other arithmetic  6.77 us (3%)
    all_to_all x1, waiting for transfers between devices, per_device(): gathered_parts = lax.all_to_all(stacked_parts, 'factor', 0, 0, tiled=True)  68 us
    all_to_all x1, waiting for transfers between devices, per_device(): received = lax.all_to_all(sending, 'factor', 0, 0, tiled=True)  28.5 us
    ppermute x5, waiting for transfers between devices, butterfly_gather(): other = lax.ppermute(block, axis, [(i, i ^ step) for i in range(size)])  14.1 us
    ppermute x5, starting transfers between devices, butterfly_gather(): other = lax.ppermute(block, axis, [(i, i ^ step) for i in range(size)])  13 us
    ppermute x3, waiting for transfers between devices, butterfly_sum(): lax.ppermute(block, axis, [(i, i ^ step) for i in range(size)])  9.36 us
    all_to_all x1, starting transfers between devices, per_device(): gathered_parts = lax.all_to_all(stacked_parts, 'factor', 0, 0, tiled=True)  7.61 us
    ppermute x1, starting transfers between devices, from_behind(): return lax.ppermute(block, axis, route)  5.52 us
    dot_general x1, matrix products, per_device(): in_part = jnp.dot(activations, proj_in, preferred_element_type=jnp.float32)  5.22 us
  transfers between devices with their start and end apart: 12, of which 9 were waited for; matrix products, arithmetic and copies ran while one was open for 11% of the time, Pallas kernels for 0%

profile of v2, /device:TPU:1, one launch (start us, length us, event | category | flops | bytes accessed | tf_op | source)
XLA Modules:
  0.0 205.1 jit_solution(1621359341057153939)
XLA Ops:
  6.5 1.6 copy-done
  8.1 1.7 fusion.34
  9.8 5.2 %fusion.33 = f32[2048,256]{0,1:T(8,128)S(1)} fusion(bf16[2048,1792]{1,0:T(8,128)(2,1)} %param.17, bf16[1792,256]{1,0:T(8,128)(2,1)S(1)} %copy-done.9), kind=kOutput, calls=%fused_computation.65 | convolution fusion | flops 1879048192 | bytes 10354688 | tf_op jit(solution)/shard_map/dot_general | solution.py:76
  15.3 2.3 %copy.53 = f32[64,8,8,256]{3,2,0,1:T(8,128)} copy(f32[64,8,8,256]{3,2,1,0:T(8,128)S(1)} %bitcast.59) | data formatting | bytes 8388608 | tf_op jit(solution)/shard_map/all_to_all | solution.py:79
  17.7 7.6 %all-to-all-start = ((f32[8,256,512]{1,2,0:T(8,128)}), f32[8,256,512]{1,2,0:T(8,128)}, u32[]{:S(2)}, u32[]{:S(2)}) async-start(f32[8,256,512]{1,2,0:T(8,128)} %bitcast.58), calls=%async_computation | async-start | bytes 8388608 | tf_op jit(solution)/shard_map/all_to_all | solution.py:79
  26.4 0.7 multiply_convert_fusion
  27.1 68.0 %all-to-all-done = f32[8,256,512]{1,2,0:T(8,128)} async-done(((f32[8,256,512]{1,2,0:T(8,128)}), f32[8,256,512]{1,2,0:T(8,128)}, u32[]{:S(2)}, u32[]{:S(2)}) %all-to-all-start) | async-done | bytes 4194336 | tf_op jit(solution)/shard_map/all_to_all | solution.py:79
  95.1 2.5 %reduce_sum.28 = f32[256,512]{0,1:T(8,128)S(1)} reduce(f32[8,256,512]{1,2,0:T(8,128)} %all-to-all-done, f32[]{:T(128)} %constant.163.clone.1), dimensions={0}, to_apply=%region_2.3 | reduce | flops 917504 | bytes 4718596 | tf_op jit(solution)/shard_map/reduce_sum | solution.py:80
  98.5 1.6 pad_maximum_fusion.1
  100.1 4.5 %all-to-all-start.1 = ((f32[8,256,288]{1,2,0:T(8,128)}), f32[8,256,288]{1,2,0:T(8,128)}, u32[]{:S(2)}, u32[]{:S(2)}) async-start(f32[8,256,288]{1,2,0:T(8,128)} %pad_maximum_fusion.1), calls=%async_computation.1 | async-start | bytes 4718592 | tf_op jit(solution)/shard_map/all_to_all | solution.py:89
  105.0 28.5 %all-to-all-done.1 = f32[8,256,288]{1,2,0:T(8,128)} async-done(((f32[8,256,288]{1,2,0:T(8,128)}), f32[8,256,288]{1,2,0:T(8,128)}, u32[]{:S(2)}, u32[]{:S(2)}) %all-to-all-start.1) | async-done | bytes 2359328 | tf_op jit(solution)/shard_map/all_to_all | solution.py:89
  133.5 1.9 copy.47
  135.4 0.5 broadcast_multiply_fusion
  136.0 3.5 %fusion = f32[512,256]{1,0:T(8,128)S(1)} fusion(f32[2048,512]{0,1:T(8,128)S(1)} %bitcast.60, f32[2048,288]{0,1:T(8,128)S(1)} %bitcast.62), kind=kOutput, calls=%fused_computation.5 | convolution fusion | flops 3221225472 | bytes 6815744 | tf_op jit(solution)/shard_map/dot_general | solution.py:103
  139.5 5.5 %collective-permute-start = (f32[8192]{0:T(1024)S(1)}, f32[8192]{0:T(1024)S(1)}, u32[]{:S(2)}, u32[]{:S(2)}) collective-permute-start(f32[8192]{0:T(1024)S(1)} %bitcast.69), channel_id=1, source_target_pairs={{0,8},{8,16},{16,24},{24,32},{32,40},{40,48},{48,56},{56,64},{64,7... | collective-permute-start | bytes 98312 | tf_op jit(solution)/shard_map/ppermute | solution.py:16
  145.0 0.6 fusion.32
  147.7 3.4 %fusion.13 = f32[16,256]{1,0:T(8,128)S(1)} fusion(bf16[256,8192]{1,0:T(8,128)(2,1)} %all-gather.2.cloned.1.call-done, f32[16,8192]{1,0:T(8,128)S(1)} %scatter-mul.4), kind=kOutput, calls=%fused_computation.27 | convolution fusion | flops 67239936 | bytes 4734976 | tf_op jit(solution)/shard_map/dot_general | solution.py:128
  151.1 1.4 collective-permute-start.1
  152.5 3.1 %collective-permute-done.1 = f32[16,257]{1,0:T(8,128)S(1)} collective-permute-done((f32[16,257]{1,0:T(8,128)S(1)}, f32[16,257]{1,0:T(8,128)S(1)}, u32[]{:S(2)}, u32[]{:S(2)}) %collective-permute-start.1) | collective-permute-done | bytes 16480 | tf_op jit(solution)/shard_map/ppermute | solution.py:23
  155.6 2.7 %collective-permute-done.2 = f32[16,257]{1,0:T(8,128)S(1)} collective-permute-done((f32[16,257]{1,0:T(8,128)S(1)}, f32[16,257]{1,0:T(8,128)S(1)}, u32[]{:S(2)}, u32[]{:S(2)}) %collective-permute-start.2) | collective-permute-done | bytes 16480 | tf_op jit(solution)/shard_map/ppermute | solution.py:23
  158.2 0.6 collective-permute-start.3
  158.8 3.6 %collective-permute-done.3 = f32[16,257]{1,0:T(8,128)S(1)} collective-permute-done((f32[16,257]{1,0:T(8,128)S(1)}, f32[16,257]{1,0:T(8,128)S(1)}, u32[]{:S(2)}, u32[]{:S(2)}) %collective-permute-start.3) | collective-permute-done | bytes 16480 | tf_op jit(solution)/shard_map/ppermute | solution.py:23
  162.7 6.5 %collective-permute-done.4 = f32[16,256]{1,0:T(8,128)S(1)} collective-permute-done((f32[16,256]{1,0:T(8,128)S(1)}, f32[16,256]{1,0:T(8,128)S(1)}, u32[]{:S(2)}, u32[]{:S(2)}) %collective-permute-start.4) | collective-permute-done | bytes 16416 | tf_op jit(solution)/shard_map/ppermute | solution.py:33
  169.3 3.5 %collective-permute-done.5 = f32[32,256]{1,0:T(8,128)S(1)} collective-permute-done((f32[32,256]{1,0:T(8,128)S(1)}, f32[32,256]{1,0:T(8,128)S(1)}, u32[]{:S(2)}, u32[]{:S(2)}) %collective-permute-start.5) | collective-permute-done | bytes 32800 | tf_op jit(solution)/shard_map/ppermute | solution.py:33
  172.8 2.6 %collective-permute-start.6 = (f32[64,256]{1,0:T(8,128)S(1)}, f32[64,256]{1,0:T(8,128)S(1)}, u32[]{:S(2)}, u32[]{:S(2)}) collective-permute-start(f32[64,256]{1,0:T(8,128)S(1)} %maximum_select_fusion.4), channel_id=1, source_target_pairs={{0,32},{8,40},{16,48},{24,56},{32,0},{40,8},{48,16},{56,24},{64,96... | collective-permute-start | bytes 196616 | tf_op jit(solution)/shard_map/ppermute | solution.py:33
  175.4 2.0 collective-permute-done.6
  177.5 2.5 %collective-permute-start.7 = (f32[128,256]{1,0:T(8,128)S(1)}, f32[128,256]{1,0:T(8,128)S(1)}, u32[]{:S(2)}, u32[]{:S(2)}) collective-permute-start(f32[128,256]{1,0:T(8,128)S(1)} %maximum_select_fusion.3), channel_id=1, source_target_pairs={{0,16},{8,24},{16,0},{24,8},{32,48},{40,56},{48,32},{56,40},{64,80... | collective-permute-start | bytes 393224 | tf_op jit(solution)/shard_map/ppermute | solution.py:33
  180.2 2.1 %collective-permute-done.7 = f32[128,256]{1,0:T(8,128)S(1)} collective-permute-done((f32[128,256]{1,0:T(8,128)S(1)}, f32[128,256]{1,0:T(8,128)S(1)}, u32[]{:S(2)}, u32[]{:S(2)}) %collective-permute-start.7) | collective-permute-done | bytes 131104 | tf_op jit(solution)/shard_map/ppermute | solution.py:33
  182.3 7.9 %collective-permute-start.8 = (f32[256,256]{1,0:T(8,128)S(1)}, f32[256,256]{1,0:T(8,128)S(1)}, u32[]{:S(2)}, u32[]{:S(2)}) collective-permute-start(f32[256,256]{1,0:T(8,128)S(1)} %maximum_select_fusion.2), channel_id=1, source_target_pairs={{0,8},{8,0},{16,24},{24,16},{32,40},{40,32},{48,56},{56,48},{64,72... | collective-permute-start | bytes 786440 | tf_op jit(solution)/shard_map/ppermute | solution.py:33
  190.2 3.5 %gather_fusion = s32[512]{0:T(512)S(1)} fusion(s32[512]{0:T(512)S(1)} %bitcast.57, s32[1024]{0:T(1024)S(1)} %pad_clamp_fusion), kind=kCustom, calls=%fused_computation | custom fusion | bytes 6144 | tf_op jit(solution)/shard_map/gather | solution.py:144
  193.7 3.5 %gather_fusion.1 = s32[512]{0:T(512)S(1)} fusion(s32[512]{0:T(512)S(1)} %convert_reduce_fusion, s32[1024]{0:T(1024)S(1)} %pad_clamp_fusion), kind=kCustom, calls=%fused_computation.1 | custom fusion | bytes 6144 | tf_op jit(solution)/shard_map/gather | solution.py:144
  197.3 0.9 fusion.3
  (71 shorter events, 4.1 us)
Async XLA Ops:
  6.5 1.6 copy-start
  6.5 3.3 %copy-start.9 = (bf16[1792,256]{1,0:T(8,128)(2,1)S(1)}, bf16[1792,256]{1,0:T(8,128)(2,1)}, u32[]{:S(2)}) copy-start(bf16[1792,256]{1,0:T(8,128)(2,1)} %param.19) | copy-start | bytes 2752516
  17.7 7.7 %copy-start.5 = (f32[32,256]{1,0:T(8,128)S(1)}, f32[32,256]{1,0:T(8,128)}, u32[]{:S(2)}) copy-start(f32[32,256]{1,0:T(8,128)} %param.23) | copy-start | bytes 98308
  17.7 7.7 %copy-start.2 = (bf16[256,256]{1,0:T(8,128)(2,1)S(1)}, bf16[256,256]{1,0:T(8,128)(2,1)}, u32[]{:S(2)}) copy-start(bf16[256,256]{1,0:T(8,128)(2,1)} %param.21) | copy-start | bytes 393220
  17.7 7.8 %copy-start.4 = (bf16[8,8,256]{2,1,0:T(8,128)(2,1)S(1)}, bf16[8,8,256]{2,1,0:T(8,128)(2,1)}, u32[]{:S(2)}) copy-start(bf16[8,8,256]{2,1,0:T(8,128)(2,1)} %param.24) | copy-start | bytes 98308
  17.7 7.9 %copy-start.3 = (bf16[256,256]{1,0:T(8,128)(2,1)S(1)}, bf16[256,256]{1,0:T(8,128)(2,1)}, u32[]{:S(2)}) copy-start(bf16[256,256]{1,0:T(8,128)(2,1)} %param.22) | copy-start | bytes 393220
  17.7 7.9 %copy-start.10 = (bf16[8,8,256]{2,1,0:T(8,128)(2,1)S(1)}, bf16[8,8,256]{2,1,0:T(8,128)(2,1)}, u32[]{:S(2)}) copy-start(bf16[8,8,256]{2,1,0:T(8,128)(2,1)} %param.25) | copy-start | bytes 98308
  17.7 77.4 %all-to-all-start = ((f32[8,256,512]{1,2,0:T(8,128)}), f32[8,256,512]{1,2,0:T(8,128)}, u32[]{:S(2)}, u32[]{:S(2)}) async-start(f32[8,256,512]{1,2,0:T(8,128)} %bitcast.58), calls=%async_computation | async-start | bytes 8388608 | tf_op jit(solution)/shard_map/all_to_all | solution.py:79
  25.3 122.4 %all-gather.2.cloned.1.call-start = ((), (), s32[]{:S(2)}) async-start(), calls=%async_computation.2 | async-start | bytes 4325376 | tf_op jit(solution)/shard_map/all_gather | solution.py:122
  100.1 4.5 %copy-start.7 = (s32[1,16]{1,0:T(1,128)S(1)}, s32[1,16]{1,0:T(1,128)}, u32[]{:S(2)}) copy-start(s32[1,16]{1,0:T(1,128)} %param.26) | copy-start | bytes 196
  100.1 33.4 %all-to-all-start.1 = ((f32[8,256,288]{1,2,0:T(8,128)}), f32[8,256,288]{1,2,0:T(8,128)}, u32[]{:S(2)}, u32[]{:S(2)}) async-start(f32[8,256,288]{1,2,0:T(8,128)} %pad_maximum_fusion.1), calls=%async_computation.1 | async-start | bytes 4718592 | tf_op jit(solution)/shard_map/all_to_all | solution.py:89
  135.9 9.1 %copy-start.6 = (s32[32]{0:T(128)S(1)}, s32[32]{0:T(128)}, u32[]{:S(2)}) copy-start(s32[32]{0:T(128)} %param.27) | copy-start | bytes 388
  139.5 7.5 %collective-permute-start = (f32[8192]{0:T(1024)S(1)}, f32[8192]{0:T(1024)S(1)}, u32[]{:S(2)}, u32[]{:S(2)}) collective-permute-start(f32[8192]{0:T(1024)S(1)} %bitcast.69), channel_id=1, source_target_pairs={{0,8},{8,16},{16,24},{24,32},{32,40},{40,48},{48,56},{56,64},{64,7... | collective-permute-start | bytes 98312 | tf_op jit(solution)/shard_map/ppermute | solution.py:16
  147.7 21.5 %copy-start.8 = (s32[32]{0:T(128)S(1)}, s32[32]{0:T(128)}, u32[]{:S(2)}) copy-start(s32[32]{0:T(128)} %constant.175) | copy-start | bytes 388
  147.7 32.3 %copy-start.1 = (s32[512,1]{0,1:T(1,128)S(1)}, s32[512,1]{0,1:T(1,128)}, u32[]{:S(2)}) copy-start(s32[512,1]{0,1:T(1,128)} %param.28) | copy-start | bytes 6148
  151.1 4.4 %collective-permute-start.1 = (f32[16,257]{1,0:T(8,128)S(1)}, f32[16,257]{1,0:T(8,128)S(1)}, u32[]{:S(2)}, u32[]{:S(2)}) collective-permute-start(f32[16,257]{1,0:T(8,128)S(1)} %pad_maximum_fusion.2), channel_id=1, source_target_pairs={{0,1},{1,0},{2,3},{3,2},{4,5},{5,4},{6,7},{7,6},{8,9},{9,8},{10,11... | collective-permute-start | bytes 49352 | tf_op jit(solution)/shard_map/ppermute | solution.py:23
  155.6 2.7 %collective-permute-start.2 = (f32[16,257]{1,0:T(8,128)S(1)}, f32[16,257]{1,0:T(8,128)S(1)}, u32[]{:S(2)}, u32[]{:S(2)}) collective-permute-start(f32[16,257]{1,0:T(8,128)S(1)} %fusion.31), channel_id=1, source_target_pairs={{0,2},{1,3},{2,0},{3,1},{4,6},{5,7},{6,4},{7,5},{8,10},{9,11},{10,... | collective-permute-start | bytes 49352 | tf_op jit(solution)/shard_map/ppermute | solution.py:23
  158.2 4.2 %collective-permute-start.3 = (f32[16,257]{1,0:T(8,128)S(1)}, f32[16,257]{1,0:T(8,128)S(1)}, u32[]{:S(2)}, u32[]{:S(2)}) collective-permute-start(f32[16,257]{1,0:T(8,128)S(1)} %add.111), channel_id=1, source_target_pairs={{0,4},{1,5},{2,6},{3,7},{4,0},{5,1},{6,2},{7,3},{8,12},{9,13},{10,... | collective-permute-start | bytes 49352 | tf_op jit(solution)/shard_map/ppermute | solution.py:23
  162.6 6.5 %collective-permute-start.4 = (f32[16,256]{1,0:T(8,128)S(1)}, f32[16,256]{1,0:T(8,128)S(1)}, u32[]{:S(2)}, u32[]{:S(2)}) collective-permute-start(f32[16,256]{1,0:T(8,128)S(1)} %slice_divide_fusion), channel_id=1, source_target_pairs={{0,128},{8,136},{16,144},{24,152},{32,160},{40,168},{48,176},{56,1... | collective-permute-start | bytes 49160 | tf_op jit(solution)/shard_map/ppermute | solution.py:33
  169.2 3.7 %collective-permute-start.5 = (f32[32,256]{1,0:T(8,128)S(1)}, f32[32,256]{1,0:T(8,128)S(1)}, u32[]{:S(2)}, u32[]{:S(2)}) collective-permute-start(f32[32,256]{1,0:T(8,128)S(1)} %maximum_select_fusion.5), channel_id=1, source_target_pairs={{0,64},{8,72},{16,80},{24,88},{32,96},{40,104},{48,112},{56,120},{... | collective-permute-start | bytes 98312 | tf_op jit(solution)/shard_map/ppermute | solution.py:33
  172.8 4.6 %collective-permute-start.6 = (f32[64,256]{1,0:T(8,128)S(1)}, f32[64,256]{1,0:T(8,128)S(1)}, u32[]{:S(2)}, u32[]{:S(2)}) collective-permute-start(f32[64,256]{1,0:T(8,128)S(1)} %maximum_select_fusion.4), channel_id=1, source_target_pairs={{0,32},{8,40},{16,48},{24,56},{32,0},{40,8},{48,16},{56,24},{64,96... | collective-permute-start | bytes 196616 | tf_op jit(solution)/shard_map/ppermute | solution.py:33
  177.5 4.8 %collective-permute-start.7 = (f32[128,256]{1,0:T(8,128)S(1)}, f32[128,256]{1,0:T(8,128)S(1)}, u32[]{:S(2)}, u32[]{:S(2)}) collective-permute-start(f32[128,256]{1,0:T(8,128)S(1)} %maximum_select_fusion.3), channel_id=1, source_target_pairs={{0,16},{8,24},{16,0},{24,8},{32,48},{40,56},{48,32},{56,40},{64,80... | collective-permute-start | bytes 393224 | tf_op jit(solution)/shard_map/ppermute | solution.py:33
  182.3 15.0 %collective-permute-start.8 = (f32[256,256]{1,0:T(8,128)S(1)}, f32[256,256]{1,0:T(8,128)S(1)}, u32[]{:S(2)}, u32[]{:S(2)}) collective-permute-start(f32[256,256]{1,0:T(8,128)S(1)} %maximum_select_fusion.2), channel_id=1, source_target_pairs={{0,8},{8,0},{16,24},{24,16},{32,40},{40,32},{48,56},{56,48},{64,72... | collective-permute-start | bytes 786440 | tf_op jit(solution)/shard_map/ppermute | solution.py:33
Sparse Core Ops, SparseCore 0:
  28.0 70.3 all-gather.1

commit v3 on v2

--- a/solution.py
+++ b/solution.py
@@ -41,11 +41,6 @@
     return block
 
 
-def bit_reversed(count):
-    width = count.bit_length() - 1
-    return [int(format(i, f"0{width}b")[::-1], 2) for i in range(count)]
-
-
 def per_device(
     activations,
     out_grads,
@@ -73,22 +68,29 @@
     chunk = tokens_here // factor_count
 
 
+    basis_in_wide = basis_in.astype(jnp.float32)
+    basis_out_wide = basis_out.astype(jnp.float32)
     in_part = jnp.dot(activations, proj_in, preferred_element_type=jnp.float32)
     out_part = jnp.dot(out_grads, proj_out, preferred_element_type=jnp.float32)
-    stacked_parts = jnp.concatenate([in_part, out_part], axis=1)
-    gathered_parts = lax.all_to_all(stacked_parts, "factor", 0, 0, tiled=True)
-    chunk_sums = jnp.sum(gathered_parts.reshape(factor_count, chunk, rank_in + rank_out), axis=0)
-    basis_in_wide = basis_in.astype(jnp.float32)
-    basis_out_wide = basis_out.astype(jnp.float32)
-    rot_in_chunk = jnp.dot(chunk_sums[:, :rank_in], basis_in_wide, precision=highest)
-    rot_out_chunk = jnp.dot(chunk_sums[:, rank_in:], basis_out_wide, precision=highest)
-    out_blocks = rot_out_chunk.reshape(chunk, factor_count, rank_slice).transpose(1, 0, 2)
+    rot_out_part = jnp.dot(out_part, basis_out_wide, precision=highest)
+    out_cols = rot_out_part.reshape(tokens_here, factor_count, rank_slice).transpose(1, 0, 2)
+    in_rows = in_part.reshape(factor_count, chunk, rank_in)
     sending = jnp.concatenate(
-        [jnp.broadcast_to(rot_in_chunk[None], (factor_count, chunk, rank_in)), out_blocks], axis=2
-    ).reshape(factor_count * chunk, rank_in + rank_slice)
-    received = lax.all_to_all(sending, "factor", 0, 0, tiled=True)
-    rot_in = received[:, :rank_in]
-    rot_out_rows = received[:, rank_in:]
+        [out_cols.reshape(factor_count, -1), in_rows.reshape(factor_count, -1)], axis=1
+    )
+    gathered = jnp.sum(lax.all_to_all(sending, "factor", 0, 0, tiled=True), axis=0)
+    rot_out_rows = gathered[: tokens_here * rank_slice].reshape(tokens_here, rank_slice)
+    in_chunk = gathered[tokens_here * rank_slice :].reshape(chunk, rank_in)
+    rot_in_chunk = jnp.dot(in_chunk, basis_in_wide, precision=highest)
+    rot_in = lax.all_to_all(
+        jnp.broadcast_to(rot_in_chunk[None], (factor_count, chunk, rank_in)).reshape(
+            factor_count * chunk, rank_in
+        ),
+        "factor",
+        0,
+        0,
+        tiled=True,
+    )
 
     piece_lengths = lengths[0]
     piece_ends = jnp.cumsum(piece_lengths)
@@ -139,9 +141,11 @@
     earlier = (own_all[None, :] == own_all[:, None]) & (numbers[None, :] < numbers[:, None])
     rank_all = jnp.sum(earlier.astype(jnp.int32), axis=1)
     slots = jnp.arange(OWN_CAP, dtype=jnp.int32)[:, None]
-    arrival = jnp.asarray(bit_reversed(data_count), jnp.int32)
-    order = (arrival[:, None] * pieces + jnp.arange(pieces, dtype=jnp.int32)[None, :]).reshape(-1)
-    placing = ((own_all[order][None, :] == data_index) & (rank_all[order][None, :] == slots)).astype(
+    bits = data_count.bit_length() - 1
+    twisted = tuple(range(bits - 1, -1, -1)) + (bits,)
+    own_arrived = own_all.reshape((2,) * bits + (pieces,)).transpose(twisted).reshape(-1)
+    rank_arrived = rank_all.reshape((2,) * bits + (pieces,)).transpose(twisted).reshape(-1)
+    placing = ((own_arrived[None, :] == data_index) & (rank_arrived[None, :] == slots)).astype(
         jnp.float32
     )
     return jnp.dot(placing, relative_all, precision=highest)

time: 206 us -> 228 us (1.11)
  local copies, waits for them, and re-layouts: 14.6 us -> 30.7 us
  matrix products: 16.2 us -> 22.2 us
  waiting for transfers between devices: 120 us -> 114 us
  other arithmetic: 6.77 us -> 12 us
    reshape x0 -> x3, local copies, waits for them, and re-layouts: none -> 14.9 us  [the longest x1 8.56 us: per_device(): out_cols.reshape(factor_count, -1)]
    gather x2 -> x0, local copies, waits for them, and re-layouts: 7.02 us -> none  [the longest x1 3.51 us: per_device(): rank_all[order][None, :] == slots]
    all_to_all x2, waiting for transfers between devices: 96.5 us -> 89.5 us  [the longest x1 67.2 us: per_device(): lax.all_to_all(sending, 'factor', 0, 0, tiled=True)]
    another operation x1 -> x2, local copies, waits for them, and re-layouts: 0.08 us -> 3.38 us  [the longest x1 3.3 us: per_device(): in_rows.reshape(factor_count, -1)]
    reduce_sum x1, other arithmetic: 2.53 us -> 5.24 us  [per_device(): jnp.sum(lax.all_to_all(sending, 'factor', 0, 0, tiled=True), axis=0)]
    dot_general x1, matrix products: 3.46 us -> 6.02 us  [per_device(): lax.dot_general(stacked, rot_in, (((0,), (0,)), ((), ())), precision=high...]
    all_to_all x0 -> x1, other arithmetic: none -> 2.49 us  [per_device(): lax.all_to_all(sending, 'factor', 0, 0, tiled=True)]
    all_to_all x2 -> x1, local copies, waits for them, and re-layouts: 4.25 us -> 6.28 us  [per_device(): lax.all_to_all(sending, 'factor', 0, 0, tiled=True)]
  transfers between devices with their start and end apart: 12 -> 12, of which waited for: 9 -> 10; matrix products, arithmetic and copies ran while one was open for 11% -> 9% of each run, Pallas kernels for 0% -> 0%
where the time goes in v3:
time: 228 us; the launch traced here: 226 us
  waiting for transfers between devices  114 us (50%)
  starting transfers between devices  32.7 us (14%)
  local copies, waits for them, and re-layouts  30.7 us (13%)
  matrix products  22.2 us (10%)
  between operations  15.1 us (7%)
  other arithmetic  12 us (5%)
    all_to_all x1, waiting for transfers between devices, per_device(): lax.all_to_all(sending, 'factor', 0, 0, tiled=True)  67.2 us
    all_to_all x1, waiting for transfers between devices, per_device(): lax.all_to_all(jnp.broadcast_to(rot_in_chunk[None], (factor_count, chunk,...  22.3 us
    ppermute x5, waiting for transfers between devices, butterfly_gather(): other = lax.ppermute(block, axis, [(i, i ^ step) for i in range(size)])  14.9 us
    ppermute x5, starting transfers between devices, butterfly_gather(): other = lax.ppermute(block, axis, [(i, i ^ step) for i in range(size)])  12.9 us
    ppermute x3, waiting for transfers between devices, butterfly_sum(): lax.ppermute(block, axis, [(i, i ^ step) for i in range(size)])  9.36 us
    reshape x1, local copies, waits for them, and re-layouts, per_device(): out_cols.reshape(factor_count, -1)  8.56 us
    all_to_all x1, starting transfers between devices, per_device(): lax.all_to_all(sending, 'factor', 0, 0, tiled=True)  7.62 us
    dot_general x1, matrix products, per_device(): in_part = jnp.dot(activations, proj_in, preferred_element_type=jnp.float32)  6.51 us
  transfers between devices with their start and end apart: 12, of which 10 were waited for; matrix products, arithmetic and copies ran while one was open for 9% of the time, Pallas kernels for 0%

profile of v3, /device:TPU:1, one launch (start us, length us, event | category | flops | bytes accessed | tf_op | source)
XLA Modules:
  0.0 226.4 jit_solution(3438820935163182817)
XLA Ops:
  6.5 1.6 copy-done
  8.1 1.6 fusion.28
  9.8 2.6 %fusion.29 = f32[2048,256]{0,1:T(8,128)} fusion(f32[2048,256]{1,0:T(8,128)S(1)} %fusion.28, bf16[256,256]{1,0:T(8,128)(2,1)S(1)} %copy-done.4), kind=kOutput, calls=%fused_computation.55 | convolution fusion | flops 1610612736 | bytes 4325376 | tf_op jit(solution)/shard_map/dot_general | solution.py:75
  12.4 6.3 %copy.38 = f32[2048,8,32]{2,0,1:T(8,128)} copy(f32[2048,8,32]{0,2,1:T(8,128)} %bitcast.60) | data formatting | bytes 4194304 | tf_op jit(solution)/shard_map/reshape | solution.py:76
  18.6 8.6 %reshape.173 = f32[8,65536]{1,0:T(8,128)} reshape(f32[8,2048,32]{2,1,0:T(8,128)} %bitcast.58) | data formatting | bytes 4194304 | tf_op jit(solution)/shard_map/reshape | solution.py:79
  27.2 6.5 %fusion.30 = f32[2048,256]{1,0:T(8,128)} fusion(bf16[2048,1792]{1,0:T(8,128)(2,1)} %param.16, bf16[1792,256]{1,0:T(8,128)(2,1)S(1)} %copy-done.10), kind=kOutput, calls=%fused_computation.56 | convolution fusion | flops 1879048192 | bytes 10354688 | tf_op jit(solution)/shard_map/dot_general | solution.py:73
  33.7 3.3 %reshape_reshape.3 = f32[8,65536]{1,0:T(8,128)} reshape(f32[2048,256]{1,0:T(8,128)} %fusion.30) | data formatting | bytes 4194304 | tf_op jit(solution)/shard_map/reshape;reshape | solution.py:79
  37.0 2.5 %maximum_bitcast_fusion = f32[8,1,131072]{2,0,1:T(8,128)S(1)} fusion(f32[8,65536]{1,0:T(8,128)} %reshape_reshape.3, f32[8,65536]{1,0:T(8,128)} %reshape.173), kind=kLoop, calls=%fused_computation | loop fusion | flops 1048576 | bytes 8388608 | tf_op jit(solution)/shard_map/all_to_all | solution.py:81
  39.5 6.3 %copy.39 = f32[8,1,131072]{2,1,0:T(1,128)} copy(f32[8,1,131072]{2,0,1:T(8,128)S(1)} %maximum_bitcast_fusion) | data formatting | bytes 8388608 | tf_op jit(solution)/shard_map/all_to_all | solution.py:81
  45.8 7.6 %all-to-all-start = ((f32[8,1,131072]{2,1,0:T(1,128)}), f32[8,1,131072]{2,1,0:T(1,128)}, u32[]{:S(2)}, u32[]{:S(2)}) async-start(f32[8,1,131072]{2,1,0:T(1,128)} %copy.39), calls=%async_computation | async-start | bytes 8388608 | tf_op jit(solution)/shard_map/all_to_all | solution.py:81
  55.3 0.7 multiply_convert_fusion
  56.0 67.2 %all-to-all-done = f32[8,1,131072]{2,1,0:T(1,128)} async-done(((f32[8,1,131072]{2,1,0:T(1,128)}), f32[8,1,131072]{2,1,0:T(1,128)}, u32[]{:S(2)}, u32[]{:S(2)}) %all-to-all-start) | async-done | bytes 4194336 | tf_op jit(solution)/shard_map/all_to_all | solution.py:81
  123.2 5.2 %reduce_sum.28 = f32[131072]{0:T(1024)S(1)} reduce(f32[8,1,131072]{2,1,0:T(1,128)} %all-to-all-done, f32[]{:T(128)} %constant.156.clone.1), dimensions={0,1}, to_apply=%region_2.3 | reduce | flops 917504 | bytes 4718596 | tf_op jit(solution)/shard_map/reduce_sum | solution.py:81
  128.9 1.5 broadcast_in_dim.4
  130.4 4.4 %all-to-all-start.1 = ((f32[8,256,256]{2,1,0:T(8,128)}), f32[8,256,256]{2,1,0:T(8,128)}, u32[]{:S(2)}, u32[]{:S(2)}) async-start(f32[8,256,256]{2,1,0:T(8,128)} %broadcast_in_dim.4), calls=%async_computation.1 | async-start | bytes 4194304 | tf_op jit(solution)/shard_map/all_to_all | solution.py:85
  135.7 2.5 %broadcast_multiply_fusion = f32[2048,16,32]{0,2,1:T(8,128)} fusion(f32[2048,32]{0,1:T(8,128)S(1)} %copy.40, f32[2048,16]{0,1:T(8,128)S(1)} %fusion.13), kind=kLoop, calls=%fused_computation.1 | loop fusion | flops 1048576 | bytes 4587520 | tf_op jit(solution)/shard_map/mul | solution.py:102
  138.2 22.3 %all-to-all-done.1 = f32[8,256,256]{2,1,0:T(8,128)} async-done(((f32[8,256,256]{2,1,0:T(8,128)}), f32[8,256,256]{2,1,0:T(8,128)}, u32[]{:S(2)}, u32[]{:S(2)}) %all-to-all-start.1) | async-done | bytes 2097184 | tf_op jit(solution)/shard_map/all_to_all | solution.py:85
  160.6 6.0 %fusion.32 = f32[512,256]{1,0:T(8,128)S(1)} fusion(f32[2048,512]{0,1:T(8,128)} %bitcast.59, f32[2048,256]{1,0:T(8,128)} %bitcast.9), kind=kOutput, calls=%fused_computation.58 | convolution fusion | flops 3221225472 | bytes 6815744 | tf_op jit(solution)/shard_map/dot_general | solution.py:105
  166.6 5.8 %collective-permute-start = (f32[8192]{0:T(1024)S(1)}, f32[8192]{0:T(1024)S(1)}, u32[]{:S(2)}, u32[]{:S(2)}) collective-permute-start(f32[8192]{0:T(1024)S(1)} %bitcast.67), channel_id=1, source_target_pairs={{0,8},{8,16},{16,24},{24,32},{32,40},{40,48},{48,56},{56,64},{64,7... | collective-permute-start | bytes 98312 | tf_op jit(solution)/shard_map/ppermute | solution.py:16
  175.2 3.4 %fusion.7 = f32[16,256]{1,0:T(8,128)S(1)} fusion(bf16[256,8192]{1,0:T(8,128)(2,1)} %all-gather.2.cloned.1.call-done, f32[16,8192]{1,0:T(8,128)S(1)} %scatter-mul.4), kind=kOutput, calls=%fused_computation.17 | convolution fusion | flops 67239936 | bytes 4734976 | tf_op jit(solution)/shard_map/dot_general | solution.py:130
  178.6 1.2 collective-permute-start.1
  179.8 3.1 %collective-permute-done.1 = f32[16,257]{1,0:T(8,128)S(1)} collective-permute-done((f32[16,257]{1,0:T(8,128)S(1)}, f32[16,257]{1,0:T(8,128)S(1)}, u32[]{:S(2)}, u32[]{:S(2)}) %collective-permute-start.1) | collective-permute-done | bytes 16480 | tf_op jit(solution)/shard_map/ppermute | solution.py:23
  182.9 2.7 %collective-permute-done.2 = f32[16,257]{1,0:T(8,128)S(1)} collective-permute-done((f32[16,257]{1,0:T(8,128)S(1)}, f32[16,257]{1,0:T(8,128)S(1)}, u32[]{:S(2)}, u32[]{:S(2)}) %collective-permute-start.2) | collective-permute-done | bytes 16480 | tf_op jit(solution)/shard_map/ppermute | solution.py:23
  186.1 3.6 %collective-permute-done.3 = f32[16,257]{1,0:T(8,128)S(1)} collective-permute-done((f32[16,257]{1,0:T(8,128)S(1)}, f32[16,257]{1,0:T(8,128)S(1)}, u32[]{:S(2)}, u32[]{:S(2)}) %collective-permute-start.3) | collective-permute-done | bytes 16480 | tf_op jit(solution)/shard_map/ppermute | solution.py:23
  190.0 6.5 %collective-permute-done.4 = f32[16,256]{1,0:T(8,128)S(1)} collective-permute-done((f32[16,256]{1,0:T(8,128)S(1)}, f32[16,256]{1,0:T(8,128)S(1)}, u32[]{:S(2)}, u32[]{:S(2)}) %collective-permute-start.4) | collective-permute-done | bytes 16416 | tf_op jit(solution)/shard_map/ppermute | solution.py:33
  196.5 3.6 %collective-permute-done.5 = f32[32,256]{1,0:T(8,128)S(1)} collective-permute-done((f32[32,256]{1,0:T(8,128)S(1)}, f32[32,256]{1,0:T(8,128)S(1)}, u32[]{:S(2)}, u32[]{:S(2)}) %collective-permute-start.5) | collective-permute-done | bytes 32800 | tf_op jit(solution)/shard_map/ppermute | solution.py:33
  200.2 2.6 %collective-permute-start.6 = (f32[64,256]{1,0:T(8,128)S(1)}, f32[64,256]{1,0:T(8,128)S(1)}, u32[]{:S(2)}, u32[]{:S(2)}) collective-permute-start(f32[64,256]{1,0:T(8,128)S(1)} %maximum_select_fusion.4), channel_id=1, source_target_pairs={{0,32},{8,40},{16,48},{24,56},{32,0},{40,8},{48,16},{56,24},{64,96... | collective-permute-start | bytes 196616 | tf_op jit(solution)/shard_map/ppermute | solution.py:33
  202.8 2.0 collective-permute-done.6
  204.8 2.5 %collective-permute-start.7 = (f32[128,256]{1,0:T(8,128)S(1)}, f32[128,256]{1,0:T(8,128)S(1)}, u32[]{:S(2)}, u32[]{:S(2)}) collective-permute-start(f32[128,256]{1,0:T(8,128)S(1)} %maximum_select_fusion.3), channel_id=1, source_target_pairs={{0,16},{8,24},{16,0},{24,8},{32,48},{40,56},{48,32},{56,40},{64,80... | collective-permute-start | bytes 393224 | tf_op jit(solution)/shard_map/ppermute | solution.py:33
  207.3 2.4 %collective-permute-done.7 = f32[128,256]{1,0:T(8,128)S(1)} collective-permute-done((f32[128,256]{1,0:T(8,128)S(1)}, f32[128,256]{1,0:T(8,128)S(1)}, u32[]{:S(2)}, u32[]{:S(2)}) %collective-permute-start.7) | collective-permute-done | bytes 131104 | tf_op jit(solution)/shard_map/ppermute | solution.py:33
  209.6 7.8 %collective-permute-start.8 = (f32[256,256]{1,0:T(8,128)S(1)}, f32[256,256]{1,0:T(8,128)S(1)}, u32[]{:S(2)}, u32[]{:S(2)}) collective-permute-start(f32[256,256]{1,0:T(8,128)S(1)} %maximum_select_fusion.2), channel_id=1, source_target_pairs={{0,8},{8,0},{16,24},{24,16},{32,40},{40,32},{48,56},{56,48},{64,72... | collective-permute-start | bytes 786440 | tf_op jit(solution)/shard_map/ppermute | solution.py:33
  218.6 0.9 fusion.1
  (77 shorter events, 6.6 us)
Async XLA Ops:
  6.5 1.6 copy-start
  6.5 3.2 %copy-start.4 = (bf16[256,256]{1,0:T(8,128)(2,1)S(1)}, bf16[256,256]{1,0:T(8,128)(2,1)}, u32[]{:S(2)}) copy-start(bf16[256,256]{1,0:T(8,128)(2,1)} %param.21) | copy-start | bytes 393220
  18.6 8.6 %copy-start.10 = (bf16[1792,256]{1,0:T(8,128)(2,1)S(1)}, bf16[1792,256]{1,0:T(8,128)(2,1)}, u32[]{:S(2)}) copy-start(bf16[1792,256]{1,0:T(8,128)(2,1)} %param.18) | copy-start | bytes 2752516
  45.8 7.9 %copy-start.1 = (bf16[256,256]{1,0:T(8,128)(2,1)S(1)}, bf16[256,256]{1,0:T(8,128)(2,1)}, u32[]{:S(2)}) copy-start(bf16[256,256]{1,0:T(8,128)(2,1)} %param.20) | copy-start | bytes 393220
  45.8 7.9 %copy-start.5 = (bf16[8,8,256]{2,1,0:T(8,128)(2,1)S(1)}, bf16[8,8,256]{2,1,0:T(8,128)(2,1)}, u32[]{:S(2)}) copy-start(bf16[8,8,256]{2,1,0:T(8,128)(2,1)} %param.23) | copy-start | bytes 98308
  45.8 8.0 %copy-start.11 = (bf16[8,8,256]{2,1,0:T(8,128)(2,1)S(1)}, bf16[8,8,256]{2,1,0:T(8,128)(2,1)}, u32[]{:S(2)}) copy-start(bf16[8,8,256]{2,1,0:T(8,128)(2,1)} %param.24) | copy-start | bytes 98308
  45.8 8.9 %copy-start.6 = (f32[32,256]{1,0:T(8,128)S(1)}, f32[32,256]{1,0:T(8,128)}, u32[]{:S(2)}) copy-start(f32[32,256]{1,0:T(8,128)} %param.22) | copy-start | bytes 98308
  45.8 77.4 %all-to-all-start = ((f32[8,1,131072]{2,1,0:T(1,128)}), f32[8,1,131072]{2,1,0:T(1,128)}, u32[]{:S(2)}, u32[]{:S(2)}) async-start(f32[8,1,131072]{2,1,0:T(1,128)} %copy.39), calls=%async_computation | async-start | bytes 8388608 | tf_op jit(solution)/shard_map/all_to_all | solution.py:81
  53.4 121.8 %all-gather.2.cloned.1.call-start = ((), (), s32[]{:S(2)}) async-start(), calls=%async_computation.2 | async-start | bytes 4325376 | tf_op jit(solution)/shard_map/all_gather | solution.py:124
  54.7 0.6 copy-start.2
  128.5 6.3 %copy-start.9 = (s32[1,16]{1,0:T(1,128)S(1)}, s32[1,16]{1,0:T(1,128)}, u32[]{:S(2)}) copy-start(s32[1,16]{1,0:T(1,128)} %param.25) | copy-start | bytes 196
  130.4 30.1 %all-to-all-start.1 = ((f32[8,256,256]{2,1,0:T(8,128)}), f32[8,256,256]{2,1,0:T(8,128)}, u32[]{:S(2)}, u32[]{:S(2)}) async-start(f32[8,256,256]{2,1,0:T(8,128)} %broadcast_in_dim.4), calls=%async_computation.1 | async-start | bytes 4194304 | tf_op jit(solution)/shard_map/all_to_all | solution.py:85
  138.2 34.2 %copy-start.8 = (s32[32]{0:T(128)S(1)}, s32[32]{0:T(128)}, u32[]{:S(2)}) copy-start(s32[32]{0:T(128)} %param.26) | copy-start | bytes 388
  160.6 14.4 %copy-start.3 = (f32[4,2,8,128]{3,1,2,0:T(2,128)S(1)}, f32[4,2,8,128]{3,1,2,0:T(2,128)}, u32[]{:S(2)}) copy-start(f32[4,2,8,128]{3,1,2,0:T(2,128)} %copy-done.2) | copy-start | bytes 98308
  166.6 50.9 %copy-start.7 = (s32[512,1]{0,1:T(1,128)S(1)}, s32[512,1]{0,1:T(1,128)}, u32[]{:S(2)}) copy-start(s32[512,1]{0,1:T(1,128)} %param.27) | copy-start | bytes 6148
  166.6 7.9 %collective-permute-start = (f32[8192]{0:T(1024)S(1)}, f32[8192]{0:T(1024)S(1)}, u32[]{:S(2)}, u32[]{:S(2)}) collective-permute-start(f32[8192]{0:T(1024)S(1)} %bitcast.67), channel_id=1, source_target_pairs={{0,8},{8,16},{16,24},{24,32},{32,40},{40,48},{48,56},{56,64},{64,7... | collective-permute-start | bytes 98312 | tf_op jit(solution)/shard_map/ppermute | solution.py:16
  178.6 4.3 %collective-permute-start.1 = (f32[16,257]{1,0:T(8,128)S(1)}, f32[16,257]{1,0:T(8,128)S(1)}, u32[]{:S(2)}, u32[]{:S(2)}) collective-permute-start(f32[16,257]{1,0:T(8,128)S(1)} %pad_maximum_fusion), channel_id=1, source_target_pairs={{0,1},{1,0},{2,3},{3,2},{4,5},{5,4},{6,7},{7,6},{8,9},{9,8},{10,11... | collective-permute-start | bytes 49352 | tf_op jit(solution)/shard_map/ppermute | solution.py:23
  182.9 2.7 %collective-permute-start.2 = (f32[16,257]{1,0:T(8,128)S(1)}, f32[16,257]{1,0:T(8,128)S(1)}, u32[]{:S(2)}, u32[]{:S(2)}) collective-permute-start(f32[16,257]{1,0:T(8,128)S(1)} %fusion.25), channel_id=1, source_target_pairs={{0,2},{1,3},{2,0},{3,1},{4,6},{5,7},{6,4},{7,5},{8,10},{9,11},{10,... | collective-permute-start | bytes 49352 | tf_op jit(solution)/shard_map/ppermute | solution.py:23
  185.6 4.2 %collective-permute-start.3 = (f32[16,257]{1,0:T(8,128)S(1)}, f32[16,257]{1,0:T(8,128)S(1)}, u32[]{:S(2)}, u32[]{:S(2)}) collective-permute-start(f32[16,257]{1,0:T(8,128)S(1)} %add.71), channel_id=1, source_target_pairs={{0,4},{1,5},{2,6},{3,7},{4,0},{5,1},{6,2},{7,3},{8,12},{9,13},{10,... | collective-permute-start | bytes 49352 | tf_op jit(solution)/shard_map/ppermute | solution.py:23
  190.0 6.5 %collective-permute-start.4 = (f32[16,256]{1,0:T(8,128)S(1)}, f32[16,256]{1,0:T(8,128)S(1)}, u32[]{:S(2)}, u32[]{:S(2)}) collective-permute-start(f32[16,256]{1,0:T(8,128)S(1)} %slice_divide_fusion), channel_id=1, source_target_pairs={{0,128},{8,136},{16,144},{24,152},{32,160},{40,168},{48,176},{56,1... | collective-permute-start | bytes 49160 | tf_op jit(solution)/shard_map/ppermute | solution.py:33
  196.5 3.7 %collective-permute-start.5 = (f32[32,256]{1,0:T(8,128)S(1)}, f32[32,256]{1,0:T(8,128)S(1)}, u32[]{:S(2)}, u32[]{:S(2)}) collective-permute-start(f32[32,256]{1,0:T(8,128)S(1)} %maximum_select_fusion.5), channel_id=1, source_target_pairs={{0,64},{8,72},{16,80},{24,88},{32,96},{40,104},{48,112},{56,120},{... | collective-permute-start | bytes 98312 | tf_op jit(solution)/shard_map/ppermute | solution.py:33
  200.2 4.6 %collective-permute-start.6 = (f32[64,256]{1,0:T(8,128)S(1)}, f32[64,256]{1,0:T(8,128)S(1)}, u32[]{:S(2)}, u32[]{:S(2)}) collective-permute-start(f32[64,256]{1,0:T(8,128)S(1)} %maximum_select_fusion.4), channel_id=1, source_target_pairs={{0,32},{8,40},{16,48},{24,56},{32,0},{40,8},{48,16},{56,24},{64,96... | collective-permute-start | bytes 196616 | tf_op jit(solution)/shard_map/ppermute | solution.py:33
  204.8 4.8 %collective-permute-start.7 = (f32[128,256]{1,0:T(8,128)S(1)}, f32[128,256]{1,0:T(8,128)S(1)}, u32[]{:S(2)}, u32[]{:S(2)}) collective-permute-start(f32[128,256]{1,0:T(8,128)S(1)} %maximum_select_fusion.3), channel_id=1, source_target_pairs={{0,16},{8,24},{16,0},{24,8},{32,48},{40,56},{48,32},{56,40},{64,80... | collective-permute-start | bytes 393224 | tf_op jit(solution)/shard_map/ppermute | solution.py:33
  209.6 9.0 %collective-permute-start.8 = (f32[256,256]{1,0:T(8,128)S(1)}, f32[256,256]{1,0:T(8,128)S(1)}, u32[]{:S(2)}, u32[]{:S(2)}) collective-permute-start(f32[256,256]{1,0:T(8,128)S(1)} %maximum_select_fusion.2), channel_id=1, source_target_pairs={{0,8},{8,0},{16,24},{24,16},{32,40},{40,32},{48,56},{56,48},{64,72... | collective-permute-start | bytes 786440 | tf_op jit(solution)/shard_map/ppermute | solution.py:33
Sparse Core Ops, SparseCore 0:
  56.2 70.1 all-gather.1

commit v4 on v2

--- a/solution.py
+++ b/solution.py
@@ -41,9 +41,11 @@
     return block
 
 
-def bit_reversed(count):
-    width = count.bit_length() - 1
-    return [int(format(i, f"0{width}b")[::-1], 2) for i in range(count)]
+def bit_reversed(rows, count):
+    bits = count.bit_length() - 1
+    shaped = rows.reshape((2,) * bits + (rows.shape[0] // count,) + rows.shape[1:])
+    twisted = tuple(range(bits - 1, -1, -1)) + tuple(range(bits, shaped.ndim))
+    return shaped.transpose(twisted).reshape(rows.shape)
 
 
 def per_device(
@@ -119,15 +121,14 @@
     q_out = jnp.einsum("qtk,kl->qtl", query_out.astype(jnp.float32), basis_cut, precision=highest)
     q_in = jnp.einsum("qtk,kl->qtl", query_in.astype(jnp.float32), basis_in_wide, precision=highest)
     outer = jnp.einsum("qti,qtj->qij", q_out, q_in, precision=highest)
-    query_grad = lax.all_gather(
+    query_grad = butterfly_gather(
         (outer.reshape(query_in.shape[0], rank_slice * rank_in) * scale[None, :]).astype(jnp.bfloat16),
         "dp",
-        axis=0,
-        tiled=True,
     )
     part = lax.dot_general(
         grad_low, query_grad, (((1,), (1,)), ((), ())), preferred_element_type=jnp.float32
     )
+    part = bit_reversed(part.T, data_count).T
 
     totals = butterfly_sum(jnp.concatenate([part, self_part[:, None]], axis=1), "factor")
     relative = totals[:, :-1] / jnp.sqrt(totals[:, -1:] + EPSILON)
@@ -139,9 +140,9 @@
     earlier = (own_all[None, :] == own_all[:, None]) & (numbers[None, :] < numbers[:, None])
     rank_all = jnp.sum(earlier.astype(jnp.int32), axis=1)
     slots = jnp.arange(OWN_CAP, dtype=jnp.int32)[:, None]
-    arrival = jnp.asarray(bit_reversed(data_count), jnp.int32)
-    order = (arrival[:, None] * pieces + jnp.arange(pieces, dtype=jnp.int32)[None, :]).reshape(-1)
-    placing = ((own_all[order][None, :] == data_index) & (rank_all[order][None, :] == slots)).astype(
+    own_arrived = bit_reversed(own_all, data_count)
+    rank_arrived = bit_reversed(rank_all, data_count)
+    placing = ((own_arrived[None, :] == data_index) & (rank_arrived[None, :] == slots)).astype(
         jnp.float32
     )
     return jnp.dot(placing, relative_all, precision=highest)

time: 206 us -> 183 us (0.89)
  waiting for transfers between devices: 120 us -> 82.1 us
  starting transfers between devices: 32.6 us -> 60.3 us
  between operations: 15 us -> 1.77 us
  local copies, waits for them, and re-layouts: 14.6 us -> 9.82 us
  other arithmetic: 6.77 us -> 11.2 us
    all_to_all x1, waiting for transfers between devices: 68 us -> 34.3 us  [per_device(): gathered_parts = lax.all_to_all(stacked_parts, 'factor', 0, 0, tiled=True)]
    ppermute x5 -> x10, starting transfers between devices: 13 us -> 33.8 us  [butterfly_gather(): other = lax.ppermute(block, axis, [(i, i ^ step) for i in range(size)])]
    all_to_all x1, waiting for transfers between devices: 28.5 us -> 14.9 us  [per_device(): received = lax.all_to_all(sending, 'factor', 0, 0, tiled=True)]
    ppermute x5 -> x10, waiting for transfers between devices: 14.1 us -> 27.6 us  [butterfly_gather(): other = lax.ppermute(block, axis, [(i, i ^ step) for i in range(size)])]
    gather x2 -> x0, local copies, waits for them, and re-layouts: 7.02 us -> none  [the longest x1 3.51 us: per_device(): rank_all[order][None, :] == slots]
    ppermute x3, starting transfers between devices: 1.94 us -> 7.24 us  [butterfly_sum(): lax.ppermute(block, axis, [(i, i ^ step) for i in range(size)])]
    select_n x4 -> x8, other arithmetic: 0.04 us -> 5.28 us  [butterfly_gather(): jnp.where(upper, jnp.concatenate([other, block], axis=0), jnp.concatenate...]
    ppermute x3, waiting for transfers between devices: 9.36 us -> 5.25 us  [butterfly_sum(): lax.ppermute(block, axis, [(i, i ^ step) for i in range(size)])]
  transfers between devices with their start and end apart: 12 -> 16, of which waited for: 9 -> 14; matrix products, arithmetic and copies ran while one was open for 11% -> 11% of each run, Pallas kernels for 0% -> 0%
where the time goes in v4:
time: 183 us; the launch traced here: 182 us
  waiting for transfers between devices  82.1 us (45%)
  starting transfers between devices  60.3 us (33%)
  matrix products  17 us (9%)
  other arithmetic  11.2 us (6%)
  local copies, waits for them, and re-layouts  9.82 us (5%)
    all_to_all x1, waiting for transfers between devices, per_device(): gathered_parts = lax.all_to_all(stacked_parts, 'factor', 0, 0, tiled=True)  34.3 us
    ppermute x10, starting transfers between devices, butterfly_gather(): other = lax.ppermute(block, axis, [(i, i ^ step) for i in range(size)])  33.8 us
    ppermute x10, waiting for transfers between devices, butterfly_gather(): other = lax.ppermute(block, axis, [(i, i ^ step) for i in range(size)])  27.6 us
    all_to_all x1, waiting for transfers between devices, per_device(): received = lax.all_to_all(sending, 'factor', 0, 0, tiled=True)  14.9 us
    all_to_all x1, starting transfers between devices, per_device(): gathered_parts = lax.all_to_all(stacked_parts, 'factor', 0, 0, tiled=True)  7.61 us
    ppermute x3, starting transfers between devices, butterfly_sum(): lax.ppermute(block, axis, [(i, i ^ step) for i in range(size)])  7.24 us
    ppermute x1, starting transfers between devices, from_behind(): return lax.ppermute(block, axis, route)  7.12 us
    select_n x8, other arithmetic, butterfly_gather(): jnp.where(upper, jnp.concatenate([other, block], axis=0), jnp.concatenate...  5.28 us
  transfers between devices with their start and end apart: 16, of which 14 were waited for; matrix products, arithmetic and copies ran while one was open for 11% of the time, Pallas kernels for 0%

profile of v4, /device:TPU:1, one launch (start us, length us, event | category | flops | bytes accessed | tf_op | source)
XLA Modules:
  0.0 182.1 jit_solution(6804561370158574297)
XLA Ops:
  0.0 1.6 copy-done
  1.6 1.7 fusion.41
  3.3 5.2 %fusion.40 = f32[2048,256]{0,1:T(8,128)S(1)} fusion(bf16[2048,1792]{1,0:T(8,128)(2,1)} %param.16, bf16[1792,256]{1,0:T(8,128)(2,1)S(1)} %copy-done.10), kind=kOutput, calls=%fused_computation.73 | convolution fusion | flops 1879048192 | bytes 10354688 | tf_op jit(solution)/shard_map/dot_general | solution.py:78
  8.8 2.3 %copy.78 = f32[64,8,8,256]{3,2,0,1:T(8,128)} copy(f32[64,8,8,256]{3,2,1,0:T(8,128)S(1)} %bitcast.65) | data formatting | bytes 8388608 | tf_op jit(solution)/shard_map/all_to_all | solution.py:81
  11.1 7.6 %all-to-all-start = ((f32[8,256,512]{1,2,0:T(8,128)}), f32[8,256,512]{1,2,0:T(8,128)}, u32[]{:S(2)}, u32[]{:S(2)}) async-start(f32[8,256,512]{1,2,0:T(8,128)} %bitcast.64), calls=%async_computation | async-start | bytes 8388608 | tf_op jit(solution)/shard_map/all_to_all | solution.py:81
  19.9 7.0 %collective-permute-start = (bf16[8,8192]{1,0:T(8,128)(2,1)S(1)}, bf16[8,8192]{1,0:T(8,128)(2,1)S(1)}, u32[]{:S(2)}, u32[]{:S(2)}) collective-permute-start(bf16[8,8192]{1,0:T(8,128)(2,1)S(1)} %multiply_convert_fusion), channel_id=1, source_target_pairs={{0,128},{8,136},{16,144},{24,152},{32,160},{40,168},{48,176},{56,1... | collective-permute-start | bytes 393224 | tf_op jit(solution)/shard_map/ppermute | solution.py:33
  27.1 2.7 %collective-permute-done = bf16[8,8192]{1,0:T(8,128)(2,1)S(1)} collective-permute-done((bf16[8,8192]{1,0:T(8,128)(2,1)S(1)}, bf16[8,8192]{1,0:T(8,128)(2,1)S(1)}, u32[]{:S(2)}, u32[]{:S(2)}) %collective-permute-start) | collective-permute-done | bytes 131104 | tf_op jit(solution)/shard_map/ppermute | solution.py:33
  29.8 4.8 %collective-permute-start.1 = (bf16[16,8192]{1,0:T(8,128)(2,1)S(1)}, bf16[16,8192]{1,0:T(8,128)(2,1)S(1)}, u32[]{:S(2)}, u32[]{:S(2)}) collective-permute-start(bf16[16,8192]{1,0:T(8,128)(2,1)S(1)} %maximum_select_fusion.7), channel_id=1, source_target_pairs={{0,64},{8,72},{16,80},{24,88},{32,96},{40,104},{48,112},{56,120},{... | collective-permute-start | bytes 786440 | tf_op jit(solution)/shard_map/ppermute | solution.py:33
  34.6 34.3 %all-to-all-done = f32[8,256,512]{1,2,0:T(8,128)} async-done(((f32[8,256,512]{1,2,0:T(8,128)}), f32[8,256,512]{1,2,0:T(8,128)}, u32[]{:S(2)}, u32[]{:S(2)}) %all-to-all-start) | async-done | bytes 4194336 | tf_op jit(solution)/shard_map/all_to_all | solution.py:81
  68.9 2.5 %reduce_sum.28 = f32[256,512]{0,1:T(8,128)S(1)} reduce(f32[8,256,512]{1,2,0:T(8,128)} %all-to-all-done, f32[]{:T(128)} %constant.181.clone.1), dimensions={0}, to_apply=%region_2.3 | reduce | flops 917504 | bytes 4718596 | tf_op jit(solution)/shard_map/reduce_sum | solution.py:82
  73.8 4.5 %all-to-all-start.1 = ((f32[8,256,288]{1,2,0:T(8,128)}), f32[8,256,288]{1,2,0:T(8,128)}, u32[]{:S(2)}, u32[]{:S(2)}) async-start(f32[8,256,288]{1,2,0:T(8,128)} %pad_maximum_fusion.1), calls=%async_computation.1 | async-start | bytes 4718592 | tf_op jit(solution)/shard_map/all_to_all | solution.py:91
  78.4 1.7 collective-permute-start.2
  82.3 8.3 %collective-permute-done.2 = bf16[32,8192]{1,0:T(8,128)(2,1)} collective-permute-done((bf16[32,8192]{1,0:T(8,128)(2,1)S(1)}, bf16[32,8192]{1,0:T(8,128)(2,1)}, u32[]{:S(2)}, u32[]{:S(2)}) %collective-permute-start.2) | collective-permute-done | bytes 524320 | tf_op jit(solution)/shard_map/ppermute | solution.py:33
  90.6 1.8 maximum_select_fusion.3
  93.0 14.9 %all-to-all-done.1 = f32[8,256,288]{1,2,0:T(8,128)} async-done(((f32[8,256,288]{1,2,0:T(8,128)}), f32[8,256,288]{1,2,0:T(8,128)}, u32[]{:S(2)}, u32[]{:S(2)}) %all-to-all-start.1) | async-done | bytes 2359328 | tf_op jit(solution)/shard_map/all_to_all | solution.py:91
  107.8 1.9 %copy.71 = f32[8,36,8,256]{3,2,0,1:T(8,128)S(1)} copy(f32[8,36,8,256]{3,2,1,0:T(8,128)} %bitcast.26) | data formatting | bytes 4718592 | tf_op jit(solution)/shard_map/all_to_all | solution.py:91
  110.3 3.5 %fusion.7 = f32[512,256]{1,0:T(8,128)S(1)} fusion(f32[2048,512]{0,1:T(8,128)S(1)} %bitcast.66, f32[2048,288]{0,1:T(8,128)S(1)} %bitcast.68), kind=kOutput, calls=%fused_computation.11 | convolution fusion | flops 3221225472 | bytes 6815744 | tf_op jit(solution)/shard_map/dot_general | solution.py:105
  114.6 7.1 %collective-permute-start.5 = (f32[8192]{0:T(1024)S(1)}, f32[8192]{0:T(1024)S(1)}, u32[]{:S(2)}, u32[]{:S(2)}) collective-permute-start(f32[8192]{0:T(1024)S(1)} %bitcast.78), channel_id=1, source_target_pairs={{0,8},{8,16},{16,24},{24,32},{32,40},{40,48},{48,56},{56,64},{64,7... | collective-permute-start | bytes 98312 | tf_op jit(solution)/shard_map/ppermute | solution.py:16
  121.8 4.1 %collective-permute-done.3 = bf16[64,8192]{1,0:T(8,128)(2,1)} collective-permute-done((bf16[64,8192]{1,0:T(8,128)(2,1)S(1)}, bf16[64,8192]{1,0:T(8,128)(2,1)}, u32[]{:S(2)}, u32[]{:S(2)}) %collective-permute-start.3) | collective-permute-done | bytes 1048608 | tf_op jit(solution)/shard_map/ppermute | solution.py:33
  125.8 3.3 %maximum_select_fusion.2 = bf16[128,8192]{1,0:T(8,128)(2,1)} fusion(bf16[64,8192]{1,0:T(8,128)(2,1)S(1)} %maximum_select_fusion.3, bf16[64,8192]{1,0:T(8,128)(2,1)} %collective-permute-done.3, pred[]{:T(512)S(6)} %eq.95), kind=kLoop, calls=%fused_computation.13 | loop fusion | flops 9437184 | bytes 4194305 | tf_op jit(solution)/shard_map/jit(_where)/select_n | solution.py:35
  129.2 2.4 %collective-permute-start.4 = (bf16[128,8192]{1,0:T(8,128)(2,1)}, bf16[128,8192]{1,0:T(8,128)(2,1)}, u32[]{:S(2)}, u32[]{:S(2)}) collective-permute-start(bf16[128,8192]{1,0:T(8,128)(2,1)} %maximum_select_fusion.2), channel_id=1, source_target_pairs={{0,8},{8,0},{16,24},{24,16},{32,40},{40,32},{48,56},{56,48},{64,72... | collective-permute-start | bytes 6291464 | tf_op jit(solution)/shard_map/ppermute | solution.py:33
  133.5 2.3 %collective-permute-done.4 = bf16[128,8192]{1,0:T(8,128)(2,1)} collective-permute-done((bf16[128,8192]{1,0:T(8,128)(2,1)}, bf16[128,8192]{1,0:T(8,128)(2,1)}, u32[]{:S(2)}, u32[]{:S(2)}) %collective-permute-start.4) | collective-permute-done | bytes 2097184 | tf_op jit(solution)/shard_map/ppermute | solution.py:33
  135.8 4.3 %fusion = f32[256,16]{1,0:T(8,128)S(1)} fusion(bf16[128,8192]{1,0:T(8,128)(2,1)} %maximum_select_fusion.2, bf16[128,8192]{1,0:T(8,128)(2,1)} %collective-permute-done.4, pred[]{:T(512)S(6)} %eq.94, f32[16,8192]{1,0:T(8,128)S(1)} %scatter-mul.4), kind=kOutput, calls=%fused_computation.2 | convolution fusion | flops 86114304 | bytes 4734977 | tf_op jit(solution)/shard_map/dot_general | solution.py:128
  140.1 4.4 %collective-permute-start.6 = (f32[16,257]{1,0:T(8,128)S(1)}, f32[16,257]{1,0:T(8,128)S(1)}, u32[]{:S(2)}, u32[]{:S(2)}) collective-permute-start(f32[16,257]{1,0:T(8,128)S(1)} %pad_maximum_fusion.2), channel_id=1, source_target_pairs={{0,1},{1,0},{2,3},{3,2},{4,5},{5,4},{6,7},{7,6},{8,9},{9,8},{10,11... | collective-permute-start | bytes 49352 | tf_op jit(solution)/shard_map/ppermute | solution.py:23
  146.1 2.3 %collective-permute-done.7 = f32[16,257]{1,0:T(8,128)S(1)} collective-permute-done((f32[16,257]{1,0:T(8,128)S(1)}, f32[16,257]{1,0:T(8,128)S(1)}, u32[]{:S(2)}, u32[]{:S(2)}) %collective-permute-start.7) | collective-permute-done | bytes 16480 | tf_op jit(solution)/shard_map/ppermute | solution.py:23
  148.4 2.5 %collective-permute-start.8 = (f32[16,257]{1,0:T(8,128)S(1)}, f32[16,257]{1,0:T(8,128)S(1)}, u32[]{:S(2)}, u32[]{:S(2)}) collective-permute-start(f32[16,257]{1,0:T(8,128)S(1)} %add.76), channel_id=1, source_target_pairs={{0,4},{1,5},{2,6},{3,7},{4,0},{5,1},{6,2},{7,3},{8,12},{9,13},{10,... | collective-permute-start | bytes 49352 | tf_op jit(solution)/shard_map/ppermute | solution.py:23
  150.9 1.7 collective-permute-done.8
  152.8 7.3 %collective-permute-start.9 = (f32[16,256]{1,0:T(8,128)S(1)}, f32[16,256]{1,0:T(8,128)S(1)}, u32[]{:S(2)}, u32[]{:S(2)}) collective-permute-start(f32[16,256]{1,0:T(8,128)S(1)} %slice_divide_fusion), channel_id=1, source_target_pairs={{0,128},{8,136},{16,144},{24,152},{32,160},{40,168},{48,176},{56,1... | collective-permute-start | bytes 49160 | tf_op jit(solution)/shard_map/ppermute | solution.py:33
  162.7 2.5 %collective-permute-done.10 = f32[32,256]{1,0:T(8,128)S(1)} collective-permute-done((f32[32,256]{1,0:T(8,128)S(1)}, f32[32,256]{1,0:T(8,128)S(1)}, u32[]{:S(2)}, u32[]{:S(2)}) %collective-permute-start.10) | collective-permute-done | bytes 32800 | tf_op jit(solution)/shard_map/ppermute | solution.py:33
  166.1 2.3 %collective-permute-done.11 = f32[64,256]{1,0:T(8,128)S(1)} collective-permute-done((f32[64,256]{1,0:T(8,128)S(1)}, f32[64,256]{1,0:T(8,128)S(1)}, u32[]{:S(2)}, u32[]{:S(2)}) %collective-permute-start.11) | collective-permute-done | bytes 65568 | tf_op jit(solution)/shard_map/ppermute | solution.py:33
  168.6 3.8 %collective-permute-done.12 = f32[128,256]{1,0:T(8,128)S(1)} collective-permute-done((f32[128,256]{1,0:T(8,128)S(1)}, f32[128,256]{1,0:T(8,128)S(1)}, u32[]{:S(2)}, u32[]{:S(2)}) %collective-permute-start.12) | collective-permute-done | bytes 131104 | tf_op jit(solution)/shard_map/ppermute | solution.py:33
  172.4 7.6 %collective-permute-start.13 = (f32[256,256]{1,0:T(8,128)S(1)}, f32[256,256]{1,0:T(8,128)S(1)}, u32[]{:S(2)}, u32[]{:S(2)}) collective-permute-start(f32[256,256]{1,0:T(8,128)S(1)} %maximum_select_fusion.8), channel_id=1, source_target_pairs={{0,8},{8,0},{16,24},{24,16},{32,40},{40,32},{48,56},{56,48},{64,72... | collective-permute-start | bytes 786440 | tf_op jit(solution)/shard_map/ppermute | solution.py:33
  (86 shorter events, 16.0 us)
Async XLA Ops:
  0.0 1.6 copy-start
  0.0 3.3 %copy-start.10 = (bf16[1792,256]{1,0:T(8,128)(2,1)S(1)}, bf16[1792,256]{1,0:T(8,128)(2,1)}, u32[]{:S(2)}) copy-start(bf16[1792,256]{1,0:T(8,128)(2,1)} %param.18) | copy-start | bytes 2752516
  11.1 7.6 %copy-start.6 = (f32[32,256]{1,0:T(8,128)S(1)}, f32[32,256]{1,0:T(8,128)}, u32[]{:S(2)}) copy-start(f32[32,256]{1,0:T(8,128)} %param.22) | copy-start | bytes 98308
  11.1 7.7 %copy-start.4 = (bf16[256,256]{1,0:T(8,128)(2,1)S(1)}, bf16[256,256]{1,0:T(8,128)(2,1)}, u32[]{:S(2)}) copy-start(bf16[256,256]{1,0:T(8,128)(2,1)} %param.21) | copy-start | bytes 393220
  11.1 7.7 %copy-start.11 = (bf16[8,8,256]{2,1,0:T(8,128)(2,1)S(1)}, bf16[8,8,256]{2,1,0:T(8,128)(2,1)}, u32[]{:S(2)}) copy-start(bf16[8,8,256]{2,1,0:T(8,128)(2,1)} %param.24) | copy-start | bytes 98308
  11.1 7.9 %copy-start.3 = (bf16[256,256]{1,0:T(8,128)(2,1)S(1)}, bf16[256,256]{1,0:T(8,128)(2,1)}, u32[]{:S(2)}) copy-start(bf16[256,256]{1,0:T(8,128)(2,1)} %param.20) | copy-start | bytes 393220
  11.1 7.9 %copy-start.5 = (bf16[8,8,256]{2,1,0:T(8,128)(2,1)S(1)}, bf16[8,8,256]{2,1,0:T(8,128)(2,1)}, u32[]{:S(2)}) copy-start(bf16[8,8,256]{2,1,0:T(8,128)(2,1)} %param.23) | copy-start | bytes 98308
  11.1 15.7 %copy-start.9 = (s32[1,16]{1,0:T(1,128)S(1)}, s32[1,16]{1,0:T(1,128)}, u32[]{:S(2)}) copy-start(s32[1,16]{1,0:T(1,128)} %param.25) | copy-start | bytes 196
  11.1 57.8 %all-to-all-start = ((f32[8,256,512]{1,2,0:T(8,128)}), f32[8,256,512]{1,2,0:T(8,128)}, u32[]{:S(2)}, u32[]{:S(2)}) async-start(f32[8,256,512]{1,2,0:T(8,128)} %bitcast.64), calls=%async_computation | async-start | bytes 8388608 | tf_op jit(solution)/shard_map/all_to_all | solution.py:81
  19.9 9.9 %collective-permute-start = (bf16[8,8192]{1,0:T(8,128)(2,1)S(1)}, bf16[8,8192]{1,0:T(8,128)(2,1)S(1)}, u32[]{:S(2)}, u32[]{:S(2)}) collective-permute-start(bf16[8,8192]{1,0:T(8,128)(2,1)S(1)} %multiply_convert_fusion), channel_id=1, source_target_pairs={{0,128},{8,136},{16,144},{24,152},{32,160},{40,168},{48,176},{56,1... | collective-permute-start | bytes 393224 | tf_op jit(solution)/shard_map/ppermute | solution.py:33
  29.8 48.5 %collective-permute-start.1 = (bf16[16,8192]{1,0:T(8,128)(2,1)S(1)}, bf16[16,8192]{1,0:T(8,128)(2,1)S(1)}, u32[]{:S(2)}, u32[]{:S(2)}) collective-permute-start(bf16[16,8192]{1,0:T(8,128)(2,1)S(1)} %maximum_select_fusion.7), channel_id=1, source_target_pairs={{0,64},{8,72},{16,80},{24,88},{32,96},{40,104},{48,112},{56,120},{... | collective-permute-start | bytes 786440 | tf_op jit(solution)/shard_map/ppermute | solution.py:33
  73.8 6.3 %copy-start.8 = (s32[32]{0:T(128)S(1)}, s32[32]{0:T(128)}, u32[]{:S(2)}) copy-start(s32[32]{0:T(128)} %param.26) | copy-start | bytes 388
  73.8 34.0 %all-to-all-start.1 = ((f32[8,256,288]{1,2,0:T(8,128)}), f32[8,256,288]{1,2,0:T(8,128)}, u32[]{:S(2)}, u32[]{:S(2)}) async-start(f32[8,256,288]{1,2,0:T(8,128)} %pad_maximum_fusion.1), calls=%async_computation.1 | async-start | bytes 4718592 | tf_op jit(solution)/shard_map/all_to_all | solution.py:91
  78.4 3.9 %copy-start.2 = (bf16[32,8192]{1,0:T(8,128)(2,1)}, bf16[32,8192]{1,0:T(8,128)(2,1)S(1)}, u32[]{:S(2)}) copy-start(bf16[32,8192]{1,0:T(8,128)(2,1)S(1)} %maximum_select_fusion.4) | copy-start | bytes 1572868
  78.4 12.2 %collective-permute-start.2 = (bf16[32,8192]{1,0:T(8,128)(2,1)S(1)}, bf16[32,8192]{1,0:T(8,128)(2,1)}, u32[]{:S(2)}, u32[]{:S(2)}) collective-permute-start(bf16[32,8192]{1,0:T(8,128)(2,1)S(1)} %maximum_select_fusion.4), channel_id=1, source_target_pairs={{0,32},{8,40},{16,48},{24,56},{32,0},{40,8},{48,16},{56,24},{64,96... | collective-permute-start | bytes 1572872 | tf_op jit(solution)/shard_map/ppermute | solution.py:33
  92.4 33.5 %collective-permute-start.3 = (bf16[64,8192]{1,0:T(8,128)(2,1)S(1)}, bf16[64,8192]{1,0:T(8,128)(2,1)}, u32[]{:S(2)}, u32[]{:S(2)}) collective-permute-start(bf16[64,8192]{1,0:T(8,128)(2,1)S(1)} %maximum_select_fusion.3), channel_id=1, source_target_pairs={{0,16},{8,24},{16,0},{24,8},{32,48},{40,56},{48,32},{56,40},{64,80... | collective-permute-start | bytes 3145736 | tf_op jit(solution)/shard_map/ppermute | solution.py:33
  113.8 0.8 copy-start.1
  114.6 18.2 %collective-permute-start.5 = (f32[8192]{0:T(1024)S(1)}, f32[8192]{0:T(1024)S(1)}, u32[]{:S(2)}, u32[]{:S(2)}) collective-permute-start(f32[8192]{0:T(1024)S(1)} %bitcast.78), channel_id=1, source_target_pairs={{0,8},{8,16},{16,24},{24,32},{32,40},{40,48},{48,56},{56,64},{64,7... | collective-permute-start | bytes 98312 | tf_op jit(solution)/shard_map/ppermute | solution.py:16
  129.2 6.6 %collective-permute-start.4 = (bf16[128,8192]{1,0:T(8,128)(2,1)}, bf16[128,8192]{1,0:T(8,128)(2,1)}, u32[]{:S(2)}, u32[]{:S(2)}) collective-permute-start(bf16[128,8192]{1,0:T(8,128)(2,1)} %maximum_select_fusion.2), channel_id=1, source_target_pairs={{0,8},{8,0},{16,24},{24,16},{32,40},{40,32},{48,56},{56,48},{64,72... | collective-permute-start | bytes 6291464 | tf_op jit(solution)/shard_map/ppermute | solution.py:33
  133.5 46.6 %copy-start.7 = (s32[512,1]{0,1:T(1,128)S(1)}, s32[512,1]{0,1:T(1,128)}, u32[]{:S(2)}) copy-start(s32[512,1]{0,1:T(1,128)} %param.27) | copy-start | bytes 6148
  140.1 5.6 %collective-permute-start.6 = (f32[16,257]{1,0:T(8,128)S(1)}, f32[16,257]{1,0:T(8,128)S(1)}, u32[]{:S(2)}, u32[]{:S(2)}) collective-permute-start(f32[16,257]{1,0:T(8,128)S(1)} %pad_maximum_fusion.2), channel_id=1, source_target_pairs={{0,1},{1,0},{2,3},{3,2},{4,5},{5,4},{6,7},{7,6},{8,9},{9,8},{10,11... | collective-permute-start | bytes 49352 | tf_op jit(solution)/shard_map/ppermute | solution.py:23
  145.8 2.7 %collective-permute-start.7 = (f32[16,257]{1,0:T(8,128)S(1)}, f32[16,257]{1,0:T(8,128)S(1)}, u32[]{:S(2)}, u32[]{:S(2)}) collective-permute-start(f32[16,257]{1,0:T(8,128)S(1)} %fusion.38), channel_id=1, source_target_pairs={{0,2},{1,3},{2,0},{3,1},{4,6},{5,7},{6,4},{7,5},{8,10},{9,11},{10,... | collective-permute-start | bytes 49352 | tf_op jit(solution)/shard_map/ppermute | solution.py:23
  148.4 4.2 %collective-permute-start.8 = (f32[16,257]{1,0:T(8,128)S(1)}, f32[16,257]{1,0:T(8,128)S(1)}, u32[]{:S(2)}, u32[]{:S(2)}) collective-permute-start(f32[16,257]{1,0:T(8,128)S(1)} %add.76), channel_id=1, source_target_pairs={{0,4},{1,5},{2,6},{3,7},{4,0},{5,1},{6,2},{7,3},{8,12},{9,13},{10,... | collective-permute-start | bytes 49352 | tf_op jit(solution)/shard_map/ppermute | solution.py:23
  152.8 8.4 %collective-permute-start.9 = (f32[16,256]{1,0:T(8,128)S(1)}, f32[16,256]{1,0:T(8,128)S(1)}, u32[]{:S(2)}, u32[]{:S(2)}) collective-permute-start(f32[16,256]{1,0:T(8,128)S(1)} %slice_divide_fusion), channel_id=1, source_target_pairs={{0,128},{8,136},{16,144},{24,152},{32,160},{40,168},{48,176},{56,1... | collective-permute-start | bytes 49160 | tf_op jit(solution)/shard_map/ppermute | solution.py:33
  161.3 4.0 %collective-permute-start.10 = (f32[32,256]{1,0:T(8,128)S(1)}, f32[32,256]{1,0:T(8,128)S(1)}, u32[]{:S(2)}, u32[]{:S(2)}) collective-permute-start(f32[32,256]{1,0:T(8,128)S(1)} %maximum_select_fusion.11), channel_id=1, source_target_pairs={{0,64},{8,72},{16,80},{24,88},{32,96},{40,104},{48,112},{56,120},{... | collective-permute-start | bytes 98312 | tf_op jit(solution)/shard_map/ppermute | solution.py:33
  165.2 3.2 %collective-permute-start.11 = (f32[64,256]{1,0:T(8,128)S(1)}, f32[64,256]{1,0:T(8,128)S(1)}, u32[]{:S(2)}, u32[]{:S(2)}) collective-permute-start(f32[64,256]{1,0:T(8,128)S(1)} %maximum_select_fusion.10), channel_id=1, source_target_pairs={{0,32},{8,40},{16,48},{24,56},{32,0},{40,8},{48,16},{56,24},{64,96... | collective-permute-start | bytes 196616 | tf_op jit(solution)/shard_map/ppermute | solution.py:33
  168.5 3.9 %collective-permute-start.12 = (f32[128,256]{1,0:T(8,128)S(1)}, f32[128,256]{1,0:T(8,128)S(1)}, u32[]{:S(2)}, u32[]{:S(2)}) collective-permute-start(f32[128,256]{1,0:T(8,128)S(1)} %maximum_select_fusion.9), channel_id=1, source_target_pairs={{0,16},{8,24},{16,0},{24,8},{32,48},{40,56},{48,32},{56,40},{64,80... | collective-permute-start | bytes 393224 | tf_op jit(solution)/shard_map/ppermute | solution.py:33
  172.4 8.8 %collective-permute-start.13 = (f32[256,256]{1,0:T(8,128)S(1)}, f32[256,256]{1,0:T(8,128)S(1)}, u32[]{:S(2)}, u32[]{:S(2)}) collective-permute-start(f32[256,256]{1,0:T(8,128)S(1)} %maximum_select_fusion.8), channel_id=1, source_target_pairs={{0,8},{8,0},{16,24},{24,16},{32,40},{40,32},{48,56},{56,48},{64,72... | collective-permute-start | bytes 786440 | tf_op jit(solution)/shard_map/ppermute | solution.py:33

commit v5 on v4

--- a/solution.py
+++ b/solution.py
@@ -73,6 +73,8 @@
     data_count = lax.axis_size("dp")
     highest = lax.Precision.HIGHEST
     chunk = tokens_here // factor_count
+    scale = (1.0 / (eigen_values + DAMPING)).reshape(-1)
+    queries = butterfly_gather(jnp.concatenate([query_in, query_out], axis=2), "dp")
 
 
     in_part = jnp.dot(activations, proj_in, preferred_element_type=jnp.float32)
@@ -113,17 +115,19 @@
     )
     grad_rows = grad_rows.at[0].add(joined_prev * preceding)
     grad_rows = grad_rows.at[pieces - 1].multiply(1.0 - joined_next)
-    scale = (1.0 / (eigen_values + DAMPING)).reshape(-1)
     self_part = jnp.sum(grad_rows * grad_rows * scale[None, :], axis=1)
     grad_low = grad_rows.astype(jnp.bfloat16)
 
     basis_cut = lax.dynamic_slice_in_dim(basis_out_wide, factor_index * rank_slice, rank_slice, 1)
-    q_out = jnp.einsum("qtk,kl->qtl", query_out.astype(jnp.float32), basis_cut, precision=highest)
-    q_in = jnp.einsum("qtk,kl->qtl", query_in.astype(jnp.float32), basis_in_wide, precision=highest)
+    q_in = jnp.einsum(
+        "qtk,kl->qtl", queries[:, :, :rank_in].astype(jnp.float32), basis_in_wide, precision=highest
+    )
+    q_out = jnp.einsum(
+        "qtk,kl->qtl", queries[:, :, rank_in:].astype(jnp.float32), basis_cut, precision=highest
+    )
     outer = jnp.einsum("qti,qtj->qij", q_out, q_in, precision=highest)
-    query_grad = butterfly_gather(
-        (outer.reshape(query_in.shape[0], rank_slice * rank_in) * scale[None, :]).astype(jnp.bfloat16),
-        "dp",
+    query_grad = (outer.reshape(queries.shape[0], rank_slice * rank_in) * scale[None, :]).astype(
+        jnp.bfloat16
     )
     part = lax.dot_general(
         grad_low, query_grad, (((1,), (1,)), ((), ())), preferred_element_type=jnp.float32

time: 183 us -> 182 us (level)
  matrix products: 17 us -> 28.2 us
  starting transfers between devices: 60.3 us -> 50.9 us
  waiting for transfers between devices: 82.1 us -> 74.7 us
  local copies, waits for them, and re-layouts: 9.82 us -> 16.4 us
    reshape x0 -> x1, local copies, waits for them, and re-layouts: none -> 9.44 us  [per_device(): outer.reshape(queries.shape[0], rank_slice * rank_in) * scale[None, :]]
    dot_general x1, matrix products: 0.46 us -> 8.94 us  [per_device(): outer = jnp.einsum('qti,qtj->qij', q_out, q_in, precision=highest)]
    all_to_all x1, waiting for transfers between devices: 34.3 us -> 27.9 us  [per_device(): gathered_parts = lax.all_to_all(stacked_parts, 'factor', 0, 0, tiled=True)]
    ppermute x10, waiting for transfers between devices: 27.6 us -> 22 us  [butterfly_gather(): other = lax.ppermute(block, axis, [(i, i ^ step) for i in range(size)])]
    ppermute x3, starting transfers between devices: 7.24 us -> 1.75 us  [butterfly_sum(): lax.ppermute(block, axis, [(i, i ^ step) for i in range(size)])]
    ppermute x3, waiting for transfers between devices: 5.25 us -> 9.31 us  [butterfly_sum(): lax.ppermute(block, axis, [(i, i ^ step) for i in range(size)])]
    ppermute x10, starting transfers between devices: 33.8 us -> 30.6 us  [butterfly_gather(): other = lax.ppermute(block, axis, [(i, i ^ step) for i in range(size)])]
    dot_general x2, matrix products: 0.35 us -> 3.16 us  [the longest x1 1.81 us: per_device(): jnp.einsum('qtk,kl->qtl', queries[:, :, :rank_in].astype(jnp.float32), ba...]
  transfers between devices with their start and end apart: 16 -> 16, of which waited for: 14 -> 14; matrix products, arithmetic and copies ran while one was open for 11% -> 17% of each run, Pallas kernels for 0% -> 0%
where the time goes in v5:
time: 182 us; the launch traced here: 181 us
  waiting for transfers between devices  74.7 us (41%)
  starting transfers between devices  50.9 us (28%)
  matrix products  28.2 us (15%)
  local copies, waits for them, and re-layouts  16.4 us (9%)
  other arithmetic  9.51 us (5%)
    ppermute x10, starting transfers between devices, butterfly_gather(): other = lax.ppermute(block, axis, [(i, i ^ step) for i in range(size)])  30.6 us
    all_to_all x1, waiting for transfers between devices, per_device(): gathered_parts = lax.all_to_all(stacked_parts, 'factor', 0, 0, tiled=True)  27.9 us
    ppermute x10, waiting for transfers between devices, butterfly_gather(): other = lax.ppermute(block, axis, [(i, i ^ step) for i in range(size)])  22 us
    all_to_all x1, waiting for transfers between devices, per_device(): received = lax.all_to_all(sending, 'factor', 0, 0, tiled=True)  15.5 us
    reshape x1, local copies, waits for them, and re-layouts, per_device(): outer.reshape(queries.shape[0], rank_slice * rank_in) * scale[None, :]  9.44 us
    ppermute x3, waiting for transfers between devices, butterfly_sum(): lax.ppermute(block, axis, [(i, i ^ step) for i in range(size)])  9.31 us
    dot_general x1, matrix products, per_device(): outer = jnp.einsum('qti,qtj->qij', q_out, q_in, precision=highest)  8.94 us
    all_to_all x1, starting transfers between devices, per_device(): gathered_parts = lax.all_to_all(stacked_parts, 'factor', 0, 0, tiled=True)  7.6 us
  transfers between devices with their start and end apart: 16, of which 14 were waited for; matrix products, arithmetic and copies ran while one was open for 17% of the time, Pallas kernels for 0%

profile of v5, /device:TPU:1, one launch (start us, length us, event | category | flops | bytes accessed | tf_op | source)
XLA Modules:
  0.0 181.5 jit_solution(14243114326873283887)
XLA Ops:
  0.0 5.5 %fusion.40 = f32[2048,256]{0,1:T(8,128)S(1)} fusion(bf16[2048,1792]{1,0:T(8,128)(2,1)} %param.16, bf16[1792,256]{1,0:T(8,128)(2,1)} %param.18), kind=kOutput, calls=%fused_computation.73 | convolution fusion | flops 1879048192 | bytes 10354688 | tf_op jit(solution)/shard_map/dot_general | solution.py:80
  6.8 2.3 %copy.72 = f32[64,8,8,256]{3,2,0,1:T(8,128)} copy(f32[64,8,8,256]{3,2,1,0:T(8,128)S(1)} %bitcast.62) | data formatting | bytes 8388608 | tf_op jit(solution)/shard_map/all_to_all | solution.py:83
  9.1 7.6 %all-to-all-start = ((f32[8,256,512]{1,2,0:T(8,128)}), f32[8,256,512]{1,2,0:T(8,128)}, u32[]{:S(2)}, u32[]{:S(2)}) async-start(f32[8,256,512]{1,2,0:T(8,128)} %bitcast.61), calls=%async_computation | async-start | bytes 8388608 | tf_op jit(solution)/shard_map/all_to_all | solution.py:83
  16.8 7.0 %collective-permute-start = (bf16[8,8,512]{2,1,0:T(8,128)(2,1)S(1)}, bf16[8,8,512]{2,1,0:T(8,128)(2,1)S(1)}, u32[]{:S(2)}, u32[]{:S(2)}) collective-permute-start(bf16[8,8,512]{2,1,0:T(8,128)(2,1)S(1)} %constant_dynamic-update-slice_fusion), channel_id=1, source_target_pairs={{0,128},{8,136},{16,144},{24,152},{32,160},{40,168},{48,176},{56,1... | collective-permute-start | bytes 196616 | tf_op jit(solution)/shard_map/ppermute | solution.py:33
  23.8 1.7 collective-permute-done
  25.5 1.5 collective-permute-start.1
  27.0 5.7 %collective-permute-done.1 = bf16[16,8,512]{2,1,0:T(8,128)(2,1)S(1)} collective-permute-done((bf16[16,8,512]{2,1,0:T(8,128)(2,1)S(1)}, bf16[16,8,512]{2,1,0:T(8,128)(2,1)S(1)}, u32[]{:S(2)}, u32[]{:S(2)}) %collective-permute-start.1) | collective-permute-done | bytes 131104 | tf_op jit(solution)/shard_map/ppermute | solution.py:33
  32.9 5.6 %collective-permute-done.2 = bf16[32,8,512]{2,1,0:T(8,128)(2,1)S(1)} collective-permute-done((bf16[32,8,512]{2,1,0:T(8,128)(2,1)S(1)}, bf16[32,8,512]{2,1,0:T(8,128)(2,1)S(1)}, u32[]{:S(2)}, u32[]{:S(2)}) %collective-permute-start.2) | collective-permute-done | bytes 262176 | tf_op jit(solution)/shard_map/ppermute | solution.py:33
  39.0 27.9 %all-to-all-done = f32[8,256,512]{1,2,0:T(8,128)} async-done(((f32[8,256,512]{1,2,0:T(8,128)}), f32[8,256,512]{1,2,0:T(8,128)}, u32[]{:S(2)}, u32[]{:S(2)}) %all-to-all-start) | async-done | bytes 4194336 | tf_op jit(solution)/shard_map/all_to_all | solution.py:83
  66.9 2.5 %reduce_sum.28 = f32[256,512]{0,1:T(8,128)S(1)} reduce(f32[8,256,512]{1,2,0:T(8,128)} %all-to-all-done, f32[]{:T(128)} %constant.181.clone.1), dimensions={0}, to_apply=%region_2.3 | reduce | flops 917504 | bytes 4718596 | tf_op jit(solution)/shard_map/reduce_sum | solution.py:84
  70.3 1.6 pad_maximum_fusion.1
  71.9 4.5 %all-to-all-start.1 = ((f32[8,256,288]{1,2,0:T(8,128)}), f32[8,256,288]{1,2,0:T(8,128)}, u32[]{:S(2)}, u32[]{:S(2)}) async-start(f32[8,256,288]{1,2,0:T(8,128)} %pad_maximum_fusion.1), calls=%async_computation.1 | async-start | bytes 4718592 | tf_op jit(solution)/shard_map/all_to_all | solution.py:93
  77.8 3.5 %collective-permute-start.4 = (bf16[128,8,512]{2,1,0:T(8,128)(2,1)S(1)}, bf16[128,8,512]{2,1,0:T(8,128)(2,1)}, u32[]{:S(2)}, u32[]{:S(2)}) collective-permute-start(bf16[128,8,512]{2,1,0:T(8,128)(2,1)S(1)} %maximum_select_fusion.1), channel_id=1, source_target_pairs={{0,8},{8,0},{16,24},{24,16},{32,40},{40,32},{48,56},{56,48},{64,72... | collective-permute-start | bytes 3145736 | tf_op jit(solution)/shard_map/ppermute | solution.py:33
  83.7 1.9 %maximum_select_fusion = bf16[256,8,512]{2,1,0:T(8,128)(2,1)S(1)} fusion(bf16[128,8,512]{2,1,0:T(8,128)(2,1)S(1)} %maximum_select_fusion.1, bf16[128,8,512]{2,1,0:T(8,128)(2,1)} %collective-permute-done.4, pred[]{:T(512)S(6)} %eq.94), kind=kLoop, calls=%fused_computation.8 | loop fusion | flops 3145728 | bytes 4194305 | tf_op jit(solution)/shard_map/jit(_where)/select_n | solution.py:35
  86.9 1.8 fusion.5
  88.7 15.5 %all-to-all-done.1 = f32[8,256,288]{1,2,0:T(8,128)} async-done(((f32[8,256,288]{1,2,0:T(8,128)}), f32[8,256,288]{1,2,0:T(8,128)}, u32[]{:S(2)}, u32[]{:S(2)}) %all-to-all-start.1) | async-done | bytes 2359328 | tf_op jit(solution)/shard_map/all_to_all | solution.py:93
  104.2 1.9 %copy.66 = f32[8,36,8,256]{3,2,0,1:T(8,128)S(1)} copy(f32[8,36,8,256]{3,2,1,0:T(8,128)} %bitcast.26) | data formatting | bytes 4718592 | tf_op jit(solution)/shard_map/all_to_all | solution.py:93
  106.7 3.5 %fusion.2 = f32[512,256]{1,0:T(8,128)S(1)} fusion(f32[2048,512]{0,1:T(8,128)S(1)} %bitcast.63, f32[2048,288]{0,1:T(8,128)S(1)} %bitcast.65), kind=kOutput, calls=%fused_computation.6 | convolution fusion | flops 3221225472 | bytes 6815744 | tf_op jit(solution)/shard_map/dot_general | solution.py:107
  111.0 6.5 %collective-permute-start.5 = (f32[8192]{0:T(1024)S(1)}, f32[8192]{0:T(1024)S(1)}, u32[]{:S(2)}, u32[]{:S(2)}) collective-permute-start(f32[8192]{0:T(1024)S(1)} %bitcast.73), channel_id=1, source_target_pairs={{0,8},{8,16},{16,24},{24,32},{32,40},{40,48},{48,56},{56,64},{64,7... | collective-permute-start | bytes 98312 | tf_op jit(solution)/shard_map/ppermute | solution.py:16
  117.5 8.9 %fusion.39 = f32[256,32,256]{2,1,0:T(8,128)} fusion(f32[256,8,32]{2,1,0:T(8,128)S(1)} %fusion.7, f32[256,8,256]{2,1,0:T(8,128)S(1)} %copy-done.2), kind=kOutput, calls=%fused_computation.72 | convolution fusion | flops 201326592 | bytes 10747904 | tf_op jit(solution)/shard_map/qti,qtj->qij/dot_general | solution.py:128
  126.4 9.4 %reshape.154 = f32[2,2,2,2,2,8,8192]{6,5,4,3,2,1,0:T(8,128)} reshape(f32[256,32,256]{2,1,0:T(8,128)} %fusion.39) | data formatting | bytes 16777216 | tf_op jit(solution)/shard_map/reshape | solution.py:129
  136.6 4.7 %fusion.4 = f32[2,2,2,2,2,8,16]{6,5,0,1,2,3,4:T(8,128)S(1)} fusion(f32[2,2,2,2,2,8,8192]{6,5,4,3,2,1,0:T(8,128)} %reshape.154, f32[8192]{0:T(1024)S(1)} %bitcast.68, f32[16,8192]{1,0:T(8,128)S(1)} %scatter-mul.4), kind=kOutput, calls=%fused_computation.10 | convolution fusion | flops 71434240 | bytes 8962048 | tf_op jit(solution)/shard_map/dot_general | solution.py:132
  142.7 3.0 %collective-permute-done.6 = f32[16,257]{1,0:T(8,128)S(1)} collective-permute-done((f32[16,257]{1,0:T(8,128)S(1)}, f32[16,257]{1,0:T(8,128)S(1)}, u32[]{:S(2)}, u32[]{:S(2)}) %collective-permute-start.6) | collective-permute-done | bytes 16480 | tf_op jit(solution)/shard_map/ppermute | solution.py:23
  145.8 2.7 %collective-permute-done.7 = f32[16,257]{1,0:T(8,128)S(1)} collective-permute-done((f32[16,257]{1,0:T(8,128)S(1)}, f32[16,257]{1,0:T(8,128)S(1)}, u32[]{:S(2)}, u32[]{:S(2)}) %collective-permute-start.7) | collective-permute-done | bytes 16480 | tf_op jit(solution)/shard_map/ppermute | solution.py:23
  149.0 3.6 %collective-permute-done.8 = f32[16,257]{1,0:T(8,128)S(1)} collective-permute-done((f32[16,257]{1,0:T(8,128)S(1)}, f32[16,257]{1,0:T(8,128)S(1)}, u32[]{:S(2)}, u32[]{:S(2)}) %collective-permute-start.8) | collective-permute-done | bytes 16480 | tf_op jit(solution)/shard_map/ppermute | solution.py:23
  152.8 6.9 %collective-permute-start.9 = (f32[16,256]{1,0:T(8,128)S(1)}, f32[16,256]{1,0:T(8,128)S(1)}, u32[]{:S(2)}, u32[]{:S(2)}) collective-permute-start(f32[16,256]{1,0:T(8,128)S(1)} %slice_divide_fusion), channel_id=1, source_target_pairs={{0,128},{8,136},{16,144},{24,152},{32,160},{40,168},{48,176},{56,1... | collective-permute-start | bytes 49160 | tf_op jit(solution)/shard_map/ppermute | solution.py:33
  160.9 1.5 collective-permute-start.10
  162.3 2.3 %collective-permute-done.10 = f32[32,256]{1,0:T(8,128)S(1)} collective-permute-done((f32[32,256]{1,0:T(8,128)S(1)}, f32[32,256]{1,0:T(8,128)S(1)}, u32[]{:S(2)}, u32[]{:S(2)}) %collective-permute-start.10) | collective-permute-done | bytes 32800 | tf_op jit(solution)/shard_map/ppermute | solution.py:33
  165.5 2.3 %collective-permute-done.11 = f32[64,256]{1,0:T(8,128)S(1)} collective-permute-done((f32[64,256]{1,0:T(8,128)S(1)}, f32[64,256]{1,0:T(8,128)S(1)}, u32[]{:S(2)}, u32[]{:S(2)}) %collective-permute-start.11) | collective-permute-done | bytes 65568 | tf_op jit(solution)/shard_map/ppermute | solution.py:33
  167.9 3.0 %collective-permute-start.12 = (f32[128,256]{1,0:T(8,128)S(1)}, f32[128,256]{1,0:T(8,128)S(1)}, u32[]{:S(2)}, u32[]{:S(2)}) collective-permute-start(f32[128,256]{1,0:T(8,128)S(1)} %maximum_select_fusion.8), channel_id=1, source_target_pairs={{0,16},{8,24},{16,0},{24,8},{32,48},{40,56},{48,32},{56,40},{64,80... | collective-permute-start | bytes 393224 | tf_op jit(solution)/shard_map/ppermute | solution.py:33
  170.9 2.7 %collective-permute-done.12 = f32[128,256]{1,0:T(8,128)S(1)} collective-permute-done((f32[128,256]{1,0:T(8,128)S(1)}, f32[128,256]{1,0:T(8,128)S(1)}, u32[]{:S(2)}, u32[]{:S(2)}) %collective-permute-start.12) | collective-permute-done | bytes 131104 | tf_op jit(solution)/shard_map/ppermute | solution.py:33
  173.5 5.8 %collective-permute-start.13 = (f32[256,256]{1,0:T(8,128)S(1)}, f32[256,256]{1,0:T(8,128)S(1)}, u32[]{:S(2)}, u32[]{:S(2)}) collective-permute-start(f32[256,256]{1,0:T(8,128)S(1)} %maximum_select_fusion.6), channel_id=1, source_target_pairs={{0,8},{8,0},{16,24},{24,16},{32,40},{40,32},{48,56},{56,48},{64,72... | collective-permute-start | bytes 786440 | tf_op jit(solution)/shard_map/ppermute | solution.py:33
  (96 shorter events, 14.8 us)
Async XLA Ops:
  0.0 5.5 %copy-start = (bf16[2048,512]{1,0:T(8,128)(2,1)S(1)}, bf16[2048,512]{1,0:T(8,128)(2,1)}, u32[]{:S(2)}) copy-start(bf16[2048,512]{1,0:T(8,128)(2,1)} %param.17) | copy-start | bytes 6291460
  0.0 5.5 %copy-start.9 = (bf16[512,256]{1,0:T(8,128)(2,1)S(1)}, bf16[512,256]{1,0:T(8,128)(2,1)}, u32[]{:S(2)}) copy-start(bf16[512,256]{1,0:T(8,128)(2,1)} %param.19) | copy-start | bytes 786436
  9.1 7.6 %copy-start.10 = (bf16[8,8,256]{2,1,0:T(8,128)(2,1)S(1)}, bf16[8,8,256]{2,1,0:T(8,128)(2,1)}, u32[]{:S(2)}) copy-start(bf16[8,8,256]{2,1,0:T(8,128)(2,1)} %param.23) | copy-start | bytes 98308
  9.1 7.6 %copy-start.11 = (bf16[8,8,256]{2,1,0:T(8,128)(2,1)S(1)}, bf16[8,8,256]{2,1,0:T(8,128)(2,1)}, u32[]{:S(2)}) copy-start(bf16[8,8,256]{2,1,0:T(8,128)(2,1)} %param.24) | copy-start | bytes 98308
  9.1 57.8 %all-to-all-start = ((f32[8,256,512]{1,2,0:T(8,128)}), f32[8,256,512]{1,2,0:T(8,128)}, u32[]{:S(2)}, u32[]{:S(2)}) async-start(f32[8,256,512]{1,2,0:T(8,128)} %bitcast.61), calls=%async_computation | async-start | bytes 8388608 | tf_op jit(solution)/shard_map/all_to_all | solution.py:83
  16.8 8.7 %collective-permute-start = (bf16[8,8,512]{2,1,0:T(8,128)(2,1)S(1)}, bf16[8,8,512]{2,1,0:T(8,128)(2,1)S(1)}, u32[]{:S(2)}, u32[]{:S(2)}) collective-permute-start(bf16[8,8,512]{2,1,0:T(8,128)(2,1)S(1)} %constant_dynamic-update-slice_fusion), channel_id=1, source_target_pairs={{0,128},{8,136},{16,144},{24,152},{32,160},{40,168},{48,176},{56,1... | collective-permute-start | bytes 196616 | tf_op jit(solution)/shard_map/ppermute | solution.py:33
  25.5 7.2 %collective-permute-start.1 = (bf16[16,8,512]{2,1,0:T(8,128)(2,1)S(1)}, bf16[16,8,512]{2,1,0:T(8,128)(2,1)S(1)}, u32[]{:S(2)}, u32[]{:S(2)}) collective-permute-start(bf16[16,8,512]{2,1,0:T(8,128)(2,1)S(1)} %maximum_select_fusion.7), channel_id=1, source_target_pairs={{0,64},{8,72},{16,80},{24,88},{32,96},{40,104},{48,112},{56,120},{... | collective-permute-start | bytes 393224 | tf_op jit(solution)/shard_map/ppermute | solution.py:33
  32.8 5.7 %collective-permute-start.2 = (bf16[32,8,512]{2,1,0:T(8,128)(2,1)S(1)}, bf16[32,8,512]{2,1,0:T(8,128)(2,1)S(1)}, u32[]{:S(2)}, u32[]{:S(2)}) collective-permute-start(bf16[32,8,512]{2,1,0:T(8,128)(2,1)S(1)} %maximum_select_fusion.5), channel_id=1, source_target_pairs={{0,32},{8,40},{16,48},{24,56},{32,0},{40,8},{48,16},{56,24},{64,96... | collective-permute-start | bytes 786440 | tf_op jit(solution)/shard_map/ppermute | solution.py:33
  38.5 30.9 %copy-start.5 = (bf16[64,8,512]{2,1,0:T(8,128)(2,1)}, bf16[64,8,512]{2,1,0:T(8,128)(2,1)S(1)}, u32[]{:S(2)}) copy-start(bf16[64,8,512]{2,1,0:T(8,128)(2,1)S(1)} %maximum_select_fusion.2) | copy-start | bytes 1572868
  38.6 30.9 %copy-start.7 = (bf16[256,256]{1,0:T(8,128)(2,1)S(1)}, bf16[256,256]{1,0:T(8,128)(2,1)}, u32[]{:S(2)}) copy-start(bf16[256,256]{1,0:T(8,128)(2,1)} %param.20) | copy-start | bytes 393220
  38.6 31.2 %copy-start.8 = (bf16[256,256]{1,0:T(8,128)(2,1)S(1)}, bf16[256,256]{1,0:T(8,128)(2,1)}, u32[]{:S(2)}) copy-start(bf16[256,256]{1,0:T(8,128)(2,1)} %param.21) | copy-start | bytes 393220
  38.6 37.8 %collective-permute-start.3 = (bf16[64,8,512]{2,1,0:T(8,128)(2,1)S(1)}, bf16[64,8,512]{2,1,0:T(8,128)(2,1)}, u32[]{:S(2)}, u32[]{:S(2)}) collective-permute-start(bf16[64,8,512]{2,1,0:T(8,128)(2,1)S(1)} %maximum_select_fusion.2), channel_id=1, source_target_pairs={{0,16},{8,24},{16,0},{24,8},{32,48},{40,56},{48,32},{56,40},{64,80... | collective-permute-start | bytes 1572872 | tf_op jit(solution)/shard_map/ppermute | solution.py:33
  71.8 4.6 %copy-start.6 = (bf16[64,8,512]{2,1,0:T(8,128)(2,1)S(1)}, bf16[64,8,512]{2,1,0:T(8,128)(2,1)}, u32[]{:S(2)}) copy-start(bf16[64,8,512]{2,1,0:T(8,128)(2,1)} %copy-done.5) | copy-start | bytes 1572868
  71.8 9.4 %copy-start.14 = (s32[32]{0:T(128)S(1)}, s32[32]{0:T(128)}, u32[]{:S(2)}) copy-start(s32[32]{0:T(128)} %param.26) | copy-start | bytes 388
  71.8 10.7 %copy-start.15 = (s32[1,16]{1,0:T(1,128)S(1)}, s32[1,16]{1,0:T(1,128)}, u32[]{:S(2)}) copy-start(s32[1,16]{1,0:T(1,128)} %param.25) | copy-start | bytes 196
  71.8 11.6 %copy-start.12 = (f32[32,256]{1,0:T(8,128)S(1)}, f32[32,256]{1,0:T(8,128)}, u32[]{:S(2)}) copy-start(f32[32,256]{1,0:T(8,128)} %param.22) | copy-start | bytes 98308
  71.9 32.4 %all-to-all-start.1 = ((f32[8,256,288]{1,2,0:T(8,128)}), f32[8,256,288]{1,2,0:T(8,128)}, u32[]{:S(2)}, u32[]{:S(2)}) async-start(f32[8,256,288]{1,2,0:T(8,128)} %pad_maximum_fusion.1), calls=%async_computation.1 | async-start | bytes 4718592 | tf_op jit(solution)/shard_map/all_to_all | solution.py:93
  77.8 5.9 %collective-permute-start.4 = (bf16[128,8,512]{2,1,0:T(8,128)(2,1)S(1)}, bf16[128,8,512]{2,1,0:T(8,128)(2,1)}, u32[]{:S(2)}, u32[]{:S(2)}) collective-permute-start(bf16[128,8,512]{2,1,0:T(8,128)(2,1)S(1)} %maximum_select_fusion.1), channel_id=1, source_target_pairs={{0,8},{8,0},{16,24},{24,16},{32,40},{40,32},{48,56},{56,48},{64,72... | collective-permute-start | bytes 3145736 | tf_op jit(solution)/shard_map/ppermute | solution.py:33
  106.7 10.8 %copy-start.2 = (f32[256,8,256]{2,1,0:T(8,128)S(1)}, f32[256,8,256]{2,1,0:T(8,128)}, u32[]{:S(2)}) copy-start(f32[256,8,256]{2,1,0:T(8,128)} %fusion.5) | copy-start | bytes 6291460
  110.2 0.8 copy-start.3
  111.0 25.0 %collective-permute-start.5 = (f32[8192]{0:T(1024)S(1)}, f32[8192]{0:T(1024)S(1)}, u32[]{:S(2)}, u32[]{:S(2)}) collective-permute-start(f32[8192]{0:T(1024)S(1)} %bitcast.73), channel_id=1, source_target_pairs={{0,8},{8,16},{16,24},{24,32},{32,40},{40,48},{48,56},{56,64},{64,7... | collective-permute-start | bytes 98312 | tf_op jit(solution)/shard_map/ppermute | solution.py:16
  126.4 9.4 %copy-start.4 = (f32[512,256]{1,0:T(8,128)S(1)}, f32[512,256]{1,0:T(8,128)}, u32[]{:S(2)}) copy-start(f32[512,256]{1,0:T(8,128)} %copy-done.3) | copy-start | bytes 1572868
  136.6 42.8 %copy-start.13 = (s32[512,1]{0,1:T(1,128)S(1)}, s32[512,1]{0,1:T(1,128)}, u32[]{:S(2)}) copy-start(s32[512,1]{0,1:T(1,128)} %param.27) | copy-start | bytes 6148
  136.6 44.9 %copy-start.1 = (bf16[2048,512]{1,0:T(8,128)(2,1)S(1)}, bf16[2048,512]{1,0:T(8,128)(2,1)}, u32[]{:S(2)}) copy-start(bf16[2048,512]{1,0:T(8,128)(2,1)} %param.17) | copy-start | bytes 6291460
  141.5 4.2 %collective-permute-start.6 = (f32[16,257]{1,0:T(8,128)S(1)}, f32[16,257]{1,0:T(8,128)S(1)}, u32[]{:S(2)}, u32[]{:S(2)}) collective-permute-start(f32[16,257]{1,0:T(8,128)S(1)} %pad_maximum_fusion.2), channel_id=1, source_target_pairs={{0,1},{1,0},{2,3},{3,2},{4,5},{5,4},{6,7},{7,6},{8,9},{9,8},{10,11... | collective-permute-start | bytes 49352 | tf_op jit(solution)/shard_map/ppermute | solution.py:23
  145.7 2.7 %collective-permute-start.7 = (f32[16,257]{1,0:T(8,128)S(1)}, f32[16,257]{1,0:T(8,128)S(1)}, u32[]{:S(2)}, u32[]{:S(2)}) collective-permute-start(f32[16,257]{1,0:T(8,128)S(1)} %fusion.37), channel_id=1, source_target_pairs={{0,2},{1,3},{2,0},{3,1},{4,6},{5,7},{6,4},{7,5},{8,10},{9,11},{10,... | collective-permute-start | bytes 49352 | tf_op jit(solution)/shard_map/ppermute | solution.py:23
  148.4 4.2 %collective-permute-start.8 = (f32[16,257]{1,0:T(8,128)S(1)}, f32[16,257]{1,0:T(8,128)S(1)}, u32[]{:S(2)}, u32[]{:S(2)}) collective-permute-start(f32[16,257]{1,0:T(8,128)S(1)} %add.76), channel_id=1, source_target_pairs={{0,4},{1,5},{2,6},{3,7},{4,0},{5,1},{6,2},{7,3},{8,12},{9,13},{10,... | collective-permute-start | bytes 49352 | tf_op jit(solution)/shard_map/ppermute | solution.py:23
  152.8 8.1 %collective-permute-start.9 = (f32[16,256]{1,0:T(8,128)S(1)}, f32[16,256]{1,0:T(8,128)S(1)}, u32[]{:S(2)}, u32[]{:S(2)}) collective-permute-start(f32[16,256]{1,0:T(8,128)S(1)} %slice_divide_fusion), channel_id=1, source_target_pairs={{0,128},{8,136},{16,144},{24,152},{32,160},{40,168},{48,176},{56,1... | collective-permute-start | bytes 49160 | tf_op jit(solution)/shard_map/ppermute | solution.py:33
  160.9 3.7 %collective-permute-start.10 = (f32[32,256]{1,0:T(8,128)S(1)}, f32[32,256]{1,0:T(8,128)S(1)}, u32[]{:S(2)}, u32[]{:S(2)}) collective-permute-start(f32[32,256]{1,0:T(8,128)S(1)} %maximum_select_fusion.10), channel_id=1, source_target_pairs={{0,64},{8,72},{16,80},{24,88},{32,96},{40,104},{48,112},{56,120},{... | collective-permute-start | bytes 98312 | tf_op jit(solution)/shard_map/ppermute | solution.py:33
  164.6 3.2 %collective-permute-start.11 = (f32[64,256]{1,0:T(8,128)S(1)}, f32[64,256]{1,0:T(8,128)S(1)}, u32[]{:S(2)}, u32[]{:S(2)}) collective-permute-start(f32[64,256]{1,0:T(8,128)S(1)} %maximum_select_fusion.9), channel_id=1, source_target_pairs={{0,32},{8,40},{16,48},{24,56},{32,0},{40,8},{48,16},{56,24},{64,96... | collective-permute-start | bytes 196616 | tf_op jit(solution)/shard_map/ppermute | solution.py:33
  167.9 5.7 %collective-permute-start.12 = (f32[128,256]{1,0:T(8,128)S(1)}, f32[128,256]{1,0:T(8,128)S(1)}, u32[]{:S(2)}, u32[]{:S(2)}) collective-permute-start(f32[128,256]{1,0:T(8,128)S(1)} %maximum_select_fusion.8), channel_id=1, source_target_pairs={{0,16},{8,24},{16,0},{24,8},{32,48},{40,56},{48,32},{56,40},{64,80... | collective-permute-start | bytes 393224 | tf_op jit(solution)/shard_map/ppermute | solution.py:33
  173.5 7.0 %collective-permute-start.13 = (f32[256,256]{1,0:T(8,128)S(1)}, f32[256,256]{1,0:T(8,128)S(1)}, u32[]{:S(2)}, u32[]{:S(2)}) collective-permute-start(f32[256,256]{1,0:T(8,128)S(1)} %maximum_select_fusion.6), channel_id=1, source_target_pairs={{0,8},{8,0},{16,24},{24,16},{32,40},{40,32},{48,56},{56,48},{64,72... | collective-permute-start | bytes 786440 | tf_op jit(solution)/shard_map/ppermute | solution.py:33

commit v6 on v4

--- a/solution.py
+++ b/solution.py
@@ -73,15 +73,27 @@
     data_count = lax.axis_size("dp")
     highest = lax.Precision.HIGHEST
     chunk = tokens_here // factor_count
+    scale_block = 1.0 / (eigen_values + DAMPING)
+    queries = butterfly_gather(jnp.concatenate([query_in, query_out], axis=2), "dp")
 
 
+    basis_in_wide = basis_in.astype(jnp.float32)
+    basis_out_wide = basis_out.astype(jnp.float32)
     in_part = jnp.dot(activations, proj_in, preferred_element_type=jnp.float32)
     out_part = jnp.dot(out_grads, proj_out, preferred_element_type=jnp.float32)
     stacked_parts = jnp.concatenate([in_part, out_part], axis=1)
     gathered_parts = lax.all_to_all(stacked_parts, "factor", 0, 0, tiled=True)
+    basis_cut = lax.dynamic_slice_in_dim(basis_out_wide, factor_index * rank_slice, rank_slice, 1)
+    q_in = jnp.einsum(
+        "qtk,kl->qtl", queries[:, :, :rank_in].astype(jnp.float32), basis_in_wide, precision=highest
+    )
+    q_out = jnp.einsum(
+        "qtk,kl->qtl", queries[:, :, rank_in:].astype(jnp.float32), basis_cut, precision=highest
+    )
+    outer = jnp.einsum("qti,qtj->qij", q_out, q_in, precision=highest)
+    query_grad = (outer * scale_block[None]).astype(jnp.bfloat16)
+    gathered_parts, query_grad = lax.optimization_barrier((gathered_parts, query_grad))
     chunk_sums = jnp.sum(gathered_parts.reshape(factor_count, chunk, rank_in + rank_out), axis=0)
-    basis_in_wide = basis_in.astype(jnp.float32)
-    basis_out_wide = basis_out.astype(jnp.float32)
     rot_in_chunk = jnp.dot(chunk_sums[:, :rank_in], basis_in_wide, precision=highest)
     rot_out_chunk = jnp.dot(chunk_sums[:, rank_in:], basis_out_wide, precision=highest)
     out_blocks = rot_out_chunk.reshape(chunk, factor_count, rank_slice).transpose(1, 0, 2)
@@ -103,7 +115,7 @@
         tokens_here, pieces * rank_slice
     )
     grad_rows = lax.dot_general(stacked, rot_in, (((0,), (0,)), ((), ())), precision=highest)
-    grad_rows = grad_rows.reshape(pieces, rank_slice * rank_in)
+    grad_rows = grad_rows.reshape(pieces, rank_slice, rank_in)
     preceding = from_behind(grad_rows[pieces - 1], "dp", 1)
     joined_next = jnp.where(data_index < data_count - 1, continues[data_index], 0).astype(
         jnp.float32
@@ -113,20 +125,11 @@
     )
     grad_rows = grad_rows.at[0].add(joined_prev * preceding)
     grad_rows = grad_rows.at[pieces - 1].multiply(1.0 - joined_next)
-    scale = (1.0 / (eigen_values + DAMPING)).reshape(-1)
-    self_part = jnp.sum(grad_rows * grad_rows * scale[None, :], axis=1)
+    self_part = jnp.sum(grad_rows * grad_rows * scale_block[None], axis=(1, 2))
     grad_low = grad_rows.astype(jnp.bfloat16)
 
-    basis_cut = lax.dynamic_slice_in_dim(basis_out_wide, factor_index * rank_slice, rank_slice, 1)
-    q_out = jnp.einsum("qtk,kl->qtl", query_out.astype(jnp.float32), basis_cut, precision=highest)
-    q_in = jnp.einsum("qtk,kl->qtl", query_in.astype(jnp.float32), basis_in_wide, precision=highest)
-    outer = jnp.einsum("qti,qtj->qij", q_out, q_in, precision=highest)
-    query_grad = butterfly_gather(
-        (outer.reshape(query_in.shape[0], rank_slice * rank_in) * scale[None, :]).astype(jnp.bfloat16),
-        "dp",
-    )
     part = lax.dot_general(
-        grad_low, query_grad, (((1,), (1,)), ((), ())), preferred_element_type=jnp.float32
+        grad_low, query_grad, (((1, 2), (1, 2)), ((), ())), preferred_element_type=jnp.float32
     )
     part = bit_reversed(part.T, data_count).T
 

time: 183 us -> 209 us (1.14)
  waiting for transfers between devices: 82.1 us -> 112 us
  starting transfers between devices: 60.3 us -> 42.5 us
  matrix products: 17 us -> 28.2 us
  local copies, waits for them, and re-layouts: 9.82 us -> 14 us
    ppermute x10, waiting for transfers between devices: 27.6 us -> 72.2 us  [butterfly_gather(): other = lax.ppermute(block, axis, [(i, i ^ step) for i in range(size)])]
    all_to_all x1, waiting for transfers between devices: 34.3 us -> 0.01 us  [per_device(): gathered_parts = lax.all_to_all(stacked_parts, 'factor', 0, 0, tiled=True)]
    all_to_all x1, waiting for transfers between devices: 14.9 us -> 30.5 us  [per_device(): received = lax.all_to_all(sending, 'factor', 0, 0, tiled=True)]
    ppermute x10, starting transfers between devices: 33.8 us -> 22.7 us  [butterfly_gather(): other = lax.ppermute(block, axis, [(i, i ^ step) for i in range(size)])]
    dot_general x1, matrix products: 0.46 us -> 8.68 us  [per_device(): outer = jnp.einsum('qti,qtj->qij', q_out, q_in, precision=highest)]
    all_to_all x1 -> x2, local copies, waits for them, and re-layouts: 2.33 us -> 7.69 us  [per_device(): gathered_parts = lax.all_to_all(stacked_parts, 'factor', 0, 0, tiled=True)]
    ppermute x3, starting transfers between devices: 7.24 us -> 2.12 us  [butterfly_sum(): lax.ppermute(block, axis, [(i, i ^ step) for i in range(size)])]
    ppermute x3, waiting for transfers between devices: 5.25 us -> 9.53 us  [butterfly_sum(): lax.ppermute(block, axis, [(i, i ^ step) for i in range(size)])]
  transfers between devices with their start and end apart: 16 -> 16, of which waited for: 14 -> 13; matrix products, arithmetic and copies ran while one was open for 11% -> 12% of each run, Pallas kernels for 0% -> 0%
where the time goes in v6:
time: 209 us
  waiting for transfers between devices  112 us (54%)
  starting transfers between devices  42.5 us (20%)
  matrix products  28.2 us (13%)
  local copies, waits for them, and re-layouts  14 us (7%)
  other arithmetic  9.89 us (5%)
    ppermute x10, waiting for transfers between devices, butterfly_gather(): other = lax.ppermute(block, axis, [(i, i ^ step) for i in range(size)])  72.2 us
    all_to_all x1, waiting for transfers between devices, per_device(): received = lax.all_to_all(sending, 'factor', 0, 0, tiled=True)  30.5 us
    ppermute x10, starting transfers between devices, butterfly_gather(): other = lax.ppermute(block, axis, [(i, i ^ step) for i in range(size)])  22.7 us
    ppermute x3, waiting for transfers between devices, butterfly_sum(): lax.ppermute(block, axis, [(i, i ^ step) for i in range(size)])  9.53 us
    dot_general x1, matrix products, per_device(): outer = jnp.einsum('qti,qtj->qij', q_out, q_in, precision=highest)  8.68 us
    all_to_all x1, starting transfers between devices, per_device(): received = lax.all_to_all(sending, 'factor', 0, 0, tiled=True)  7.77 us
    all_to_all x2, local copies, waits for them, and re-layouts, per_device(): gathered_parts = lax.all_to_all(stacked_parts, 'factor', 0, 0, tiled=True)  7.69 us
    all_to_all x1, starting transfers between devices, per_device(): gathered_parts = lax.all_to_all(stacked_parts, 'factor', 0, 0, tiled=True)  6.65 us
  transfers between devices with their start and end apart: 16, of which 13 were waited for; matrix products, arithmetic and copies ran while one was open for 12% of the time, Pallas kernels for 0%

profile of v6, /device:TPU:1, one launch (start us, length us, event | category | flops | bytes accessed | tf_op | source)
XLA Modules:
  0.0 208.6 jit_solution(10591920656287168782)
XLA Ops:
  1.7 7.7 %collective-permute-start = (bf16[8,8,512]{2,1,0:T(8,128)(2,1)S(1)}, bf16[8,8,512]{2,1,0:T(8,128)(2,1)S(1)}, u32[]{:S(2)}, u32[]{:S(2)}) collective-permute-start(bf16[8,8,512]{2,1,0:T(8,128)(2,1)S(1)} %constant_dynamic-update-slice_fusion), channel_id=1, source_target_pairs={{0,128},{8,136},{16,144},{24,152},{32,160},{40,168},{48,176},{56,1... | collective-permute-start | bytes 196616 | tf_op jit(solution)/shard_map/ppermute | solution.py:33
  9.4 1.7 fusion.39
  11.1 5.2 %fusion.38 = f32[2048,256]{0,1:T(8,128)S(1)} fusion(bf16[2048,1792]{1,0:T(8,128)(2,1)} %param.16, bf16[1792,256]{1,0:T(8,128)(2,1)S(1)} %copy-done.8), kind=kOutput, calls=%fused_computation.69 | convolution fusion | flops 1879048192 | bytes 10354688 | tf_op jit(solution)/shard_map/dot_general | solution.py:82
  16.6 2.3 %copy.96 = f32[64,8,8,256]{3,2,0,1:T(8,128)} copy(f32[64,8,8,256]{3,2,1,0:T(8,128)S(1)} %bitcast.55) | data formatting | bytes 8388608 | tf_op jit(solution)/shard_map/all_to_all | solution.py:85
  19.0 6.7 %all-to-all-start = ((f32[8,256,512]{1,2,0:T(8,128)}), f32[8,256,512]{1,2,0:T(8,128)}, u32[]{:S(2)}, u32[]{:S(2)}) async-start(f32[8,256,512]{1,2,0:T(8,128)} %bitcast.54), calls=%async_computation | async-start | bytes 8388608 | tf_op jit(solution)/shard_map/all_to_all | solution.py:85
  25.7 1.3 collective-permute-start.1
  27.0 7.6 %collective-permute-done.1 = bf16[16,8,512]{2,1,0:T(8,128)(2,1)S(1)} collective-permute-done((bf16[16,8,512]{2,1,0:T(8,128)(2,1)S(1)}, bf16[16,8,512]{2,1,0:T(8,128)(2,1)S(1)}, u32[]{:S(2)}, u32[]{:S(2)}) %collective-permute-start.1) | collective-permute-done | bytes 131104 | tf_op jit(solution)/shard_map/ppermute | solution.py:33
  34.7 7.1 %collective-permute-done.2 = bf16[32,8,512]{2,1,0:T(8,128)(2,1)S(1)} collective-permute-done((bf16[32,8,512]{2,1,0:T(8,128)(2,1)S(1)}, bf16[32,8,512]{2,1,0:T(8,128)(2,1)S(1)}, u32[]{:S(2)}, u32[]{:S(2)}) %collective-permute-start.2) | collective-permute-done | bytes 262176 | tf_op jit(solution)/shard_map/ppermute | solution.py:33
  42.7 39.8 %collective-permute-done.3 = bf16[64,8,512]{2,1,0:T(8,128)(2,1)} collective-permute-done((bf16[64,8,512]{2,1,0:T(8,128)(2,1)S(1)}, bf16[64,8,512]{2,1,0:T(8,128)(2,1)}, u32[]{:S(2)}, u32[]{:S(2)}) %collective-permute-start.3) | collective-permute-done | bytes 524320 | tf_op jit(solution)/shard_map/ppermute | solution.py:33
  82.4 1.7 maximum_select_fusion.1
  84.2 2.1 collective-permute-start.4
  86.3 2.4 %collective-permute-done.4 = bf16[128,8,512]{2,1,0:T(8,128)(2,1)} collective-permute-done((bf16[128,8,512]{2,1,0:T(8,128)(2,1)S(1)}, bf16[128,8,512]{2,1,0:T(8,128)(2,1)}, u32[]{:S(2)}, u32[]{:S(2)}) %collective-permute-start.4) | collective-permute-done | bytes 1048608 | tf_op jit(solution)/shard_map/ppermute | solution.py:33
  88.7 1.9 maximum_select_fusion
  91.5 8.7 %multiply_convert_fusion = bf16[256,32,256]{2,1,0:T(8,128)(2,1)} fusion(f32[32,256]{1,0:T(8,128)S(1)} %add_divide_fusion, f32[256,8,32]{2,1,0:T(8,128)S(1)} %fusion.6, f32[256,8,256]{2,1,0:T(8,128)S(1)} %fusion.4), kind=kOutput, calls=%fused_computation | convolution fusion | flops 205520896 | bytes 6586368 | tf_op jit(solution)/shard_map/qti,qtj->qij/dot_general | solution.py:93
  100.2 5.4 %copy.70 = f32[8,256,512]{2,1,0:T(8,128)} copy(f32[8,256,512]{1,2,0:T(8,128)} %all-to-all-done) | data formatting | bytes 8388608 | tf_op jit(solution)/shard_map/all_to_all | solution.py:85
  105.6 2.7 %reduce_sum.28 = f32[256,512]{1,0:T(8,128)S(1)} reduce(f32[8,256,512]{2,1,0:T(8,128)} %copy.70, f32[]{:T(128)} %constant.180.clone.1), dimensions={0}, to_apply=%region_2.3 | reduce | flops 917504 | bytes 4718596 | tf_op jit(solution)/shard_map/reduce_sum | solution.py:96
  109.1 1.6 pad_maximum_fusion.1
  110.8 7.8 %all-to-all-start.1 = ((f32[8,256,288]{1,2,0:T(8,128)}), f32[8,256,288]{1,2,0:T(8,128)}, u32[]{:S(2)}, u32[]{:S(2)}) async-start(f32[8,256,288]{1,2,0:T(8,128)} %pad_maximum_fusion.1), calls=%async_computation.1 | async-start | bytes 4718592 | tf_op jit(solution)/shard_map/all_to_all | solution.py:103
  118.9 30.5 %all-to-all-done.1 = f32[8,256,288]{1,2,0:T(8,128)} async-done(((f32[8,256,288]{1,2,0:T(8,128)}), f32[8,256,288]{1,2,0:T(8,128)}, u32[]{:S(2)}, u32[]{:S(2)}) %all-to-all-start.1) | async-done | bytes 2359328 | tf_op jit(solution)/shard_map/all_to_all | solution.py:103
  149.3 1.9 copy.91
  151.8 3.5 %fusion.2 = f32[512,256]{1,0:T(8,128)S(1)} fusion(f32[2048,512]{0,1:T(8,128)S(1)} %bitcast.56, f32[2048,288]{0,1:T(8,128)S(1)} %bitcast.58), kind=kOutput, calls=%fused_computation.6 | convolution fusion | flops 3221225472 | bytes 6815744 | tf_op jit(solution)/shard_map/dot_general | solution.py:117
  155.3 3.3 %collective-permute-start.5 = (f32[32,256]{1,0:T(8,128)S(1)}, f32[32,256]{1,0:T(8,128)S(1)}, u32[]{:S(2)}, u32[]{:S(2)}) collective-permute-start(f32[32,256]{1,0:T(8,128)S(1)} %slice.91), channel_id=1, source_target_pairs={{0,8},{8,16},{16,24},{24,32},{32,40},{40,48},{48,56},{56,64},{64,7... | collective-permute-start | bytes 98312 | tf_op jit(solution)/shard_map/ppermute | solution.py:16
  161.8 6.6 %fusion = f32[256,16,1]{1,0,2:T(8,128)S(1)} fusion(bf16[256,32,256]{2,1,0:T(8,128)(2,1)} %multiply_convert_fusion, f32[16,32,256]{2,0,1:T(8,128)S(1)} %scatter-mul.4), kind=kOutput, calls=%fused_computation.3 | convolution fusion | flops 67239936 | bytes 4734976 | tf_op jit(solution)/shard_map/dot_general | solution.py:131
  169.7 3.6 %collective-permute-done.6 = f32[16,257]{1,0:T(8,128)S(1)} collective-permute-done((f32[16,257]{1,0:T(8,128)S(1)}, f32[16,257]{1,0:T(8,128)S(1)}, u32[]{:S(2)}, u32[]{:S(2)}) %collective-permute-start.6) | collective-permute-done | bytes 16480 | tf_op jit(solution)/shard_map/ppermute | solution.py:23
  173.3 2.7 %collective-permute-done.7 = f32[16,257]{1,0:T(8,128)S(1)} collective-permute-done((f32[16,257]{1,0:T(8,128)S(1)}, f32[16,257]{1,0:T(8,128)S(1)}, u32[]{:S(2)}, u32[]{:S(2)}) %collective-permute-start.7) | collective-permute-done | bytes 16480 | tf_op jit(solution)/shard_map/ppermute | solution.py:23
  176.9 3.3 %collective-permute-done.8 = f32[16,257]{1,0:T(8,128)S(1)} collective-permute-done((f32[16,257]{1,0:T(8,128)S(1)}, f32[16,257]{1,0:T(8,128)S(1)}, u32[]{:S(2)}, u32[]{:S(2)}) %collective-permute-start.8) | collective-permute-done | bytes 16480 | tf_op jit(solution)/shard_map/ppermute | solution.py:23
  180.4 6.5 %collective-permute-done.9 = f32[16,256]{1,0:T(8,128)S(1)} collective-permute-done((f32[16,256]{1,0:T(8,128)S(1)}, f32[16,256]{1,0:T(8,128)S(1)}, u32[]{:S(2)}, u32[]{:S(2)}) %collective-permute-start.9) | collective-permute-done | bytes 16416 | tf_op jit(solution)/shard_map/ppermute | solution.py:33
  187.8 3.1 %collective-permute-done.10 = f32[32,256]{1,0:T(8,128)S(1)} collective-permute-done((f32[32,256]{1,0:T(8,128)S(1)}, f32[32,256]{1,0:T(8,128)S(1)}, u32[]{:S(2)}, u32[]{:S(2)}) %collective-permute-start.10) | collective-permute-done | bytes 32800 | tf_op jit(solution)/shard_map/ppermute | solution.py:33
  191.2 2.9 %collective-permute-done.11 = f32[64,256]{1,0:T(8,128)S(1)} collective-permute-done((f32[64,256]{1,0:T(8,128)S(1)}, f32[64,256]{1,0:T(8,128)S(1)}, u32[]{:S(2)}, u32[]{:S(2)}) %collective-permute-start.11) | collective-permute-done | bytes 65568 | tf_op jit(solution)/shard_map/ppermute | solution.py:33
  194.2 1.7 collective-permute-start.12
  195.9 2.4 %collective-permute-done.12 = f32[128,256]{1,0:T(8,128)S(1)} collective-permute-done((f32[128,256]{1,0:T(8,128)S(1)}, f32[128,256]{1,0:T(8,128)S(1)}, u32[]{:S(2)}, u32[]{:S(2)}) %collective-permute-start.12) | collective-permute-done | bytes 131104 | tf_op jit(solution)/shard_map/ppermute | solution.py:33
  198.3 8.2 %collective-permute-start.13 = (f32[256,256]{1,0:T(8,128)S(1)}, f32[256,256]{1,0:T(8,128)S(1)}, u32[]{:S(2)}, u32[]{:S(2)}) collective-permute-start(f32[256,256]{1,0:T(8,128)S(1)} %maximum_select_fusion.6), channel_id=1, source_target_pairs={{0,8},{8,0},{16,24},{24,16},{32,40},{40,32},{48,56},{56,48},{64,72... | collective-permute-start | bytes 786440 | tf_op jit(solution)/shard_map/ppermute | solution.py:33
  (80 shorter events, 13.2 us)
Async XLA Ops:
  0.0 9.4 %copy-start = (bf16[2048,512]{1,0:T(8,128)(2,1)S(1)}, bf16[2048,512]{1,0:T(8,128)(2,1)}, u32[]{:S(2)}) copy-start(bf16[2048,512]{1,0:T(8,128)(2,1)} %param.17) | copy-start | bytes 6291460
  0.0 11.1 %copy-start.8 = (bf16[1792,256]{1,0:T(8,128)(2,1)S(1)}, bf16[1792,256]{1,0:T(8,128)(2,1)}, u32[]{:S(2)}) copy-start(bf16[1792,256]{1,0:T(8,128)(2,1)} %param.18) | copy-start | bytes 2752516
  1.7 24.0 %collective-permute-start = (bf16[8,8,512]{2,1,0:T(8,128)(2,1)S(1)}, bf16[8,8,512]{2,1,0:T(8,128)(2,1)S(1)}, u32[]{:S(2)}, u32[]{:S(2)}) collective-permute-start(bf16[8,8,512]{2,1,0:T(8,128)(2,1)S(1)} %constant_dynamic-update-slice_fusion), channel_id=1, source_target_pairs={{0,128},{8,136},{16,144},{24,152},{32,160},{40,168},{48,176},{56,1... | collective-permute-start | bytes 196616 | tf_op jit(solution)/shard_map/ppermute | solution.py:33
  19.0 81.3 %all-to-all-start = ((f32[8,256,512]{1,2,0:T(8,128)}), f32[8,256,512]{1,2,0:T(8,128)}, u32[]{:S(2)}, u32[]{:S(2)}) async-start(f32[8,256,512]{1,2,0:T(8,128)} %bitcast.54), calls=%async_computation | async-start | bytes 8388608 | tf_op jit(solution)/shard_map/all_to_all | solution.py:85
  25.6 60.6 %copy-start.4 = (f32[32,256]{1,0:T(8,128)S(1)}, f32[32,256]{1,0:T(8,128)}, u32[]{:S(2)}) copy-start(f32[32,256]{1,0:T(8,128)} %param.22) | copy-start | bytes 98308
  25.7 8.9 %collective-permute-start.1 = (bf16[16,8,512]{2,1,0:T(8,128)(2,1)S(1)}, bf16[16,8,512]{2,1,0:T(8,128)(2,1)S(1)}, u32[]{:S(2)}, u32[]{:S(2)}) collective-permute-start(bf16[16,8,512]{2,1,0:T(8,128)(2,1)S(1)} %maximum_select_fusion.7), channel_id=1, source_target_pairs={{0,64},{8,72},{16,80},{24,88},{32,96},{40,104},{48,112},{56,120},{... | collective-permute-start | bytes 393224 | tf_op jit(solution)/shard_map/ppermute | solution.py:33
  34.6 7.2 %collective-permute-start.2 = (bf16[32,8,512]{2,1,0:T(8,128)(2,1)S(1)}, bf16[32,8,512]{2,1,0:T(8,128)(2,1)S(1)}, u32[]{:S(2)}, u32[]{:S(2)}) collective-permute-start(bf16[32,8,512]{2,1,0:T(8,128)(2,1)S(1)} %maximum_select_fusion.5), channel_id=1, source_target_pairs={{0,32},{8,40},{16,48},{24,56},{32,0},{40,8},{48,16},{56,24},{64,96... | collective-permute-start | bytes 786440 | tf_op jit(solution)/shard_map/ppermute | solution.py:33
  41.9 0.8 copy-start.1
  41.9 40.6 %collective-permute-start.3 = (bf16[64,8,512]{2,1,0:T(8,128)(2,1)S(1)}, bf16[64,8,512]{2,1,0:T(8,128)(2,1)}, u32[]{:S(2)}, u32[]{:S(2)}) collective-permute-start(bf16[64,8,512]{2,1,0:T(8,128)(2,1)S(1)} %maximum_select_fusion.2), channel_id=1, source_target_pairs={{0,16},{8,24},{16,0},{24,8},{32,48},{40,56},{48,32},{56,40},{64,80... | collective-permute-start | bytes 1572872 | tf_op jit(solution)/shard_map/ppermute | solution.py:33
  84.2 6.4 %copy-start.3 = (bf16[256,256]{1,0:T(8,128)(2,1)S(1)}, bf16[256,256]{1,0:T(8,128)(2,1)}, u32[]{:S(2)}) copy-start(bf16[256,256]{1,0:T(8,128)(2,1)} %param.21) | copy-start | bytes 393220
  84.2 4.5 %collective-permute-start.4 = (bf16[128,8,512]{2,1,0:T(8,128)(2,1)S(1)}, bf16[128,8,512]{2,1,0:T(8,128)(2,1)}, u32[]{:S(2)}, u32[]{:S(2)}) collective-permute-start(bf16[128,8,512]{2,1,0:T(8,128)(2,1)S(1)} %maximum_select_fusion.1), channel_id=1, source_target_pairs={{0,8},{8,0},{16,24},{24,16},{32,40},{40,32},{48,56},{56,48},{64,72... | collective-permute-start | bytes 3145736 | tf_op jit(solution)/shard_map/ppermute | solution.py:33
  86.3 4.8 %copy-start.2 = (bf16[256,256]{1,0:T(8,128)(2,1)S(1)}, bf16[256,256]{1,0:T(8,128)(2,1)}, u32[]{:S(2)}) copy-start(bf16[256,256]{1,0:T(8,128)(2,1)} %param.20) | copy-start | bytes 393220
  110.8 7.8 %copy-start.7 = (s32[1,16]{1,0:T(1,128)S(1)}, s32[1,16]{1,0:T(1,128)}, u32[]{:S(2)}) copy-start(s32[1,16]{1,0:T(1,128)} %param.25) | copy-start | bytes 196
  110.8 38.6 %all-to-all-start.1 = ((f32[8,256,288]{1,2,0:T(8,128)}), f32[8,256,288]{1,2,0:T(8,128)}, u32[]{:S(2)}, u32[]{:S(2)}) async-start(f32[8,256,288]{1,2,0:T(8,128)} %pad_maximum_fusion.1), calls=%async_computation.1 | async-start | bytes 4718592 | tf_op jit(solution)/shard_map/all_to_all | solution.py:103
  151.8 6.8 %copy-start.6 = (s32[32]{0:T(128)S(1)}, s32[32]{0:T(128)}, u32[]{:S(2)}) copy-start(s32[32]{0:T(128)} %param.26) | copy-start | bytes 388
  155.3 5.5 %collective-permute-start.5 = (f32[32,256]{1,0:T(8,128)S(1)}, f32[32,256]{1,0:T(8,128)S(1)}, u32[]{:S(2)}, u32[]{:S(2)}) collective-permute-start(f32[32,256]{1,0:T(8,128)S(1)} %slice.91), channel_id=1, source_target_pairs={{0,8},{8,16},{16,24},{24,32},{32,40},{40,48},{48,56},{56,64},{64,7... | collective-permute-start | bytes 98312 | tf_op jit(solution)/shard_map/ppermute | solution.py:16
  161.8 44.7 %copy-start.5 = (s32[512,1]{0,1:T(1,128)S(1)}, s32[512,1]{0,1:T(1,128)}, u32[]{:S(2)}) copy-start(s32[512,1]{0,1:T(1,128)} %param.27) | copy-start | bytes 6148
  168.5 4.8 %collective-permute-start.6 = (f32[16,257]{1,0:T(8,128)S(1)}, f32[16,257]{1,0:T(8,128)S(1)}, u32[]{:S(2)}, u32[]{:S(2)}) collective-permute-start(f32[16,257]{1,0:T(8,128)S(1)} %pad_maximum_fusion.2), channel_id=1, source_target_pairs={{0,1},{1,0},{2,3},{3,2},{4,5},{5,4},{6,7},{7,6},{8,9},{9,8},{10,11... | collective-permute-start | bytes 49352 | tf_op jit(solution)/shard_map/ppermute | solution.py:23
  173.3 2.7 %collective-permute-start.7 = (f32[16,257]{1,0:T(8,128)S(1)}, f32[16,257]{1,0:T(8,128)S(1)}, u32[]{:S(2)}, u32[]{:S(2)}) collective-permute-start(f32[16,257]{1,0:T(8,128)S(1)} %fusion.36), channel_id=1, source_target_pairs={{0,2},{1,3},{2,0},{3,1},{4,6},{5,7},{6,4},{7,5},{8,10},{9,11},{10,... | collective-permute-start | bytes 49352 | tf_op jit(solution)/shard_map/ppermute | solution.py:23
  176.0 4.2 %collective-permute-start.8 = (f32[16,257]{1,0:T(8,128)S(1)}, f32[16,257]{1,0:T(8,128)S(1)}, u32[]{:S(2)}, u32[]{:S(2)}) collective-permute-start(f32[16,257]{1,0:T(8,128)S(1)} %add.76), channel_id=1, source_target_pairs={{0,4},{1,5},{2,6},{3,7},{4,0},{5,1},{6,2},{7,3},{8,12},{9,13},{10,... | collective-permute-start | bytes 49352 | tf_op jit(solution)/shard_map/ppermute | solution.py:23
  180.4 6.5 %collective-permute-start.9 = (f32[16,256]{1,0:T(8,128)S(1)}, f32[16,256]{1,0:T(8,128)S(1)}, u32[]{:S(2)}, u32[]{:S(2)}) collective-permute-start(f32[16,256]{1,0:T(8,128)S(1)} %slice_divide_fusion), channel_id=1, source_target_pairs={{0,128},{8,136},{16,144},{24,152},{32,160},{40,168},{48,176},{56,1... | collective-permute-start | bytes 49160 | tf_op jit(solution)/shard_map/ppermute | solution.py:33
  186.9 4.0 %collective-permute-start.10 = (f32[32,256]{1,0:T(8,128)S(1)}, f32[32,256]{1,0:T(8,128)S(1)}, u32[]{:S(2)}, u32[]{:S(2)}) collective-permute-start(f32[32,256]{1,0:T(8,128)S(1)} %maximum_select_fusion.10), channel_id=1, source_target_pairs={{0,64},{8,72},{16,80},{24,88},{32,96},{40,104},{48,112},{56,120},{... | collective-permute-start | bytes 98312 | tf_op jit(solution)/shard_map/ppermute | solution.py:33
  191.0 3.2 %collective-permute-start.11 = (f32[64,256]{1,0:T(8,128)S(1)}, f32[64,256]{1,0:T(8,128)S(1)}, u32[]{:S(2)}, u32[]{:S(2)}) collective-permute-start(f32[64,256]{1,0:T(8,128)S(1)} %maximum_select_fusion.9), channel_id=1, source_target_pairs={{0,32},{8,40},{16,48},{24,56},{32,0},{40,8},{48,16},{56,24},{64,96... | collective-permute-start | bytes 196616 | tf_op jit(solution)/shard_map/ppermute | solution.py:33
  194.2 4.1 %collective-permute-start.12 = (f32[128,256]{1,0:T(8,128)S(1)}, f32[128,256]{1,0:T(8,128)S(1)}, u32[]{:S(2)}, u32[]{:S(2)}) collective-permute-start(f32[128,256]{1,0:T(8,128)S(1)} %maximum_select_fusion.8), channel_id=1, source_target_pairs={{0,16},{8,24},{16,0},{24,8},{32,48},{40,56},{48,32},{56,40},{64,80... | collective-permute-start | bytes 393224 | tf_op jit(solution)/shard_map/ppermute | solution.py:33
  198.3 9.4 %collective-permute-start.13 = (f32[256,256]{1,0:T(8,128)S(1)}, f32[256,256]{1,0:T(8,128)S(1)}, u32[]{:S(2)}, u32[]{:S(2)}) collective-permute-start(f32[256,256]{1,0:T(8,128)S(1)} %maximum_select_fusion.6), channel_id=1, source_target_pairs={{0,8},{8,0},{16,24},{24,16},{32,40},{40,32},{48,56},{56,48},{64,72... | collective-permute-start | bytes 786440 | tf_op jit(solution)/shard_map/ppermute | solution.py:33

commit v7 on v6

--- a/solution.py
+++ b/solution.py
@@ -92,7 +92,6 @@
     )
     outer = jnp.einsum("qti,qtj->qij", q_out, q_in, precision=highest)
     query_grad = (outer * scale_block[None]).astype(jnp.bfloat16)
-    gathered_parts, query_grad = lax.optimization_barrier((gathered_parts, query_grad))
     chunk_sums = jnp.sum(gathered_parts.reshape(factor_count, chunk, rank_in + rank_out), axis=0)
     rot_in_chunk = jnp.dot(chunk_sums[:, :rank_in], basis_in_wide, precision=highest)
     rot_out_chunk = jnp.dot(chunk_sums[:, rank_in:], basis_out_wide, precision=highest)

time: 209 us -> 176 us (0.84)
  waiting for transfers between devices: 112 us -> 74.3 us
  starting transfers between devices: 42.5 us -> 50.9 us
  local copies, waits for them, and re-layouts: 14 us -> 8.2 us
  matrix products: 28.2 us -> 30.3 us
    ppermute x10, waiting for transfers between devices: 72.2 us -> 22 us  [butterfly_gather(): other = lax.ppermute(block, axis, [(i, i ^ step) for i in range(size)])]
    all_to_all x1, waiting for transfers between devices: 0.01 us -> 27.9 us  [per_device(): gathered_parts = lax.all_to_all(stacked_parts, 'factor', 0, 0, tiled=True)]
    all_to_all x1, waiting for transfers between devices: 30.5 us -> 15 us  [per_device(): received = lax.all_to_all(sending, 'factor', 0, 0, tiled=True)]
    ppermute x10, starting transfers between devices: 22.7 us -> 30.6 us  [butterfly_gather(): other = lax.ppermute(block, axis, [(i, i ^ step) for i in range(size)])]
    all_to_all x2 -> x1, local copies, waits for them, and re-layouts: 7.69 us -> 2.33 us  [per_device(): gathered_parts = lax.all_to_all(stacked_parts, 'factor', 0, 0, tiled=True)]
    all_to_all x1, starting transfers between devices: 7.77 us -> 4.5 us  [per_device(): received = lax.all_to_all(sending, 'factor', 0, 0, tiled=True)]
    ppermute x1, starting transfers between devices: 3.29 us -> 6.45 us  [from_behind(): return lax.ppermute(block, axis, route)]
  transfers between devices with their start and end apart: 16 -> 16, of which waited for: 13 -> 14; matrix products, arithmetic and copies ran while one was open for 12% -> 13% of each run, Pallas kernels for 0% -> 0%
where the time goes in v7:
time: 176 us; the launch traced here: 175 us
  waiting for transfers between devices  74.3 us (42%)
  starting transfers between devices  50.9 us (29%)
  matrix products  30.3 us (17%)
  other arithmetic  9.76 us (6%)
  local copies, waits for them, and re-layouts  8.2 us (5%)
  between operations  1.78 us (1%)
    ppermute x10, starting transfers between devices, butterfly_gather(): other = lax.ppermute(block, axis, [(i, i ^ step) for i in range(size)])  30.6 us
    all_to_all x1, waiting for transfers between devices, per_device(): gathered_parts = lax.all_to_all(stacked_parts, 'factor', 0, 0, tiled=True)  27.9 us
    ppermute x10, waiting for transfers between devices, butterfly_gather(): other = lax.ppermute(block, axis, [(i, i ^ step) for i in range(size)])  22 us
    all_to_all x1, waiting for transfers between devices, per_device(): received = lax.all_to_all(sending, 'factor', 0, 0, tiled=True)  15 us
    ppermute x3, waiting for transfers between devices, butterfly_sum(): lax.ppermute(block, axis, [(i, i ^ step) for i in range(size)])  9.32 us
    dot_general x1, matrix products, per_device(): outer = jnp.einsum('qti,qtj->qij', q_out, q_in, precision=highest)  8.55 us
    all_to_all x1, starting transfers between devices, per_device(): gathered_parts = lax.all_to_all(stacked_parts, 'factor', 0, 0, tiled=True)  7.6 us
    dot_general x1, matrix products, per_device(): lax.dot_general(grad_low, query_grad, (((1, 2), (1, 2)), ((), ())), prefe...  6.64 us
  transfers between devices with their start and end apart: 16, of which 14 were waited for; matrix products, arithmetic and copies ran while one was open for 13% of the time, Pallas kernels for 0%

profile of v7, /device:TPU:1, one launch (start us, length us, event | category | flops | bytes accessed | tf_op | source)
XLA Modules:
  0.0 175.2 jit_solution(5587162217992293762)
XLA Ops:
  0.0 1.6 copy-done
  1.6 1.7 fusion.39
  3.3 5.2 %fusion.38 = f32[2048,256]{0,1:T(8,128)S(1)} fusion(bf16[2048,1792]{1,0:T(8,128)(2,1)} %param.16, bf16[1792,256]{1,0:T(8,128)(2,1)S(1)} %copy-done.11), kind=kOutput, calls=%fused_computation.69 | convolution fusion | flops 1879048192 | bytes 10354688 | tf_op jit(solution)/shard_map/dot_general | solution.py:82
  8.8 2.3 %copy.93 = f32[64,8,8,256]{3,2,0,1:T(8,128)} copy(f32[64,8,8,256]{3,2,1,0:T(8,128)S(1)} %bitcast.53) | data formatting | bytes 8388608 | tf_op jit(solution)/shard_map/all_to_all | solution.py:85
  11.1 7.6 %all-to-all-start = ((f32[8,256,512]{1,2,0:T(8,128)}), f32[8,256,512]{1,2,0:T(8,128)}, u32[]{:S(2)}, u32[]{:S(2)}) async-start(f32[8,256,512]{1,2,0:T(8,128)} %bitcast.52), calls=%async_computation | async-start | bytes 8388608 | tf_op jit(solution)/shard_map/all_to_all | solution.py:85
  18.8 7.0 %collective-permute-start = (bf16[8,8,512]{2,1,0:T(8,128)(2,1)S(1)}, bf16[8,8,512]{2,1,0:T(8,128)(2,1)S(1)}, u32[]{:S(2)}, u32[]{:S(2)}) collective-permute-start(bf16[8,8,512]{2,1,0:T(8,128)(2,1)S(1)} %constant_dynamic-update-slice_fusion), channel_id=1, source_target_pairs={{0,128},{8,136},{16,144},{24,152},{32,160},{40,168},{48,176},{56,1... | collective-permute-start | bytes 196616 | tf_op jit(solution)/shard_map/ppermute | solution.py:33
  25.8 1.7 collective-permute-done
  29.0 5.7 %collective-permute-done.1 = bf16[16,8,512]{2,1,0:T(8,128)(2,1)S(1)} collective-permute-done((bf16[16,8,512]{2,1,0:T(8,128)(2,1)S(1)}, bf16[16,8,512]{2,1,0:T(8,128)(2,1)S(1)}, u32[]{:S(2)}, u32[]{:S(2)}) %collective-permute-start.1) | collective-permute-done | bytes 131104 | tf_op jit(solution)/shard_map/ppermute | solution.py:33
  34.9 5.6 %collective-permute-done.2 = bf16[32,8,512]{2,1,0:T(8,128)(2,1)S(1)} collective-permute-done((bf16[32,8,512]{2,1,0:T(8,128)(2,1)S(1)}, bf16[32,8,512]{2,1,0:T(8,128)(2,1)S(1)}, u32[]{:S(2)}, u32[]{:S(2)}) %collective-permute-start.2) | collective-permute-done | bytes 262176 | tf_op jit(solution)/shard_map/ppermute | solution.py:33
  41.0 27.9 %all-to-all-done = f32[8,256,512]{1,2,0:T(8,128)} async-done(((f32[8,256,512]{1,2,0:T(8,128)}), f32[8,256,512]{1,2,0:T(8,128)}, u32[]{:S(2)}, u32[]{:S(2)}) %all-to-all-start) | async-done | bytes 4194336 | tf_op jit(solution)/shard_map/all_to_all | solution.py:85
  68.9 2.5 %reduce_sum.28 = f32[256,512]{0,1:T(8,128)S(1)} reduce(f32[8,256,512]{1,2,0:T(8,128)} %all-to-all-done, f32[]{:T(128)} %constant.180.clone.1), dimensions={0}, to_apply=%region_2.3 | reduce | flops 917504 | bytes 4718596 | tf_op jit(solution)/shard_map/reduce_sum | solution.py:95
  72.3 1.6 pad_maximum_fusion.1
  73.8 4.5 %all-to-all-start.1 = ((f32[8,256,288]{1,2,0:T(8,128)}), f32[8,256,288]{1,2,0:T(8,128)}, u32[]{:S(2)}, u32[]{:S(2)}) async-start(f32[8,256,288]{1,2,0:T(8,128)} %pad_maximum_fusion.1), calls=%async_computation.1 | async-start | bytes 4718592 | tf_op jit(solution)/shard_map/all_to_all | solution.py:102
  78.4 1.8 %maximum_select_fusion.1 = bf16[128,8,512]{2,1,0:T(8,128)(2,1)S(1)} fusion(bf16[64,8,512]{2,1,0:T(8,128)(2,1)} %copy-done.2, bf16[64,8,512]{2,1,0:T(8,128)(2,1)} %collective-permute-done.3, pred[]{:T(512)S(6)} %eq.95), kind=kLoop, calls=%fused_computation.14 | loop fusion | flops 1572864 | bytes 2097153 | tf_op jit(solution)/shard_map/jit(_where)/select_n | solution.py:35
  80.2 3.5 %collective-permute-start.4 = (bf16[128,8,512]{2,1,0:T(8,128)(2,1)S(1)}, bf16[128,8,512]{2,1,0:T(8,128)(2,1)}, u32[]{:S(2)}, u32[]{:S(2)}) collective-permute-start(bf16[128,8,512]{2,1,0:T(8,128)(2,1)S(1)} %maximum_select_fusion.1), channel_id=1, source_target_pairs={{0,8},{8,0},{16,24},{24,16},{32,40},{40,32},{48,56},{56,48},{64,72... | collective-permute-start | bytes 3145736 | tf_op jit(solution)/shard_map/ppermute | solution.py:33
  86.1 1.9 %maximum_select_fusion = bf16[256,8,512]{2,1,0:T(8,128)(2,1)S(1)} fusion(bf16[128,8,512]{2,1,0:T(8,128)(2,1)S(1)} %maximum_select_fusion.1, bf16[128,8,512]{2,1,0:T(8,128)(2,1)} %collective-permute-done.4, pred[]{:T(512)S(6)} %eq.94), kind=kLoop, calls=%fused_computation.8 | loop fusion | flops 3145728 | bytes 4194305 | tf_op jit(solution)/shard_map/jit(_where)/select_n | solution.py:35
  89.3 1.8 %fusion.4 = f32[256,8,256]{2,1,0:T(8,128)} fusion(bf16[256,8,512]{2,1,0:T(8,128)(2,1)S(1)} %maximum_select_fusion, bf16[256,256]{1,0:T(8,128)(2,1)S(1)} %copy-done.3), kind=kOutput, calls=%fused_computation.10 | convolution fusion | flops 268435456 | bytes 3276800 | tf_op jit(solution)/shard_map/qtk,kl->qtl/dot_general | solution.py:87
  91.2 15.0 %all-to-all-done.1 = f32[8,256,288]{1,2,0:T(8,128)} async-done(((f32[8,256,288]{1,2,0:T(8,128)}), f32[8,256,288]{1,2,0:T(8,128)}, u32[]{:S(2)}, u32[]{:S(2)}) %all-to-all-start.1) | async-done | bytes 2359328 | tf_op jit(solution)/shard_map/all_to_all | solution.py:102
  106.2 1.9 %copy.88 = f32[8,36,8,256]{3,2,0,1:T(8,128)S(1)} copy(f32[8,36,8,256]{3,2,1,0:T(8,128)} %bitcast.28) | data formatting | bytes 4718592 | tf_op jit(solution)/shard_map/all_to_all | solution.py:102
  108.7 3.5 %fusion.2 = f32[512,256]{1,0:T(8,128)S(1)} fusion(f32[2048,512]{0,1:T(8,128)S(1)} %bitcast.54, f32[2048,288]{0,1:T(8,128)S(1)} %bitcast.56), kind=kOutput, calls=%fused_computation.6 | convolution fusion | flops 3221225472 | bytes 6815744 | tf_op jit(solution)/shard_map/dot_general | solution.py:116
  112.2 6.5 %collective-permute-start.5 = (f32[32,256]{1,0:T(8,128)S(1)}, f32[32,256]{1,0:T(8,128)S(1)}, u32[]{:S(2)}, u32[]{:S(2)}) collective-permute-start(f32[32,256]{1,0:T(8,128)S(1)} %slice.91), channel_id=1, source_target_pairs={{0,8},{8,16},{16,24},{24,32},{32,40},{40,48},{48,56},{56,64},{64,7... | collective-permute-start | bytes 98312 | tf_op jit(solution)/shard_map/ppermute | solution.py:16
  118.6 8.6 %multiply_convert_fusion = bf16[256,32,256]{2,1,0:T(8,128)(2,1)} fusion(f32[32,256]{1,0:T(8,128)S(1)} %add_divide_fusion, f32[256,8,32]{2,1,0:T(8,128)S(1)} %fusion.6, f32[256,8,256]{2,1,0:T(8,128)S(1)} %copy-done.1), kind=kOutput, calls=%fused_computation | convolution fusion | flops 205520896 | bytes 6586368 | tf_op jit(solution)/shard_map/qti,qtj->qij/dot_general | solution.py:93
  128.5 6.6 %fusion = f32[256,16,1]{1,0,2:T(8,128)S(1)} fusion(bf16[256,32,256]{2,1,0:T(8,128)(2,1)} %multiply_convert_fusion, f32[16,32,256]{2,0,1:T(8,128)S(1)} %scatter-mul.4), kind=kOutput, calls=%fused_computation.3 | convolution fusion | flops 67239936 | bytes 4734976 | tf_op jit(solution)/shard_map/dot_general | solution.py:130
  136.4 3.0 %collective-permute-done.6 = f32[16,257]{1,0:T(8,128)S(1)} collective-permute-done((f32[16,257]{1,0:T(8,128)S(1)}, f32[16,257]{1,0:T(8,128)S(1)}, u32[]{:S(2)}, u32[]{:S(2)}) %collective-permute-start.6) | collective-permute-done | bytes 16480 | tf_op jit(solution)/shard_map/ppermute | solution.py:23
  139.5 2.7 %collective-permute-done.7 = f32[16,257]{1,0:T(8,128)S(1)} collective-permute-done((f32[16,257]{1,0:T(8,128)S(1)}, f32[16,257]{1,0:T(8,128)S(1)}, u32[]{:S(2)}, u32[]{:S(2)}) %collective-permute-start.7) | collective-permute-done | bytes 16480 | tf_op jit(solution)/shard_map/ppermute | solution.py:23
  142.7 3.6 %collective-permute-done.8 = f32[16,257]{1,0:T(8,128)S(1)} collective-permute-done((f32[16,257]{1,0:T(8,128)S(1)}, f32[16,257]{1,0:T(8,128)S(1)}, u32[]{:S(2)}, u32[]{:S(2)}) %collective-permute-start.8) | collective-permute-done | bytes 16480 | tf_op jit(solution)/shard_map/ppermute | solution.py:23
  146.5 6.9 %collective-permute-start.9 = (f32[16,256]{1,0:T(8,128)S(1)}, f32[16,256]{1,0:T(8,128)S(1)}, u32[]{:S(2)}, u32[]{:S(2)}) collective-permute-start(f32[16,256]{1,0:T(8,128)S(1)} %slice_divide_fusion), channel_id=1, source_target_pairs={{0,128},{8,136},{16,144},{24,152},{32,160},{40,168},{48,176},{56,1... | collective-permute-start | bytes 49160 | tf_op jit(solution)/shard_map/ppermute | solution.py:33
  156.0 2.3 %collective-permute-done.10 = f32[32,256]{1,0:T(8,128)S(1)} collective-permute-done((f32[32,256]{1,0:T(8,128)S(1)}, f32[32,256]{1,0:T(8,128)S(1)}, u32[]{:S(2)}, u32[]{:S(2)}) %collective-permute-start.10) | collective-permute-done | bytes 32800 | tf_op jit(solution)/shard_map/ppermute | solution.py:33
  159.2 2.3 %collective-permute-done.11 = f32[64,256]{1,0:T(8,128)S(1)} collective-permute-done((f32[64,256]{1,0:T(8,128)S(1)}, f32[64,256]{1,0:T(8,128)S(1)}, u32[]{:S(2)}, u32[]{:S(2)}) %collective-permute-start.11) | collective-permute-done | bytes 65568 | tf_op jit(solution)/shard_map/ppermute | solution.py:33
  161.6 3.0 %collective-permute-start.12 = (f32[128,256]{1,0:T(8,128)S(1)}, f32[128,256]{1,0:T(8,128)S(1)}, u32[]{:S(2)}, u32[]{:S(2)}) collective-permute-start(f32[128,256]{1,0:T(8,128)S(1)} %maximum_select_fusion.8), channel_id=1, source_target_pairs={{0,16},{8,24},{16,0},{24,8},{32,48},{40,56},{48,32},{56,40},{64,80... | collective-permute-start | bytes 393224 | tf_op jit(solution)/shard_map/ppermute | solution.py:33
  164.6 2.7 %collective-permute-done.12 = f32[128,256]{1,0:T(8,128)S(1)} collective-permute-done((f32[128,256]{1,0:T(8,128)S(1)}, f32[128,256]{1,0:T(8,128)S(1)}, u32[]{:S(2)}, u32[]{:S(2)}) %collective-permute-start.12) | collective-permute-done | bytes 131104 | tf_op jit(solution)/shard_map/ppermute | solution.py:33
  167.2 5.9 %collective-permute-start.13 = (f32[256,256]{1,0:T(8,128)S(1)}, f32[256,256]{1,0:T(8,128)S(1)}, u32[]{:S(2)}, u32[]{:S(2)}) collective-permute-start(f32[256,256]{1,0:T(8,128)S(1)} %maximum_select_fusion.6), channel_id=1, source_target_pairs={{0,8},{8,0},{16,24},{24,16},{32,40},{40,32},{48,56},{56,48},{64,72... | collective-permute-start | bytes 786440 | tf_op jit(solution)/shard_map/ppermute | solution.py:33
  (85 shorter events, 15.0 us)
Async XLA Ops:
  0.0 1.6 copy-start
  0.0 3.3 %copy-start.11 = (bf16[1792,256]{1,0:T(8,128)(2,1)S(1)}, bf16[1792,256]{1,0:T(8,128)(2,1)}, u32[]{:S(2)}) copy-start(bf16[1792,256]{1,0:T(8,128)(2,1)} %param.18) | copy-start | bytes 2752516
  11.1 7.6 %copy-start.5 = (bf16[8,8,256]{2,1,0:T(8,128)(2,1)S(1)}, bf16[8,8,256]{2,1,0:T(8,128)(2,1)}, u32[]{:S(2)}) copy-start(bf16[8,8,256]{2,1,0:T(8,128)(2,1)} %param.23) | copy-start | bytes 98308
  11.1 7.6 %copy-start.6 = (bf16[8,8,256]{2,1,0:T(8,128)(2,1)S(1)}, bf16[8,8,256]{2,1,0:T(8,128)(2,1)}, u32[]{:S(2)}) copy-start(bf16[8,8,256]{2,1,0:T(8,128)(2,1)} %param.24) | copy-start | bytes 98308
  11.1 57.8 %all-to-all-start = ((f32[8,256,512]{1,2,0:T(8,128)}), f32[8,256,512]{1,2,0:T(8,128)}, u32[]{:S(2)}, u32[]{:S(2)}) async-start(f32[8,256,512]{1,2,0:T(8,128)} %bitcast.52), calls=%async_computation | async-start | bytes 8388608 | tf_op jit(solution)/shard_map/all_to_all | solution.py:85
  18.8 8.7 %collective-permute-start = (bf16[8,8,512]{2,1,0:T(8,128)(2,1)S(1)}, bf16[8,8,512]{2,1,0:T(8,128)(2,1)S(1)}, u32[]{:S(2)}, u32[]{:S(2)}) collective-permute-start(bf16[8,8,512]{2,1,0:T(8,128)(2,1)S(1)} %constant_dynamic-update-slice_fusion), channel_id=1, source_target_pairs={{0,128},{8,136},{16,144},{24,152},{32,160},{40,168},{48,176},{56,1... | collective-permute-start | bytes 196616 | tf_op jit(solution)/shard_map/ppermute | solution.py:33
  27.5 7.2 %collective-permute-start.1 = (bf16[16,8,512]{2,1,0:T(8,128)(2,1)S(1)}, bf16[16,8,512]{2,1,0:T(8,128)(2,1)S(1)}, u32[]{:S(2)}, u32[]{:S(2)}) collective-permute-start(bf16[16,8,512]{2,1,0:T(8,128)(2,1)S(1)} %maximum_select_fusion.7), channel_id=1, source_target_pairs={{0,64},{8,72},{16,80},{24,88},{32,96},{40,104},{48,112},{56,120},{... | collective-permute-start | bytes 393224 | tf_op jit(solution)/shard_map/ppermute | solution.py:33
  34.7 5.7 %collective-permute-start.2 = (bf16[32,8,512]{2,1,0:T(8,128)(2,1)S(1)}, bf16[32,8,512]{2,1,0:T(8,128)(2,1)S(1)}, u32[]{:S(2)}, u32[]{:S(2)}) collective-permute-start(bf16[32,8,512]{2,1,0:T(8,128)(2,1)S(1)} %maximum_select_fusion.5), channel_id=1, source_target_pairs={{0,32},{8,40},{16,48},{24,56},{32,0},{40,8},{48,16},{56,24},{64,96... | collective-permute-start | bytes 786440 | tf_op jit(solution)/shard_map/ppermute | solution.py:33
  40.5 30.9 %copy-start.2 = (bf16[64,8,512]{2,1,0:T(8,128)(2,1)}, bf16[64,8,512]{2,1,0:T(8,128)(2,1)S(1)}, u32[]{:S(2)}) copy-start(bf16[64,8,512]{2,1,0:T(8,128)(2,1)S(1)} %maximum_select_fusion.2) | copy-start | bytes 1572868
  40.5 30.9 %copy-start.4 = (bf16[256,256]{1,0:T(8,128)(2,1)S(1)}, bf16[256,256]{1,0:T(8,128)(2,1)}, u32[]{:S(2)}) copy-start(bf16[256,256]{1,0:T(8,128)(2,1)} %param.21) | copy-start | bytes 393220
  40.5 31.2 %copy-start.3 = (bf16[256,256]{1,0:T(8,128)(2,1)S(1)}, bf16[256,256]{1,0:T(8,128)(2,1)}, u32[]{:S(2)}) copy-start(bf16[256,256]{1,0:T(8,128)(2,1)} %param.20) | copy-start | bytes 393220
  40.6 37.8 %collective-permute-start.3 = (bf16[64,8,512]{2,1,0:T(8,128)(2,1)S(1)}, bf16[64,8,512]{2,1,0:T(8,128)(2,1)}, u32[]{:S(2)}, u32[]{:S(2)}) collective-permute-start(bf16[64,8,512]{2,1,0:T(8,128)(2,1)S(1)} %maximum_select_fusion.2), channel_id=1, source_target_pairs={{0,16},{8,24},{16,0},{24,8},{32,48},{40,56},{48,32},{56,40},{64,80... | collective-permute-start | bytes 1572872 | tf_op jit(solution)/shard_map/ppermute | solution.py:33
  73.8 9.8 %copy-start.10 = (s32[1,16]{1,0:T(1,128)S(1)}, s32[1,16]{1,0:T(1,128)}, u32[]{:S(2)}) copy-start(s32[1,16]{1,0:T(1,128)} %param.25) | copy-start | bytes 196
  73.8 10.1 %copy-start.9 = (s32[32]{0:T(128)S(1)}, s32[32]{0:T(128)}, u32[]{:S(2)}) copy-start(s32[32]{0:T(128)} %param.26) | copy-start | bytes 388
  73.8 12.0 %copy-start.7 = (f32[32,256]{1,0:T(8,128)S(1)}, f32[32,256]{1,0:T(8,128)}, u32[]{:S(2)}) copy-start(f32[32,256]{1,0:T(8,128)} %param.22) | copy-start | bytes 98308
  73.8 32.4 %all-to-all-start.1 = ((f32[8,256,288]{1,2,0:T(8,128)}), f32[8,256,288]{1,2,0:T(8,128)}, u32[]{:S(2)}, u32[]{:S(2)}) async-start(f32[8,256,288]{1,2,0:T(8,128)} %pad_maximum_fusion.1), calls=%async_computation.1 | async-start | bytes 4718592 | tf_op jit(solution)/shard_map/all_to_all | solution.py:102
  80.2 5.9 %collective-permute-start.4 = (bf16[128,8,512]{2,1,0:T(8,128)(2,1)S(1)}, bf16[128,8,512]{2,1,0:T(8,128)(2,1)}, u32[]{:S(2)}, u32[]{:S(2)}) collective-permute-start(bf16[128,8,512]{2,1,0:T(8,128)(2,1)S(1)} %maximum_select_fusion.1), channel_id=1, source_target_pairs={{0,8},{8,0},{16,24},{24,16},{32,40},{40,32},{48,56},{56,48},{64,72... | collective-permute-start | bytes 3145736 | tf_op jit(solution)/shard_map/ppermute | solution.py:33
  108.7 10.0 %copy-start.1 = (f32[256,8,256]{2,1,0:T(8,128)S(1)}, f32[256,8,256]{2,1,0:T(8,128)}, u32[]{:S(2)}) copy-start(f32[256,8,256]{2,1,0:T(8,128)} %fusion.4) | copy-start | bytes 6291460
  112.2 15.3 %collective-permute-start.5 = (f32[32,256]{1,0:T(8,128)S(1)}, f32[32,256]{1,0:T(8,128)S(1)}, u32[]{:S(2)}, u32[]{:S(2)}) collective-permute-start(f32[32,256]{1,0:T(8,128)S(1)} %slice.91), channel_id=1, source_target_pairs={{0,8},{8,16},{16,24},{24,32},{32,40},{40,48},{48,56},{56,64},{64,7... | collective-permute-start | bytes 98312 | tf_op jit(solution)/shard_map/ppermute | solution.py:16
  128.5 44.6 %copy-start.8 = (s32[512,1]{0,1:T(1,128)S(1)}, s32[512,1]{0,1:T(1,128)}, u32[]{:S(2)}) copy-start(s32[512,1]{0,1:T(1,128)} %param.27) | copy-start | bytes 6148
  135.2 4.3 %collective-permute-start.6 = (f32[16,257]{1,0:T(8,128)S(1)}, f32[16,257]{1,0:T(8,128)S(1)}, u32[]{:S(2)}, u32[]{:S(2)}) collective-permute-start(f32[16,257]{1,0:T(8,128)S(1)} %pad_maximum_fusion.2), channel_id=1, source_target_pairs={{0,1},{1,0},{2,3},{3,2},{4,5},{5,4},{6,7},{7,6},{8,9},{9,8},{10,11... | collective-permute-start | bytes 49352 | tf_op jit(solution)/shard_map/ppermute | solution.py:23
  139.5 2.7 %collective-permute-start.7 = (f32[16,257]{1,0:T(8,128)S(1)}, f32[16,257]{1,0:T(8,128)S(1)}, u32[]{:S(2)}, u32[]{:S(2)}) collective-permute-start(f32[16,257]{1,0:T(8,128)S(1)} %fusion.36), channel_id=1, source_target_pairs={{0,2},{1,3},{2,0},{3,1},{4,6},{5,7},{6,4},{7,5},{8,10},{9,11},{10,... | collective-permute-start | bytes 49352 | tf_op jit(solution)/shard_map/ppermute | solution.py:23
  142.1 4.2 %collective-permute-start.8 = (f32[16,257]{1,0:T(8,128)S(1)}, f32[16,257]{1,0:T(8,128)S(1)}, u32[]{:S(2)}, u32[]{:S(2)}) collective-permute-start(f32[16,257]{1,0:T(8,128)S(1)} %add.76), channel_id=1, source_target_pairs={{0,4},{1,5},{2,6},{3,7},{4,0},{5,1},{6,2},{7,3},{8,12},{9,13},{10,... | collective-permute-start | bytes 49352 | tf_op jit(solution)/shard_map/ppermute | solution.py:23
  146.5 8.1 %collective-permute-start.9 = (f32[16,256]{1,0:T(8,128)S(1)}, f32[16,256]{1,0:T(8,128)S(1)}, u32[]{:S(2)}, u32[]{:S(2)}) collective-permute-start(f32[16,256]{1,0:T(8,128)S(1)} %slice_divide_fusion), channel_id=1, source_target_pairs={{0,128},{8,136},{16,144},{24,152},{32,160},{40,168},{48,176},{56,1... | collective-permute-start | bytes 49160 | tf_op jit(solution)/shard_map/ppermute | solution.py:33
  154.6 3.7 %collective-permute-start.10 = (f32[32,256]{1,0:T(8,128)S(1)}, f32[32,256]{1,0:T(8,128)S(1)}, u32[]{:S(2)}, u32[]{:S(2)}) collective-permute-start(f32[32,256]{1,0:T(8,128)S(1)} %maximum_select_fusion.10), channel_id=1, source_target_pairs={{0,64},{8,72},{16,80},{24,88},{32,96},{40,104},{48,112},{56,120},{... | collective-permute-start | bytes 98312 | tf_op jit(solution)/shard_map/ppermute | solution.py:33
  158.3 3.2 %collective-permute-start.11 = (f32[64,256]{1,0:T(8,128)S(1)}, f32[64,256]{1,0:T(8,128)S(1)}, u32[]{:S(2)}, u32[]{:S(2)}) collective-permute-start(f32[64,256]{1,0:T(8,128)S(1)} %maximum_select_fusion.9), channel_id=1, source_target_pairs={{0,32},{8,40},{16,48},{24,56},{32,0},{40,8},{48,16},{56,24},{64,96... | collective-permute-start | bytes 196616 | tf_op jit(solution)/shard_map/ppermute | solution.py:33
  161.6 5.7 %collective-permute-start.12 = (f32[128,256]{1,0:T(8,128)S(1)}, f32[128,256]{1,0:T(8,128)S(1)}, u32[]{:S(2)}, u32[]{:S(2)}) collective-permute-start(f32[128,256]{1,0:T(8,128)S(1)} %maximum_select_fusion.8), channel_id=1, source_target_pairs={{0,16},{8,24},{16,0},{24,8},{32,48},{40,56},{48,32},{56,40},{64,80... | collective-permute-start | bytes 393224 | tf_op jit(solution)/shard_map/ppermute | solution.py:33
  167.2 7.0 %collective-permute-start.13 = (f32[256,256]{1,0:T(8,128)S(1)}, f32[256,256]{1,0:T(8,128)S(1)}, u32[]{:S(2)}, u32[]{:S(2)}) collective-permute-start(f32[256,256]{1,0:T(8,128)S(1)} %maximum_select_fusion.6), channel_id=1, source_target_pairs={{0,8},{8,0},{16,24},{24,16},{32,40},{40,32},{48,56},{56,48},{64,72... | collective-permute-start | bytes 786440 | tf_op jit(solution)/shard_map/ppermute | solution.py:33

commit v8 on v7

--- a/solution.py
+++ b/solution.py
@@ -100,6 +100,7 @@
         [jnp.broadcast_to(rot_in_chunk[None], (factor_count, chunk, rank_in)), out_blocks], axis=2
     ).reshape(factor_count * chunk, rank_in + rank_slice)
     received = lax.all_to_all(sending, "factor", 0, 0, tiled=True)
+    received, query_grad = lax.optimization_barrier((received, query_grad))
     rot_in = received[:, :rank_in]
     rot_out_rows = received[:, rank_in:]
 

time: 176 us -> 189 us (1.074)
  waiting for transfers between devices: 74.3 us -> 85.5 us
    ppermute x10, waiting for transfers between devices: 22 us -> 56.5 us  [butterfly_gather(): other = lax.ppermute(block, axis, [(i, i ^ step) for i in range(size)])]
    all_to_all x1, waiting for transfers between devices: 27.9 us -> 0.01 us  [per_device(): gathered_parts = lax.all_to_all(stacked_parts, 'factor', 0, 0, tiled=True)]
    all_to_all x1, waiting for transfers between devices: 15 us -> 19.5 us  [per_device(): received = lax.all_to_all(sending, 'factor', 0, 0, tiled=True)]
    ppermute x1, starting transfers between devices: 6.45 us -> 2.94 us  [from_behind(): return lax.ppermute(block, axis, route)]
    all_to_all x1, starting transfers between devices: 4.5 us -> 7.77 us  [per_device(): received = lax.all_to_all(sending, 'factor', 0, 0, tiled=True)]
  transfers between devices with their start and end apart: 16 -> 16, of which waited for: 14 -> 13; matrix products, arithmetic and copies ran while one was open for 13% -> 12% of each run, Pallas kernels for 0% -> 0%
where the time goes in v8:
time: 189 us; the launch traced here: 188 us
  waiting for transfers between devices  85.5 us (45%)
  starting transfers between devices  51.9 us (27%)
  matrix products  30.1 us (16%)
  other arithmetic  10.6 us (6%)
  local copies, waits for them, and re-layouts  8.43 us (4%)
    ppermute x10, waiting for transfers between devices, butterfly_gather(): other = lax.ppermute(block, axis, [(i, i ^ step) for i in range(size)])  56.5 us
    ppermute x10, starting transfers between devices, butterfly_gather(): other = lax.ppermute(block, axis, [(i, i ^ step) for i in range(size)])  31.4 us
    all_to_all x1, waiting for transfers between devices, per_device(): received = lax.all_to_all(sending, 'factor', 0, 0, tiled=True)  19.5 us
    ppermute x3, waiting for transfers between devices, butterfly_sum(): lax.ppermute(block, axis, [(i, i ^ step) for i in range(size)])  9.52 us
    dot_general x1, matrix products, per_device(): outer = jnp.einsum('qti,qtj->qij', q_out, q_in, precision=highest)  8.69 us
    all_to_all x1, starting transfers between devices, per_device(): received = lax.all_to_all(sending, 'factor', 0, 0, tiled=True)  7.77 us
    all_to_all x1, starting transfers between devices, per_device(): gathered_parts = lax.all_to_all(stacked_parts, 'factor', 0, 0, tiled=True)  7.6 us
    dot_general x1, matrix products, per_device(): lax.dot_general(grad_low, query_grad, (((1, 2), (1, 2)), ((), ())), prefe...  6.64 us
  transfers between devices with their start and end apart: 16, of which 13 were waited for; matrix products, arithmetic and copies ran while one was open for 12% of the time, Pallas kernels for 0%

profile of v8, /device:TPU:1, one launch (start us, length us, event | category | flops | bytes accessed | tf_op | source)
XLA Modules:
  0.0 188.3 jit_solution(3269436008314106164)
XLA Ops:
  0.0 1.6 copy-done
  1.6 1.7 fusion.39
  3.3 5.2 %fusion.38 = f32[2048,256]{0,1:T(8,128)S(1)} fusion(bf16[2048,1792]{1,0:T(8,128)(2,1)} %param.16, bf16[1792,256]{1,0:T(8,128)(2,1)S(1)} %copy-done.11), kind=kOutput, calls=%fused_computation.69 | convolution fusion | flops 1879048192 | bytes 10354688 | tf_op jit(solution)/shard_map/dot_general | solution.py:82
  8.8 2.3 %copy.95 = f32[64,8,8,256]{3,2,0,1:T(8,128)} copy(f32[64,8,8,256]{3,2,1,0:T(8,128)S(1)} %bitcast.53) | data formatting | bytes 8388608 | tf_op jit(solution)/shard_map/all_to_all | solution.py:85
  11.1 7.6 %all-to-all-start = ((f32[8,256,512]{1,2,0:T(8,128)}), f32[8,256,512]{1,2,0:T(8,128)}, u32[]{:S(2)}, u32[]{:S(2)}) async-start(f32[8,256,512]{1,2,0:T(8,128)} %bitcast.52), calls=%async_computation | async-start | bytes 8388608 | tf_op jit(solution)/shard_map/all_to_all | solution.py:85
  18.8 7.0 %collective-permute-start = (bf16[8,8,512]{2,1,0:T(8,128)(2,1)S(1)}, bf16[8,8,512]{2,1,0:T(8,128)(2,1)S(1)}, u32[]{:S(2)}, u32[]{:S(2)}) collective-permute-start(bf16[8,8,512]{2,1,0:T(8,128)(2,1)S(1)} %constant_dynamic-update-slice_fusion), channel_id=1, source_target_pairs={{0,128},{8,136},{16,144},{24,152},{32,160},{40,168},{48,176},{56,1... | collective-permute-start | bytes 196616 | tf_op jit(solution)/shard_map/ppermute | solution.py:33
  25.8 1.7 collective-permute-done
  27.5 1.5 collective-permute-start.1
  29.0 5.7 %collective-permute-done.1 = bf16[16,8,512]{2,1,0:T(8,128)(2,1)S(1)} collective-permute-done((bf16[16,8,512]{2,1,0:T(8,128)(2,1)S(1)}, bf16[16,8,512]{2,1,0:T(8,128)(2,1)S(1)}, u32[]{:S(2)}, u32[]{:S(2)}) %collective-permute-start.1) | collective-permute-done | bytes 131104 | tf_op jit(solution)/shard_map/ppermute | solution.py:33
  34.9 5.6 %collective-permute-done.2 = bf16[32,8,512]{2,1,0:T(8,128)(2,1)S(1)} collective-permute-done((bf16[32,8,512]{2,1,0:T(8,128)(2,1)S(1)}, bf16[32,8,512]{2,1,0:T(8,128)(2,1)S(1)}, u32[]{:S(2)}, u32[]{:S(2)}) %collective-permute-start.2) | collective-permute-done | bytes 262176 | tf_op jit(solution)/shard_map/ppermute | solution.py:33
  41.4 34.5 %collective-permute-done.3 = bf16[64,8,512]{2,1,0:T(8,128)(2,1)} collective-permute-done((bf16[64,8,512]{2,1,0:T(8,128)(2,1)S(1)}, bf16[64,8,512]{2,1,0:T(8,128)(2,1)}, u32[]{:S(2)}, u32[]{:S(2)}) %collective-permute-start.3) | collective-permute-done | bytes 524320 | tf_op jit(solution)/shard_map/ppermute | solution.py:33
  75.8 1.8 maximum_select_fusion.1
  77.6 1.6 collective-permute-start.4
  79.3 3.3 %reduce_sum.28 = f32[256,512]{0,1:T(8,128)} reduce(f32[8,256,512]{1,2,0:T(8,128)} %all-to-all-done, f32[]{:T(128)} %constant.175.clone.1), dimensions={0}, to_apply=%region_1.2 | reduce | flops 917504 | bytes 4718596 | tf_op jit(solution)/shard_map/reduce_sum | solution.py:95
  85.3 1.6 pad_maximum_fusion.1
  87.0 7.8 %all-to-all-start.1 = ((f32[8,256,288]{1,2,0:T(8,128)}), f32[8,256,288]{1,2,0:T(8,128)}, u32[]{:S(2)}, u32[]{:S(2)}) async-start(f32[8,256,288]{1,2,0:T(8,128)} %pad_maximum_fusion.1), calls=%async_computation.1 | async-start | bytes 4718592 | tf_op jit(solution)/shard_map/all_to_all | solution.py:102
  94.9 1.9 maximum_select_fusion
  97.7 8.7 %multiply_convert_fusion = bf16[256,32,256]{2,1,0:T(8,128)(2,1)} fusion(f32[32,256]{1,0:T(8,128)S(1)} %add_divide_fusion, f32[256,8,32]{2,1,0:T(8,128)S(1)} %fusion.6, f32[256,8,256]{2,1,0:T(8,128)S(1)} %fusion.4), kind=kOutput, calls=%fused_computation | convolution fusion | flops 205520896 | bytes 6586368 | tf_op jit(solution)/shard_map/qti,qtj->qij/dot_general | solution.py:93
  106.4 19.5 %all-to-all-done.1 = f32[8,256,288]{1,2,0:T(8,128)} async-done(((f32[8,256,288]{1,2,0:T(8,128)}), f32[8,256,288]{1,2,0:T(8,128)}, u32[]{:S(2)}, u32[]{:S(2)}) %all-to-all-start.1) | async-done | bytes 2359328 | tf_op jit(solution)/shard_map/all_to_all | solution.py:102
  125.9 1.9 %copy.90 = f32[8,36,8,256]{3,2,0,1:T(8,128)S(1)} copy(f32[8,36,8,256]{3,2,1,0:T(8,128)} %bitcast.28) | data formatting | bytes 4718592 | tf_op jit(solution)/shard_map/all_to_all | solution.py:102
  128.4 3.5 %fusion.2 = f32[512,256]{1,0:T(8,128)S(1)} fusion(f32[2048,512]{0,1:T(8,128)S(1)} %bitcast.54, f32[2048,288]{0,1:T(8,128)S(1)} %bitcast.56), kind=kOutput, calls=%fused_computation.7 | convolution fusion | flops 3221225472 | bytes 6815744 | tf_op jit(solution)/shard_map/dot_general | solution.py:117
  131.9 2.9 %collective-permute-start.5 = (f32[32,256]{1,0:T(8,128)S(1)}, f32[32,256]{1,0:T(8,128)S(1)}, u32[]{:S(2)}, u32[]{:S(2)}) collective-permute-start(f32[32,256]{1,0:T(8,128)S(1)} %slice.89), channel_id=1, source_target_pairs={{0,8},{8,16},{16,24},{24,32},{32,40},{40,48},{48,56},{56,64},{64,7... | collective-permute-start | bytes 98312 | tf_op jit(solution)/shard_map/ppermute | solution.py:16
  138.1 6.6 %fusion = f32[256,16,1]{1,0,2:T(8,128)S(1)} fusion(bf16[256,32,256]{2,1,0:T(8,128)(2,1)} %multiply_convert_fusion, f32[16,32,256]{2,0,1:T(8,128)S(1)} %scatter-mul.4), kind=kOutput, calls=%fused_computation.3 | convolution fusion | flops 67239936 | bytes 4734976 | tf_op jit(solution)/shard_map/dot_general | solution.py:131
  146.0 3.6 %collective-permute-done.6 = f32[16,257]{1,0:T(8,128)S(1)} collective-permute-done((f32[16,257]{1,0:T(8,128)S(1)}, f32[16,257]{1,0:T(8,128)S(1)}, u32[]{:S(2)}, u32[]{:S(2)}) %collective-permute-start.6) | collective-permute-done | bytes 16480 | tf_op jit(solution)/shard_map/ppermute | solution.py:23
  149.6 2.7 %collective-permute-done.7 = f32[16,257]{1,0:T(8,128)S(1)} collective-permute-done((f32[16,257]{1,0:T(8,128)S(1)}, f32[16,257]{1,0:T(8,128)S(1)}, u32[]{:S(2)}, u32[]{:S(2)}) %collective-permute-start.7) | collective-permute-done | bytes 16480 | tf_op jit(solution)/shard_map/ppermute | solution.py:23
  153.2 3.3 %collective-permute-done.8 = f32[16,257]{1,0:T(8,128)S(1)} collective-permute-done((f32[16,257]{1,0:T(8,128)S(1)}, f32[16,257]{1,0:T(8,128)S(1)}, u32[]{:S(2)}, u32[]{:S(2)}) %collective-permute-start.8) | collective-permute-done | bytes 16480 | tf_op jit(solution)/shard_map/ppermute | solution.py:23
  156.7 6.7 %collective-permute-start.9 = (f32[16,256]{1,0:T(8,128)S(1)}, f32[16,256]{1,0:T(8,128)S(1)}, u32[]{:S(2)}, u32[]{:S(2)}) collective-permute-start(f32[16,256]{1,0:T(8,128)S(1)} %slice_divide_fusion), channel_id=1, source_target_pairs={{0,128},{8,136},{16,144},{24,152},{32,160},{40,168},{48,176},{56,1... | collective-permute-start | bytes 49160 | tf_op jit(solution)/shard_map/ppermute | solution.py:33
  165.8 2.4 %collective-permute-done.10 = f32[32,256]{1,0:T(8,128)S(1)} collective-permute-done((f32[32,256]{1,0:T(8,128)S(1)}, f32[32,256]{1,0:T(8,128)S(1)}, u32[]{:S(2)}, u32[]{:S(2)}) %collective-permute-start.10) | collective-permute-done | bytes 32800 | tf_op jit(solution)/shard_map/ppermute | solution.py:33
  168.9 2.7 %collective-permute-done.11 = f32[64,256]{1,0:T(8,128)S(1)} collective-permute-done((f32[64,256]{1,0:T(8,128)S(1)}, f32[64,256]{1,0:T(8,128)S(1)}, u32[]{:S(2)}, u32[]{:S(2)}) %collective-permute-start.11) | collective-permute-done | bytes 65568 | tf_op jit(solution)/shard_map/ppermute | solution.py:33
  171.6 3.0 %collective-permute-start.12 = (f32[128,256]{1,0:T(8,128)S(1)}, f32[128,256]{1,0:T(8,128)S(1)}, u32[]{:S(2)}, u32[]{:S(2)}) collective-permute-start(f32[128,256]{1,0:T(8,128)S(1)} %maximum_select_fusion.8), channel_id=1, source_target_pairs={{0,16},{8,24},{16,0},{24,8},{32,48},{40,56},{48,32},{56,40},{64,80... | collective-permute-start | bytes 393224 | tf_op jit(solution)/shard_map/ppermute | solution.py:33
  174.6 2.4 %collective-permute-done.12 = f32[128,256]{1,0:T(8,128)S(1)} collective-permute-done((f32[128,256]{1,0:T(8,128)S(1)}, f32[128,256]{1,0:T(8,128)S(1)}, u32[]{:S(2)}, u32[]{:S(2)}) %collective-permute-start.12) | collective-permute-done | bytes 131104 | tf_op jit(solution)/shard_map/ppermute | solution.py:33
  177.0 9.1 %collective-permute-start.13 = (f32[256,256]{1,0:T(8,128)S(1)}, f32[256,256]{1,0:T(8,128)S(1)}, u32[]{:S(2)}, u32[]{:S(2)}) collective-permute-start(f32[256,256]{1,0:T(8,128)S(1)} %maximum_select_fusion.6), channel_id=1, source_target_pairs={{0,8},{8,0},{16,24},{24,16},{32,40},{40,32},{48,56},{56,48},{64,72... | collective-permute-start | bytes 786440 | tf_op jit(solution)/shard_map/ppermute | solution.py:33
  (85 shorter events, 15.2 us)
Async XLA Ops:
  0.0 1.6 copy-start
  0.0 3.3 %copy-start.11 = (bf16[1792,256]{1,0:T(8,128)(2,1)S(1)}, bf16[1792,256]{1,0:T(8,128)(2,1)}, u32[]{:S(2)}) copy-start(bf16[1792,256]{1,0:T(8,128)(2,1)} %param.18) | copy-start | bytes 2752516
  11.1 7.6 %copy-start.5 = (bf16[8,8,256]{2,1,0:T(8,128)(2,1)S(1)}, bf16[8,8,256]{2,1,0:T(8,128)(2,1)}, u32[]{:S(2)}) copy-start(bf16[8,8,256]{2,1,0:T(8,128)(2,1)} %param.23) | copy-start | bytes 98308
  11.1 7.6 %copy-start.6 = (bf16[8,8,256]{2,1,0:T(8,128)(2,1)S(1)}, bf16[8,8,256]{2,1,0:T(8,128)(2,1)}, u32[]{:S(2)}) copy-start(bf16[8,8,256]{2,1,0:T(8,128)(2,1)} %param.24) | copy-start | bytes 98308
  11.1 29.8 %copy-start.10 = (s32[1,16]{1,0:T(1,128)S(1)}, s32[1,16]{1,0:T(1,128)}, u32[]{:S(2)}) copy-start(s32[1,16]{1,0:T(1,128)} %param.25) | copy-start | bytes 196
  11.1 68.1 %all-to-all-start = ((f32[8,256,512]{1,2,0:T(8,128)}), f32[8,256,512]{1,2,0:T(8,128)}, u32[]{:S(2)}, u32[]{:S(2)}) async-start(f32[8,256,512]{1,2,0:T(8,128)} %bitcast.52), calls=%async_computation | async-start | bytes 8388608 | tf_op jit(solution)/shard_map/all_to_all | solution.py:85
  18.8 8.7 %collective-permute-start = (bf16[8,8,512]{2,1,0:T(8,128)(2,1)S(1)}, bf16[8,8,512]{2,1,0:T(8,128)(2,1)S(1)}, u32[]{:S(2)}, u32[]{:S(2)}) collective-permute-start(bf16[8,8,512]{2,1,0:T(8,128)(2,1)S(1)} %constant_dynamic-update-slice_fusion), channel_id=1, source_target_pairs={{0,128},{8,136},{16,144},{24,152},{32,160},{40,168},{48,176},{56,1... | collective-permute-start | bytes 196616 | tf_op jit(solution)/shard_map/ppermute | solution.py:33
  27.5 7.2 %collective-permute-start.1 = (bf16[16,8,512]{2,1,0:T(8,128)(2,1)S(1)}, bf16[16,8,512]{2,1,0:T(8,128)(2,1)S(1)}, u32[]{:S(2)}, u32[]{:S(2)}) collective-permute-start(bf16[16,8,512]{2,1,0:T(8,128)(2,1)S(1)} %maximum_select_fusion.7), channel_id=1, source_target_pairs={{0,64},{8,72},{16,80},{24,88},{32,96},{40,104},{48,112},{56,120},{... | collective-permute-start | bytes 393224 | tf_op jit(solution)/shard_map/ppermute | solution.py:33
  34.7 5.7 %collective-permute-start.2 = (bf16[32,8,512]{2,1,0:T(8,128)(2,1)S(1)}, bf16[32,8,512]{2,1,0:T(8,128)(2,1)S(1)}, u32[]{:S(2)}, u32[]{:S(2)}) collective-permute-start(bf16[32,8,512]{2,1,0:T(8,128)(2,1)S(1)} %maximum_select_fusion.5), channel_id=1, source_target_pairs={{0,32},{8,40},{16,48},{24,56},{32,0},{40,8},{48,16},{56,24},{64,96... | collective-permute-start | bytes 786440 | tf_op jit(solution)/shard_map/ppermute | solution.py:33
  40.5 0.8 copy-start.1
  40.5 35.3 %collective-permute-start.3 = (bf16[64,8,512]{2,1,0:T(8,128)(2,1)S(1)}, bf16[64,8,512]{2,1,0:T(8,128)(2,1)}, u32[]{:S(2)}, u32[]{:S(2)}) collective-permute-start(bf16[64,8,512]{2,1,0:T(8,128)(2,1)S(1)} %maximum_select_fusion.2), channel_id=1, source_target_pairs={{0,16},{8,24},{16,0},{24,8},{32,48},{40,56},{48,32},{56,40},{64,80... | collective-permute-start | bytes 1572872 | tf_op jit(solution)/shard_map/ppermute | solution.py:33
  77.6 5.0 %copy-start.3 = (bf16[256,256]{1,0:T(8,128)(2,1)S(1)}, bf16[256,256]{1,0:T(8,128)(2,1)}, u32[]{:S(2)}) copy-start(bf16[256,256]{1,0:T(8,128)(2,1)} %param.21) | copy-start | bytes 393220
  77.6 6.2 %copy-start.2 = (bf16[256,256]{1,0:T(8,128)(2,1)S(1)}, bf16[256,256]{1,0:T(8,128)(2,1)}, u32[]{:S(2)}) copy-start(bf16[256,256]{1,0:T(8,128)(2,1)} %param.20) | copy-start | bytes 393220
  77.6 17.2 %collective-permute-start.4 = (bf16[128,8,512]{2,1,0:T(8,128)(2,1)S(1)}, bf16[128,8,512]{2,1,0:T(8,128)(2,1)}, u32[]{:S(2)}, u32[]{:S(2)}) collective-permute-start(bf16[128,8,512]{2,1,0:T(8,128)(2,1)S(1)} %maximum_select_fusion.1), channel_id=1, source_target_pairs={{0,8},{8,0},{16,24},{24,16},{32,40},{40,32},{48,56},{56,48},{64,72... | collective-permute-start | bytes 3145736 | tf_op jit(solution)/shard_map/ppermute | solution.py:33
  87.0 7.8 %copy-start.7 = (f32[32,256]{1,0:T(8,128)S(1)}, f32[32,256]{1,0:T(8,128)}, u32[]{:S(2)}) copy-start(f32[32,256]{1,0:T(8,128)} %param.22) | copy-start | bytes 98308
  87.0 38.9 %all-to-all-start.1 = ((f32[8,256,288]{1,2,0:T(8,128)}), f32[8,256,288]{1,2,0:T(8,128)}, u32[]{:S(2)}, u32[]{:S(2)}) async-start(f32[8,256,288]{1,2,0:T(8,128)} %pad_maximum_fusion.1), calls=%async_computation.1 | async-start | bytes 4718592 | tf_op jit(solution)/shard_map/all_to_all | solution.py:102
  94.7 2.0 %copy-start.4 = (bf16[256,256]{1,0:T(8,128)(2,1)S(1)}, bf16[256,256]{1,0:T(8,128)(2,1)}, u32[]{:S(2)}) copy-start(bf16[256,256]{1,0:T(8,128)(2,1)} %param.21) | copy-start | bytes 393220
  128.4 6.5 %copy-start.9 = (s32[32]{0:T(128)S(1)}, s32[32]{0:T(128)}, u32[]{:S(2)}) copy-start(s32[32]{0:T(128)} %param.26) | copy-start | bytes 388
  131.9 5.3 %collective-permute-start.5 = (f32[32,256]{1,0:T(8,128)S(1)}, f32[32,256]{1,0:T(8,128)S(1)}, u32[]{:S(2)}, u32[]{:S(2)}) collective-permute-start(f32[32,256]{1,0:T(8,128)S(1)} %slice.89), channel_id=1, source_target_pairs={{0,8},{8,16},{16,24},{24,32},{32,40},{40,48},{48,56},{56,64},{64,7... | collective-permute-start | bytes 98312 | tf_op jit(solution)/shard_map/ppermute | solution.py:16
  138.1 48.1 %copy-start.8 = (s32[512,1]{0,1:T(1,128)S(1)}, s32[512,1]{0,1:T(1,128)}, u32[]{:S(2)}) copy-start(s32[512,1]{0,1:T(1,128)} %param.27) | copy-start | bytes 6148
  144.8 4.8 %collective-permute-start.6 = (f32[16,257]{1,0:T(8,128)S(1)}, f32[16,257]{1,0:T(8,128)S(1)}, u32[]{:S(2)}, u32[]{:S(2)}) collective-permute-start(f32[16,257]{1,0:T(8,128)S(1)} %pad_maximum_fusion.2), channel_id=1, source_target_pairs={{0,1},{1,0},{2,3},{3,2},{4,5},{5,4},{6,7},{7,6},{8,9},{9,8},{10,11... | collective-permute-start | bytes 49352 | tf_op jit(solution)/shard_map/ppermute | solution.py:23
  149.6 2.7 %collective-permute-start.7 = (f32[16,257]{1,0:T(8,128)S(1)}, f32[16,257]{1,0:T(8,128)S(1)}, u32[]{:S(2)}, u32[]{:S(2)}) collective-permute-start(f32[16,257]{1,0:T(8,128)S(1)} %fusion.36), channel_id=1, source_target_pairs={{0,2},{1,3},{2,0},{3,1},{4,6},{5,7},{6,4},{7,5},{8,10},{9,11},{10,... | collective-permute-start | bytes 49352 | tf_op jit(solution)/shard_map/ppermute | solution.py:23
  152.3 4.2 %collective-permute-start.8 = (f32[16,257]{1,0:T(8,128)S(1)}, f32[16,257]{1,0:T(8,128)S(1)}, u32[]{:S(2)}, u32[]{:S(2)}) collective-permute-start(f32[16,257]{1,0:T(8,128)S(1)} %add.76), channel_id=1, source_target_pairs={{0,4},{1,5},{2,6},{3,7},{4,0},{5,1},{6,2},{7,3},{8,12},{9,13},{10,... | collective-permute-start | bytes 49352 | tf_op jit(solution)/shard_map/ppermute | solution.py:23
  156.7 7.8 %collective-permute-start.9 = (f32[16,256]{1,0:T(8,128)S(1)}, f32[16,256]{1,0:T(8,128)S(1)}, u32[]{:S(2)}, u32[]{:S(2)}) collective-permute-start(f32[16,256]{1,0:T(8,128)S(1)} %slice_divide_fusion), channel_id=1, source_target_pairs={{0,128},{8,136},{16,144},{24,152},{32,160},{40,168},{48,176},{56,1... | collective-permute-start | bytes 49160 | tf_op jit(solution)/shard_map/ppermute | solution.py:33
  164.5 3.7 %collective-permute-start.10 = (f32[32,256]{1,0:T(8,128)S(1)}, f32[32,256]{1,0:T(8,128)S(1)}, u32[]{:S(2)}, u32[]{:S(2)}) collective-permute-start(f32[32,256]{1,0:T(8,128)S(1)} %maximum_select_fusion.10), channel_id=1, source_target_pairs={{0,64},{8,72},{16,80},{24,88},{32,96},{40,104},{48,112},{56,120},{... | collective-permute-start | bytes 98312 | tf_op jit(solution)/shard_map/ppermute | solution.py:33
  168.2 3.4 %collective-permute-start.11 = (f32[64,256]{1,0:T(8,128)S(1)}, f32[64,256]{1,0:T(8,128)S(1)}, u32[]{:S(2)}, u32[]{:S(2)}) collective-permute-start(f32[64,256]{1,0:T(8,128)S(1)} %maximum_select_fusion.9), channel_id=1, source_target_pairs={{0,32},{8,40},{16,48},{24,56},{32,0},{40,8},{48,16},{56,24},{64,96... | collective-permute-start | bytes 196616 | tf_op jit(solution)/shard_map/ppermute | solution.py:33
  171.6 5.4 %collective-permute-start.12 = (f32[128,256]{1,0:T(8,128)S(1)}, f32[128,256]{1,0:T(8,128)S(1)}, u32[]{:S(2)}, u32[]{:S(2)}) collective-permute-start(f32[128,256]{1,0:T(8,128)S(1)} %maximum_select_fusion.8), channel_id=1, source_target_pairs={{0,16},{8,24},{16,0},{24,8},{32,48},{40,56},{48,32},{56,40},{64,80... | collective-permute-start | bytes 393224 | tf_op jit(solution)/shard_map/ppermute | solution.py:33
  177.0 10.3 %collective-permute-start.13 = (f32[256,256]{1,0:T(8,128)S(1)}, f32[256,256]{1,0:T(8,128)S(1)}, u32[]{:S(2)}, u32[]{:S(2)}) collective-permute-start(f32[256,256]{1,0:T(8,128)S(1)} %maximum_select_fusion.6), channel_id=1, source_target_pairs={{0,8},{8,0},{16,24},{24,16},{32,40},{40,32},{48,56},{56,48},{64,72... | collective-permute-start | bytes 786440 | tf_op jit(solution)/shard_map/ppermute | solution.py:33

commit v9 on v7

--- a/solution.py
+++ b/solution.py
@@ -25,11 +25,11 @@
     return block
 
 
-def butterfly_gather(block, axis):
+def butterfly_gather(block, axis, bits):
     size = lax.axis_size(axis)
     me = lax.axis_index(axis)
-    step = size // 2
-    while step >= 1:
+    for bit in bits:
+        step = 1 << bit
         other = lax.ppermute(block, axis, [(i, i ^ step) for i in range(size)])
         upper = (me // step) % 2 == 1
         block = jnp.where(
@@ -37,15 +37,28 @@
             jnp.concatenate([other, block], axis=0),
             jnp.concatenate([block, other], axis=0),
         )
-        step //= 2
     return block
 
 
-def bit_reversed(rows, count):
-    bits = count.bit_length() - 1
-    shaped = rows.reshape((2,) * bits + (rows.shape[0] // count,) + rows.shape[1:])
-    twisted = tuple(range(bits - 1, -1, -1)) + tuple(range(bits, shaped.ndim))
-    return shaped.transpose(twisted).reshape(rows.shape)
+def arrival_axes(bits):
+    top = len(bits) - 1
+    return tuple(top - bit for bit in reversed(bits))
+
+
+def to_arrival(rows, bits):
+    count = 1 << len(bits)
+    shaped = rows.reshape((2,) * len(bits) + (rows.shape[0] // count,) + rows.shape[1:])
+    axes = arrival_axes(bits) + tuple(range(len(bits), shaped.ndim))
+    return shaped.transpose(axes).reshape(rows.shape)
+
+
+def from_arrival(rows, bits):
+    count = 1 << len(bits)
+    shaped = rows.reshape((2,) * len(bits) + (rows.shape[0] // count,) + rows.shape[1:])
+    forward = arrival_axes(bits)
+    back = tuple(forward.index(i) for i in range(len(bits)))
+    axes = back + tuple(range(len(bits), shaped.ndim))
+    return shaped.transpose(axes).reshape(rows.shape)
 
 
 def per_device(
@@ -74,7 +87,10 @@
     highest = lax.Precision.HIGHEST
     chunk = tokens_here // factor_count
     scale_block = 1.0 / (eigen_values + DAMPING)
-    queries = butterfly_gather(jnp.concatenate([query_in, query_out], axis=2), "dp")
+    data_bits = data_count.bit_length() - 1
+    query_bits = (1,) + tuple(range(data_bits - 1, 1, -1)) + (0,)
+    score_bits = tuple(range(data_bits - 1, -1, -1))
+    queries = butterfly_gather(jnp.concatenate([query_in, query_out], axis=2), "dp", query_bits)
 
 
     basis_in_wide = basis_in.astype(jnp.float32)
@@ -130,11 +146,11 @@
     part = lax.dot_general(
         grad_low, query_grad, (((1, 2), (1, 2)), ((), ())), preferred_element_type=jnp.float32
     )
-    part = bit_reversed(part.T, data_count).T
+    part = from_arrival(part.T, query_bits).T
 
     totals = butterfly_sum(jnp.concatenate([part, self_part[:, None]], axis=1), "factor")
     relative = totals[:, :-1] / jnp.sqrt(totals[:, -1:] + EPSILON)
-    relative_all = butterfly_gather(relative, "dp")
+    relative_all = butterfly_gather(relative, "dp", score_bits)
 
     own_all = owners[:, 0]
     doc_count = own_all.shape[0]
@@ -142,8 +158,8 @@
     earlier = (own_all[None, :] == own_all[:, None]) & (numbers[None, :] < numbers[:, None])
     rank_all = jnp.sum(earlier.astype(jnp.int32), axis=1)
     slots = jnp.arange(OWN_CAP, dtype=jnp.int32)[:, None]
-    own_arrived = bit_reversed(own_all, data_count)
-    rank_arrived = bit_reversed(rank_all, data_count)
+    own_arrived = to_arrival(own_all, score_bits)
+    rank_arrived = to_arrival(rank_all, score_bits)
     placing = ((own_arrived[None, :] == data_index) & (rank_arrived[None, :] == slots)).astype(
         jnp.float32
     )

time: 176 us -> 201 us (1.14)
  waiting for transfers between devices: 74.3 us -> 99.2 us
    ppermute x10, waiting for transfers between devices: 22 us -> 70.1 us  [butterfly_gather(): other = lax.ppermute(block, axis, [(i, i ^ step) for i in range(size)])]
    all_to_all x1, waiting for transfers between devices: 27.9 us -> 0.01 us  [per_device(): gathered_parts = lax.all_to_all(stacked_parts, 'factor', 0, 0, tiled=True)]
    all_to_all x1, waiting for transfers between devices: 15 us -> 19.7 us  [per_device(): received = lax.all_to_all(sending, 'factor', 0, 0, tiled=True)]
    all_to_all x1, starting transfers between devices: 4.5 us -> 7.92 us  [per_device(): received = lax.all_to_all(sending, 'factor', 0, 0, tiled=True)]
    ppermute x1, starting transfers between devices: 6.45 us -> 3.53 us  [from_behind(): return lax.ppermute(block, axis, route)]
  transfers between devices with their start and end apart: 16 -> 16, of which waited for: 14 -> 13; matrix products, arithmetic and copies ran while one was open for 13% -> 11% of each run, Pallas kernels for 0% -> 0%
where the time goes in v9:
time: 201 us; the launch traced here: 200 us
  waiting for transfers between devices  99.2 us (49%)
  starting transfers between devices  50.6 us (25%)
  matrix products  30.3 us (15%)
  other arithmetic  9.92 us (5%)
  local copies, waits for them, and re-layouts  8.2 us (4%)
    ppermute x10, waiting for transfers between devices, butterfly_gather(): other = lax.ppermute(block, axis, [(i, i ^ step) for i in range(size)])  70.1 us
    ppermute x10, starting transfers between devices, butterfly_gather(): other = lax.ppermute(block, axis, [(i, i ^ step) for i in range(size)])  29.4 us
    all_to_all x1, waiting for transfers between devices, per_device(): received = lax.all_to_all(sending, 'factor', 0, 0, tiled=True)  19.7 us
    ppermute x3, waiting for transfers between devices, butterfly_sum(): lax.ppermute(block, axis, [(i, i ^ step) for i in range(size)])  9.32 us
    dot_general x1, matrix products, per_device(): outer = jnp.einsum('qti,qtj->qij', q_out, q_in, precision=highest)  8.55 us
    all_to_all x1, starting transfers between devices, per_device(): received = lax.all_to_all(sending, 'factor', 0, 0, tiled=True)  7.92 us
    all_to_all x1, starting transfers between devices, per_device(): gathered_parts = lax.all_to_all(stacked_parts, 'factor', 0, 0, tiled=True)  7.6 us
    dot_general x1, matrix products, per_device(): lax.dot_general(grad_low, query_grad, (((1, 2), (1, 2)), ((), ())), prefe...  6.64 us
  transfers between devices with their start and end apart: 16, of which 13 were waited for; matrix products, arithmetic and copies ran while one was open for 11% of the time, Pallas kernels for 0%

profile of v9, /device:TPU:1, one launch (start us, length us, event | category | flops | bytes accessed | tf_op | source)
XLA Modules:
  0.0 199.8 jit_solution(17420155576973295664)
XLA Ops:
  0.0 1.6 copy-done
  1.6 1.7 fusion.39
  3.3 5.2 %fusion.38 = f32[2048,256]{0,1:T(8,128)S(1)} fusion(bf16[2048,1792]{1,0:T(8,128)(2,1)} %param.16, bf16[1792,256]{1,0:T(8,128)(2,1)S(1)} %copy-done.11), kind=kOutput, calls=%fused_computation.69 | convolution fusion | flops 1879048192 | bytes 10354688 | tf_op jit(solution)/shard_map/dot_general | solution.py:98
  8.8 2.3 %copy.93 = f32[64,8,8,256]{3,2,0,1:T(8,128)} copy(f32[64,8,8,256]{3,2,1,0:T(8,128)S(1)} %bitcast.53) | data formatting | bytes 8388608 | tf_op jit(solution)/shard_map/all_to_all | solution.py:101
  11.1 7.6 %all-to-all-start = ((f32[8,256,512]{1,2,0:T(8,128)}), f32[8,256,512]{1,2,0:T(8,128)}, u32[]{:S(2)}, u32[]{:S(2)}) async-start(f32[8,256,512]{1,2,0:T(8,128)} %bitcast.52), calls=%async_computation | async-start | bytes 8388608 | tf_op jit(solution)/shard_map/all_to_all | solution.py:101
  19.2 46.8 %collective-permute-done = bf16[8,8,512]{2,1,0:T(8,128)(2,1)S(1)} collective-permute-done((bf16[8,8,512]{2,1,0:T(8,128)(2,1)S(1)}, bf16[8,8,512]{2,1,0:T(8,128)(2,1)S(1)}, u32[]{:S(2)}, u32[]{:S(2)}) %collective-permute-start) | collective-permute-done | bytes 65568 | tf_op jit(solution)/shard_map/ppermute | solution.py:33
  66.0 7.0 %collective-permute-start.1 = (bf16[16,8,512]{2,1,0:T(8,128)(2,1)S(1)}, bf16[16,8,512]{2,1,0:T(8,128)(2,1)S(1)}, u32[]{:S(2)}, u32[]{:S(2)}) collective-permute-start(bf16[16,8,512]{2,1,0:T(8,128)(2,1)S(1)} %maximum_select_fusion.7), channel_id=1, source_target_pairs={{0,128},{8,136},{16,144},{24,152},{32,160},{40,168},{48,176},{56,1... | collective-permute-start | bytes 393224 | tf_op jit(solution)/shard_map/ppermute | solution.py:33
  73.0 2.5 %collective-permute-done.1 = bf16[16,8,512]{2,1,0:T(8,128)(2,1)S(1)} collective-permute-done((bf16[16,8,512]{2,1,0:T(8,128)(2,1)S(1)}, bf16[16,8,512]{2,1,0:T(8,128)(2,1)S(1)}, u32[]{:S(2)}, u32[]{:S(2)}) %collective-permute-start.1) | collective-permute-done | bytes 131104 | tf_op jit(solution)/shard_map/ppermute | solution.py:33
  75.5 5.2 %collective-permute-start.2 = (bf16[32,8,512]{2,1,0:T(8,128)(2,1)S(1)}, bf16[32,8,512]{2,1,0:T(8,128)(2,1)S(1)}, u32[]{:S(2)}, u32[]{:S(2)}) collective-permute-start(bf16[32,8,512]{2,1,0:T(8,128)(2,1)S(1)} %maximum_select_fusion.5), channel_id=1, source_target_pairs={{0,64},{8,72},{16,80},{24,88},{32,96},{40,104},{48,112},{56,120},{... | collective-permute-start | bytes 786440 | tf_op jit(solution)/shard_map/ppermute | solution.py:33
  80.7 10.6 %collective-permute-done.2 = bf16[32,8,512]{2,1,0:T(8,128)(2,1)S(1)} collective-permute-done((bf16[32,8,512]{2,1,0:T(8,128)(2,1)S(1)}, bf16[32,8,512]{2,1,0:T(8,128)(2,1)S(1)}, u32[]{:S(2)}, u32[]{:S(2)}) %collective-permute-start.2) | collective-permute-done | bytes 262176 | tf_op jit(solution)/shard_map/ppermute | solution.py:33
  91.5 2.7 %reduce_sum.28 = f32[256,512]{0,1:T(8,128)S(1)} reduce(f32[8,256,512]{1,2,0:T(8,128)} %all-to-all-done, f32[]{:T(128)} %constant.180.clone.1), dimensions={0}, to_apply=%region_2.3 | reduce | flops 917504 | bytes 4718596 | tf_op jit(solution)/shard_map/reduce_sum | solution.py:111
  95.1 1.6 pad_maximum_fusion.1
  96.6 7.9 %all-to-all-start.1 = ((f32[8,256,288]{1,2,0:T(8,128)}), f32[8,256,288]{1,2,0:T(8,128)}, u32[]{:S(2)}, u32[]{:S(2)}) async-start(f32[8,256,288]{1,2,0:T(8,128)} %pad_maximum_fusion.1), calls=%async_computation.1 | async-start | bytes 4718592 | tf_op jit(solution)/shard_map/all_to_all | solution.py:118
  104.6 1.8 maximum_select_fusion.1
  106.3 1.7 collective-permute-start.4
  110.4 1.9 maximum_select_fusion
  113.7 1.8 fusion.4
  115.5 19.7 %all-to-all-done.1 = f32[8,256,288]{1,2,0:T(8,128)} async-done(((f32[8,256,288]{1,2,0:T(8,128)}), f32[8,256,288]{1,2,0:T(8,128)}, u32[]{:S(2)}, u32[]{:S(2)}) %all-to-all-start.1) | async-done | bytes 2359328 | tf_op jit(solution)/shard_map/all_to_all | solution.py:118
  135.2 1.9 copy.88
  137.7 3.5 %fusion.2 = f32[512,256]{1,0:T(8,128)S(1)} fusion(f32[2048,512]{0,1:T(8,128)S(1)} %bitcast.54, f32[2048,288]{0,1:T(8,128)S(1)} %bitcast.56), kind=kOutput, calls=%fused_computation.6 | convolution fusion | flops 3221225472 | bytes 6815744 | tf_op jit(solution)/shard_map/dot_general | solution.py:132
  141.2 3.5 %collective-permute-start.5 = (f32[32,256]{1,0:T(8,128)S(1)}, f32[32,256]{1,0:T(8,128)S(1)}, u32[]{:S(2)}, u32[]{:S(2)}) collective-permute-start(f32[32,256]{1,0:T(8,128)S(1)} %slice.91), channel_id=1, source_target_pairs={{0,8},{8,16},{16,24},{24,32},{32,40},{40,48},{48,56},{56,64},{64,7... | collective-permute-start | bytes 98312 | tf_op jit(solution)/shard_map/ppermute | solution.py:16
  144.8 8.6 %multiply_convert_fusion = bf16[256,32,256]{2,1,0:T(8,128)(2,1)} fusion(f32[32,256]{1,0:T(8,128)S(1)} %add_divide_fusion, f32[256,8,32]{2,1,0:T(8,128)S(1)} %fusion.6, f32[256,8,256]{2,1,0:T(8,128)S(1)} %copy-done.1), kind=kOutput, calls=%fused_computation | convolution fusion | flops 205520896 | bytes 6586368 | tf_op jit(solution)/shard_map/qti,qtj->qij/dot_general | solution.py:109
  154.6 6.6 %fusion = f32[256,16,1]{1,0,2:T(8,128)S(1)} fusion(bf16[256,32,256]{2,1,0:T(8,128)(2,1)} %multiply_convert_fusion, f32[16,32,256]{2,0,1:T(8,128)S(1)} %scatter-mul.4), kind=kOutput, calls=%fused_computation.3 | convolution fusion | flops 67239936 | bytes 4734976 | tf_op jit(solution)/shard_map/dot_general | solution.py:146
  162.5 3.4 %collective-permute-done.6 = f32[16,257]{1,0:T(8,128)S(1)} collective-permute-done((f32[16,257]{1,0:T(8,128)S(1)}, f32[16,257]{1,0:T(8,128)S(1)}, u32[]{:S(2)}, u32[]{:S(2)}) %collective-permute-start.6) | collective-permute-done | bytes 16480 | tf_op jit(solution)/shard_map/ppermute | solution.py:23
  165.9 2.7 %collective-permute-done.7 = f32[16,257]{1,0:T(8,128)S(1)} collective-permute-done((f32[16,257]{1,0:T(8,128)S(1)}, f32[16,257]{1,0:T(8,128)S(1)}, u32[]{:S(2)}, u32[]{:S(2)}) %collective-permute-start.7) | collective-permute-done | bytes 16480 | tf_op jit(solution)/shard_map/ppermute | solution.py:23
  169.5 3.3 %collective-permute-done.8 = f32[16,257]{1,0:T(8,128)S(1)} collective-permute-done((f32[16,257]{1,0:T(8,128)S(1)}, f32[16,257]{1,0:T(8,128)S(1)}, u32[]{:S(2)}, u32[]{:S(2)}) %collective-permute-start.8) | collective-permute-done | bytes 16480 | tf_op jit(solution)/shard_map/ppermute | solution.py:23
  173.0 5.0 %collective-permute-start.9 = (f32[16,256]{1,0:T(8,128)S(1)}, f32[16,256]{1,0:T(8,128)S(1)}, u32[]{:S(2)}, u32[]{:S(2)}) collective-permute-start(f32[16,256]{1,0:T(8,128)S(1)} %slice_divide_fusion), channel_id=1, source_target_pairs={{0,128},{8,136},{16,144},{24,152},{32,160},{40,168},{48,176},{56,1... | collective-permute-start | bytes 49160 | tf_op jit(solution)/shard_map/ppermute | solution.py:33
  179.5 3.7 %collective-permute-done.10 = f32[32,256]{1,0:T(8,128)S(1)} collective-permute-done((f32[32,256]{1,0:T(8,128)S(1)}, f32[32,256]{1,0:T(8,128)S(1)}, u32[]{:S(2)}, u32[]{:S(2)}) %collective-permute-start.10) | collective-permute-done | bytes 32800 | tf_op jit(solution)/shard_map/ppermute | solution.py:33
  184.5 1.9 collective-permute-done.11
  186.4 2.4 %collective-permute-start.12 = (f32[128,256]{1,0:T(8,128)S(1)}, f32[128,256]{1,0:T(8,128)S(1)}, u32[]{:S(2)}, u32[]{:S(2)}) collective-permute-start(f32[128,256]{1,0:T(8,128)S(1)} %maximum_select_fusion.8), channel_id=1, source_target_pairs={{0,16},{8,24},{16,0},{24,8},{32,48},{40,56},{48,32},{56,40},{64,80... | collective-permute-start | bytes 393224 | tf_op jit(solution)/shard_map/ppermute | solution.py:33
  188.8 2.7 %collective-permute-done.12 = f32[128,256]{1,0:T(8,128)S(1)} collective-permute-done((f32[128,256]{1,0:T(8,128)S(1)}, f32[128,256]{1,0:T(8,128)S(1)}, u32[]{:S(2)}, u32[]{:S(2)}) %collective-permute-start.12) | collective-permute-done | bytes 131104 | tf_op jit(solution)/shard_map/ppermute | solution.py:33
  191.5 6.2 %collective-permute-start.13 = (f32[256,256]{1,0:T(8,128)S(1)}, f32[256,256]{1,0:T(8,128)S(1)}, u32[]{:S(2)}, u32[]{:S(2)}) collective-permute-start(f32[256,256]{1,0:T(8,128)S(1)} %maximum_select_fusion.6), channel_id=1, source_target_pairs={{0,8},{8,0},{16,24},{24,16},{32,40},{40,32},{48,56},{56,48},{64,72... | collective-permute-start | bytes 786440 | tf_op jit(solution)/shard_map/ppermute | solution.py:33
  (85 shorter events, 13.2 us)
Async XLA Ops:
  0.0 1.6 copy-start
  0.0 3.3 %copy-start.11 = (bf16[1792,256]{1,0:T(8,128)(2,1)S(1)}, bf16[1792,256]{1,0:T(8,128)(2,1)}, u32[]{:S(2)}) copy-start(bf16[1792,256]{1,0:T(8,128)(2,1)} %param.18) | copy-start | bytes 2752516
  11.1 7.6 %copy-start.5 = (bf16[8,8,256]{2,1,0:T(8,128)(2,1)S(1)}, bf16[8,8,256]{2,1,0:T(8,128)(2,1)}, u32[]{:S(2)}) copy-start(bf16[8,8,256]{2,1,0:T(8,128)(2,1)} %param.23) | copy-start | bytes 98308
  11.1 7.6 %copy-start.6 = (bf16[8,8,256]{2,1,0:T(8,128)(2,1)S(1)}, bf16[8,8,256]{2,1,0:T(8,128)(2,1)}, u32[]{:S(2)}) copy-start(bf16[8,8,256]{2,1,0:T(8,128)(2,1)} %param.24) | copy-start | bytes 98308
  11.1 80.4 %all-to-all-start = ((f32[8,256,512]{1,2,0:T(8,128)}), f32[8,256,512]{1,2,0:T(8,128)}, u32[]{:S(2)}, u32[]{:S(2)}) async-start(f32[8,256,512]{1,2,0:T(8,128)} %bitcast.52), calls=%async_computation | async-start | bytes 8388608 | tf_op jit(solution)/shard_map/all_to_all | solution.py:101
  18.8 47.2 %collective-permute-start = (bf16[8,8,512]{2,1,0:T(8,128)(2,1)S(1)}, bf16[8,8,512]{2,1,0:T(8,128)(2,1)S(1)}, u32[]{:S(2)}, u32[]{:S(2)}) collective-permute-start(bf16[8,8,512]{2,1,0:T(8,128)(2,1)S(1)} %constant_dynamic-update-slice_fusion), channel_id=1, source_target_pairs={{0,16},{8,24},{16,0},{24,8},{32,48},{40,56},{48,32},{56,40},{64,80... | collective-permute-start | bytes 196616 | tf_op jit(solution)/shard_map/ppermute | solution.py:33
  66.0 9.5 %collective-permute-start.1 = (bf16[16,8,512]{2,1,0:T(8,128)(2,1)S(1)}, bf16[16,8,512]{2,1,0:T(8,128)(2,1)S(1)}, u32[]{:S(2)}, u32[]{:S(2)}) collective-permute-start(bf16[16,8,512]{2,1,0:T(8,128)(2,1)S(1)} %maximum_select_fusion.7), channel_id=1, source_target_pairs={{0,128},{8,136},{16,144},{24,152},{32,160},{40,168},{48,176},{56,1... | collective-permute-start | bytes 393224 | tf_op jit(solution)/shard_map/ppermute | solution.py:33
  75.5 15.8 %collective-permute-start.2 = (bf16[32,8,512]{2,1,0:T(8,128)(2,1)S(1)}, bf16[32,8,512]{2,1,0:T(8,128)(2,1)S(1)}, u32[]{:S(2)}, u32[]{:S(2)}) collective-permute-start(bf16[32,8,512]{2,1,0:T(8,128)(2,1)S(1)} %maximum_select_fusion.5), channel_id=1, source_target_pairs={{0,64},{8,72},{16,80},{24,88},{32,96},{40,104},{48,112},{56,120},{... | collective-permute-start | bytes 786440 | tf_op jit(solution)/shard_map/ppermute | solution.py:33
  91.4 2.8 %copy-start.2 = (bf16[64,8,512]{2,1,0:T(8,128)(2,1)}, bf16[64,8,512]{2,1,0:T(8,128)(2,1)S(1)}, u32[]{:S(2)}) copy-start(bf16[64,8,512]{2,1,0:T(8,128)(2,1)S(1)} %maximum_select_fusion.2) | copy-start | bytes 1572868
  91.4 2.8 %copy-start.4 = (bf16[256,256]{1,0:T(8,128)(2,1)S(1)}, bf16[256,256]{1,0:T(8,128)(2,1)}, u32[]{:S(2)}) copy-start(bf16[256,256]{1,0:T(8,128)(2,1)} %param.21) | copy-start | bytes 393220
  91.4 3.1 %copy-start.3 = (bf16[256,256]{1,0:T(8,128)(2,1)S(1)}, bf16[256,256]{1,0:T(8,128)(2,1)}, u32[]{:S(2)}) copy-start(bf16[256,256]{1,0:T(8,128)(2,1)} %param.20) | copy-start | bytes 393220
  91.4 13.1 %collective-permute-start.3 = (bf16[64,8,512]{2,1,0:T(8,128)(2,1)S(1)}, bf16[64,8,512]{2,1,0:T(8,128)(2,1)}, u32[]{:S(2)}, u32[]{:S(2)}) collective-permute-start(bf16[64,8,512]{2,1,0:T(8,128)(2,1)S(1)} %maximum_select_fusion.2), channel_id=1, source_target_pairs={{0,32},{8,40},{16,48},{24,56},{32,0},{40,8},{48,16},{56,24},{64,96... | collective-permute-start | bytes 1572872 | tf_op jit(solution)/shard_map/ppermute | solution.py:33
  96.6 11.4 %copy-start.10 = (s32[1,16]{1,0:T(1,128)S(1)}, s32[1,16]{1,0:T(1,128)}, u32[]{:S(2)}) copy-start(s32[1,16]{1,0:T(1,128)} %param.25) | copy-start | bytes 196
  96.6 11.6 %copy-start.9 = (s32[32]{0:T(128)S(1)}, s32[32]{0:T(128)}, u32[]{:S(2)}) copy-start(s32[32]{0:T(128)} %param.26) | copy-start | bytes 388
  96.6 13.6 %copy-start.7 = (f32[32,256]{1,0:T(8,128)S(1)}, f32[32,256]{1,0:T(8,128)}, u32[]{:S(2)}) copy-start(f32[32,256]{1,0:T(8,128)} %param.22) | copy-start | bytes 98308
  96.6 38.6 %all-to-all-start.1 = ((f32[8,256,288]{1,2,0:T(8,128)}), f32[8,256,288]{1,2,0:T(8,128)}, u32[]{:S(2)}, u32[]{:S(2)}) async-start(f32[8,256,288]{1,2,0:T(8,128)} %pad_maximum_fusion.1), calls=%async_computation.1 | async-start | bytes 4718592 | tf_op jit(solution)/shard_map/all_to_all | solution.py:118
  106.3 4.1 %collective-permute-start.4 = (bf16[128,8,512]{2,1,0:T(8,128)(2,1)S(1)}, bf16[128,8,512]{2,1,0:T(8,128)(2,1)}, u32[]{:S(2)}, u32[]{:S(2)}) collective-permute-start(bf16[128,8,512]{2,1,0:T(8,128)(2,1)S(1)} %maximum_select_fusion.1), channel_id=1, source_target_pairs={{0,8},{8,0},{16,24},{24,16},{32,40},{40,32},{48,56},{56,48},{64,72... | collective-permute-start | bytes 3145736 | tf_op jit(solution)/shard_map/ppermute | solution.py:33
  137.7 7.0 %copy-start.1 = (f32[256,8,256]{2,1,0:T(8,128)S(1)}, f32[256,8,256]{2,1,0:T(8,128)}, u32[]{:S(2)}) copy-start(f32[256,8,256]{2,1,0:T(8,128)} %fusion.4) | copy-start | bytes 6291460
  141.2 12.4 %collective-permute-start.5 = (f32[32,256]{1,0:T(8,128)S(1)}, f32[32,256]{1,0:T(8,128)S(1)}, u32[]{:S(2)}, u32[]{:S(2)}) collective-permute-start(f32[32,256]{1,0:T(8,128)S(1)} %slice.91), channel_id=1, source_target_pairs={{0,8},{8,16},{16,24},{24,32},{32,40},{40,48},{48,56},{56,64},{64,7... | collective-permute-start | bytes 98312 | tf_op jit(solution)/shard_map/ppermute | solution.py:16
  154.6 43.2 %copy-start.8 = (s32[512,1]{0,1:T(1,128)S(1)}, s32[512,1]{0,1:T(1,128)}, u32[]{:S(2)}) copy-start(s32[512,1]{0,1:T(1,128)} %param.27) | copy-start | bytes 6148
  161.3 4.6 %collective-permute-start.6 = (f32[16,257]{1,0:T(8,128)S(1)}, f32[16,257]{1,0:T(8,128)S(1)}, u32[]{:S(2)}, u32[]{:S(2)}) collective-permute-start(f32[16,257]{1,0:T(8,128)S(1)} %pad_maximum_fusion.2), channel_id=1, source_target_pairs={{0,1},{1,0},{2,3},{3,2},{4,5},{5,4},{6,7},{7,6},{8,9},{9,8},{10,11... | collective-permute-start | bytes 49352 | tf_op jit(solution)/shard_map/ppermute | solution.py:23
  165.9 2.7 %collective-permute-start.7 = (f32[16,257]{1,0:T(8,128)S(1)}, f32[16,257]{1,0:T(8,128)S(1)}, u32[]{:S(2)}, u32[]{:S(2)}) collective-permute-start(f32[16,257]{1,0:T(8,128)S(1)} %fusion.36), channel_id=1, source_target_pairs={{0,2},{1,3},{2,0},{3,1},{4,6},{5,7},{6,4},{7,5},{8,10},{9,11},{10,... | collective-permute-start | bytes 49352 | tf_op jit(solution)/shard_map/ppermute | solution.py:23
  168.6 4.2 %collective-permute-start.8 = (f32[16,257]{1,0:T(8,128)S(1)}, f32[16,257]{1,0:T(8,128)S(1)}, u32[]{:S(2)}, u32[]{:S(2)}) collective-permute-start(f32[16,257]{1,0:T(8,128)S(1)} %add.76), channel_id=1, source_target_pairs={{0,4},{1,5},{2,6},{3,7},{4,0},{5,1},{6,2},{7,3},{8,12},{9,13},{10,... | collective-permute-start | bytes 49352 | tf_op jit(solution)/shard_map/ppermute | solution.py:23
  173.0 6.5 %collective-permute-start.9 = (f32[16,256]{1,0:T(8,128)S(1)}, f32[16,256]{1,0:T(8,128)S(1)}, u32[]{:S(2)}, u32[]{:S(2)}) collective-permute-start(f32[16,256]{1,0:T(8,128)S(1)} %slice_divide_fusion), channel_id=1, source_target_pairs={{0,128},{8,136},{16,144},{24,152},{32,160},{40,168},{48,176},{56,1... | collective-permute-start | bytes 49160 | tf_op jit(solution)/shard_map/ppermute | solution.py:33
  179.5 3.7 %collective-permute-start.10 = (f32[32,256]{1,0:T(8,128)S(1)}, f32[32,256]{1,0:T(8,128)S(1)}, u32[]{:S(2)}, u32[]{:S(2)}) collective-permute-start(f32[32,256]{1,0:T(8,128)S(1)} %maximum_select_fusion.10), channel_id=1, source_target_pairs={{0,64},{8,72},{16,80},{24,88},{32,96},{40,104},{48,112},{56,120},{... | collective-permute-start | bytes 98312 | tf_op jit(solution)/shard_map/ppermute | solution.py:33
  183.2 3.2 %collective-permute-start.11 = (f32[64,256]{1,0:T(8,128)S(1)}, f32[64,256]{1,0:T(8,128)S(1)}, u32[]{:S(2)}, u32[]{:S(2)}) collective-permute-start(f32[64,256]{1,0:T(8,128)S(1)} %maximum_select_fusion.9), channel_id=1, source_target_pairs={{0,32},{8,40},{16,48},{24,56},{32,0},{40,8},{48,16},{56,24},{64,96... | collective-permute-start | bytes 196616 | tf_op jit(solution)/shard_map/ppermute | solution.py:33
  186.4 5.1 %collective-permute-start.12 = (f32[128,256]{1,0:T(8,128)S(1)}, f32[128,256]{1,0:T(8,128)S(1)}, u32[]{:S(2)}, u32[]{:S(2)}) collective-permute-start(f32[128,256]{1,0:T(8,128)S(1)} %maximum_select_fusion.8), channel_id=1, source_target_pairs={{0,16},{8,24},{16,0},{24,8},{32,48},{40,56},{48,32},{56,40},{64,80... | collective-permute-start | bytes 393224 | tf_op jit(solution)/shard_map/ppermute | solution.py:33
  191.5 7.4 %collective-permute-start.13 = (f32[256,256]{1,0:T(8,128)S(1)}, f32[256,256]{1,0:T(8,128)S(1)}, u32[]{:S(2)}, u32[]{:S(2)}) collective-permute-start(f32[256,256]{1,0:T(8,128)S(1)} %maximum_select_fusion.6), channel_id=1, source_target_pairs={{0,8},{8,0},{16,24},{24,16},{32,40},{40,32},{48,56},{56,48},{64,72... | collective-permute-start | bytes 786440 | tf_op jit(solution)/shard_map/ppermute | solution.py:33

commit v10 on v7

--- a/solution.py
+++ b/solution.py
@@ -81,8 +81,12 @@
     basis_out_wide = basis_out.astype(jnp.float32)
     in_part = jnp.dot(activations, proj_in, preferred_element_type=jnp.float32)
     out_part = jnp.dot(out_grads, proj_out, preferred_element_type=jnp.float32)
-    stacked_parts = jnp.concatenate([in_part, out_part], axis=1)
-    gathered_parts = lax.all_to_all(stacked_parts, "factor", 0, 0, tiled=True)
+    out_sums = jnp.sum(
+        lax.all_to_all(out_part, "factor", 0, 0, tiled=True).reshape(factor_count, chunk, rank_out), axis=0
+    )
+    in_sums = jnp.sum(
+        lax.all_to_all(in_part, "factor", 0, 0, tiled=True).reshape(factor_count, chunk, rank_in), axis=0
+    )
     basis_cut = lax.dynamic_slice_in_dim(basis_out_wide, factor_index * rank_slice, rank_slice, 1)
     q_in = jnp.einsum(
         "qtk,kl->qtl", queries[:, :, :rank_in].astype(jnp.float32), basis_in_wide, precision=highest
@@ -92,9 +96,8 @@
     )
     outer = jnp.einsum("qti,qtj->qij", q_out, q_in, precision=highest)
     query_grad = (outer * scale_block[None]).astype(jnp.bfloat16)
-    chunk_sums = jnp.sum(gathered_parts.reshape(factor_count, chunk, rank_in + rank_out), axis=0)
-    rot_in_chunk = jnp.dot(chunk_sums[:, :rank_in], basis_in_wide, precision=highest)
-    rot_out_chunk = jnp.dot(chunk_sums[:, rank_in:], basis_out_wide, precision=highest)
+    rot_in_chunk = jnp.dot(in_sums, basis_in_wide, precision=highest)
+    rot_out_chunk = jnp.dot(out_sums, basis_out_wide, precision=highest)
     out_blocks = rot_out_chunk.reshape(chunk, factor_count, rank_slice).transpose(1, 0, 2)
     sending = jnp.concatenate(
         [jnp.broadcast_to(rot_in_chunk[None], (factor_count, chunk, rank_in)), out_blocks], axis=2

time: 176 us -> 177 us (level)
  starting transfers between devices: 50.9 us -> 58.2 us
  waiting for transfers between devices: 74.3 us -> 67.6 us
  local copies, waits for them, and re-layouts: 8.2 us -> 5.98 us
    all_to_all x1 -> x2, starting transfers between devices: 7.6 us -> 12.1 us  [the longest x1 7.61 us: per_device(): lax.all_to_all(out_part, 'factor', 0, 0, tiled=True)]
    all_to_all x1 -> x2, waiting for transfers between devices: 27.9 us -> 23.6 us  [the longest x1 21.2 us: per_device(): lax.all_to_all(out_part, 'factor', 0, 0, tiled=True)]
    all_to_all x1 -> x0, local copies, waits for them, and re-layouts: 2.33 us -> none  [per_device(): gathered_parts = lax.all_to_all(stacked_parts, 'factor', 0, 0, tiled=True)]
    all_to_all x1, waiting for transfers between devices: 15 us -> 13.2 us  [per_device(): received = lax.all_to_all(sending, 'factor', 0, 0, tiled=True)]
  transfers between devices with their start and end apart: 16 -> 17, of which waited for: 14 -> 14; matrix products, arithmetic and copies ran while one was open for 13% -> 17% of each run, Pallas kernels for 0% -> 0%
where the time goes in v10:
time: 177 us
  waiting for transfers between devices  67.6 us (38%)
  starting transfers between devices  58.2 us (33%)
  matrix products  31.9 us (18%)
  other arithmetic  11.1 us (6%)
  local copies, waits for them, and re-layouts  5.98 us (3%)
  between operations  1.81 us (1%)
    ppermute x10, starting transfers between devices, butterfly_gather(): other = lax.ppermute(block, axis, [(i, i ^ step) for i in range(size)])  32 us
    all_to_all x1, waiting for transfers between devices, per_device(): lax.all_to_all(out_part, 'factor', 0, 0, tiled=True)  21.2 us
    ppermute x10, waiting for transfers between devices, butterfly_gather(): other = lax.ppermute(block, axis, [(i, i ^ step) for i in range(size)])  21.1 us
    all_to_all x1, waiting for transfers between devices, per_device(): received = lax.all_to_all(sending, 'factor', 0, 0, tiled=True)  13.2 us
    ppermute x3, waiting for transfers between devices, butterfly_sum(): lax.ppermute(block, axis, [(i, i ^ step) for i in range(size)])  9.64 us
    dot_general x1, matrix products, per_device(): outer = jnp.einsum('qti,qtj->qij', q_out, q_in, precision=highest)  8.55 us
    all_to_all x1, starting transfers between devices, per_device(): lax.all_to_all(out_part, 'factor', 0, 0, tiled=True)  7.61 us
    ppermute x1, starting transfers between devices, from_behind(): return lax.ppermute(block, axis, route)  7.42 us
  transfers between devices with their start and end apart: 17, of which 14 were waited for; matrix products, arithmetic and copies ran while one was open for 17% of the time, Pallas kernels for 0%

profile of v10, /device:TPU:1, one launch (start us, length us, event | category | flops | bytes accessed | tf_op | source)
XLA Modules:
  0.0 176.6 jit_solution(12539581228674451448)
XLA Ops:
  1.6 3.0 %fusion.37 = f32[2048,256]{1,0:T(8,128)} fusion(bf16[2048,512]{1,0:T(8,128)(2,1)S(1)} %copy-done, bf16[512,256]{1,0:T(8,128)(2,1)} %param.19), kind=kOutput, calls=%fused_computation.67 | convolution fusion | flops 536870912 | bytes 4456448 | tf_op jit(solution)/shard_map/dot_general | solution.py:83
  4.6 7.6 %all-to-all-start.1 = ((f32[8,256,256]{2,1,0:T(8,128)}), f32[8,256,256]{2,1,0:T(8,128)}, u32[]{:S(2)}, u32[]{:S(2)}) async-start(f32[8,256,256]{2,1,0:T(8,128)} %bitcast.56), calls=%async_computation.1 | async-start | bytes 4194304 | tf_op jit(solution)/shard_map/all_to_all | solution.py:85
  12.2 6.5 %fusion.35 = f32[2048,256]{1,0:T(8,128)} fusion(bf16[2048,1792]{1,0:T(8,128)(2,1)} %param.16, bf16[1792,256]{1,0:T(8,128)(2,1)S(1)} %copy-done.12), kind=kOutput, calls=%fused_computation.65 | convolution fusion | flops 1879048192 | bytes 10354688 | tf_op jit(solution)/shard_map/dot_general | solution.py:82
  18.7 21.2 %all-to-all-done.1 = f32[8,256,256]{2,1,0:T(8,128)} async-done(((f32[8,256,256]{2,1,0:T(8,128)}), f32[8,256,256]{2,1,0:T(8,128)}, u32[]{:S(2)}, u32[]{:S(2)}) %all-to-all-start.1) | async-done | bytes 2097184 | tf_op jit(solution)/shard_map/all_to_all | solution.py:85
  39.9 4.5 %all-to-all-start = ((f32[8,256,256]{2,1,0:T(8,128)}), f32[8,256,256]{2,1,0:T(8,128)}, u32[]{:S(2)}, u32[]{:S(2)}) async-start(f32[8,256,256]{2,1,0:T(8,128)} %bitcast.60), calls=%async_computation | async-start | bytes 4194304 | tf_op jit(solution)/shard_map/all_to_all | solution.py:88
  44.4 7.0 %collective-permute-start = (bf16[8,8,512]{2,1,0:T(8,128)(2,1)S(1)}, bf16[8,8,512]{2,1,0:T(8,128)(2,1)S(1)}, u32[]{:S(2)}, u32[]{:S(2)}) collective-permute-start(bf16[8,8,512]{2,1,0:T(8,128)(2,1)S(1)} %constant_dynamic-update-slice_fusion), channel_id=1, source_target_pairs={{0,128},{8,136},{16,144},{24,152},{32,160},{40,168},{48,176},{56,1... | collective-permute-start | bytes 196616 | tf_op jit(solution)/shard_map/ppermute | solution.py:33
  54.6 5.7 %collective-permute-done.1 = bf16[16,8,512]{2,1,0:T(8,128)(2,1)S(1)} collective-permute-done((bf16[16,8,512]{2,1,0:T(8,128)(2,1)S(1)}, bf16[16,8,512]{2,1,0:T(8,128)(2,1)S(1)}, u32[]{:S(2)}, u32[]{:S(2)}) %collective-permute-start.1) | collective-permute-done | bytes 131104 | tf_op jit(solution)/shard_map/ppermute | solution.py:33
  60.6 5.5 %collective-permute-done.2 = bf16[32,8,512]{2,1,0:T(8,128)(2,1)S(1)} collective-permute-done((bf16[32,8,512]{2,1,0:T(8,128)(2,1)S(1)}, bf16[32,8,512]{2,1,0:T(8,128)(2,1)S(1)}, u32[]{:S(2)}, u32[]{:S(2)}) %collective-permute-start.2) | collective-permute-done | bytes 262176 | tf_op jit(solution)/shard_map/ppermute | solution.py:33
  66.5 1.8 reduce_sum.38
  68.6 2.4 %all-to-all-done = f32[8,256,256]{2,1,0:T(8,128)} async-done(((f32[8,256,256]{2,1,0:T(8,128)}), f32[8,256,256]{2,1,0:T(8,128)}, u32[]{:S(2)}, u32[]{:S(2)}) %all-to-all-start) | async-done | bytes 2097184 | tf_op jit(solution)/shard_map/all_to_all | solution.py:88
  71.1 1.8 reduce_sum.37
  74.9 4.9 %all-to-all-start.2 = ((f32[8,256,288]{1,2,0:T(8,128)}), f32[8,256,288]{1,2,0:T(8,128)}, u32[]{:S(2)}, u32[]{:S(2)}) async-start(f32[8,256,288]{1,2,0:T(8,128)} %pad_maximum_fusion), calls=%async_computation.2 | async-start | bytes 4718592 | tf_op jit(solution)/shard_map/all_to_all | solution.py:105
  79.9 1.7 maximum_select_fusion.1
  81.6 4.7 %collective-permute-start.4 = (bf16[128,8,512]{2,1,0:T(8,128)(2,1)S(1)}, bf16[128,8,512]{2,1,0:T(8,128)(2,1)}, u32[]{:S(2)}, u32[]{:S(2)}) collective-permute-start(bf16[128,8,512]{2,1,0:T(8,128)(2,1)S(1)} %maximum_select_fusion.1), channel_id=1, source_target_pairs={{0,8},{8,0},{16,24},{24,16},{32,40},{40,32},{48,56},{56,48},{64,72... | collective-permute-start | bytes 3145736 | tf_op jit(solution)/shard_map/ppermute | solution.py:33
  89.2 1.9 %maximum_select_fusion = bf16[256,8,512]{2,1,0:T(8,128)(2,1)S(1)} fusion(bf16[128,8,512]{2,1,0:T(8,128)(2,1)S(1)} %maximum_select_fusion.1, bf16[128,8,512]{2,1,0:T(8,128)(2,1)} %collective-permute-done.4, pred[]{:T(512)S(6)} %eq.94), kind=kLoop, calls=%fused_computation.6 | loop fusion | flops 3145728 | bytes 4194305 | tf_op jit(solution)/shard_map/jit(_where)/select_n | solution.py:35
  91.6 1.8 %fusion.4 = f32[256,8,256]{2,1,0:T(8,128)} fusion(bf16[256,8,512]{2,1,0:T(8,128)(2,1)S(1)} %maximum_select_fusion, bf16[256,256]{1,0:T(8,128)(2,1)S(1)} %copy-done.3), kind=kOutput, calls=%fused_computation.9 | convolution fusion | flops 268435456 | bytes 3276800 | tf_op jit(solution)/shard_map/qtk,kl->qtl/dot_general | solution.py:91
  93.4 13.2 %all-to-all-done.2 = f32[8,256,288]{1,2,0:T(8,128)} async-done(((f32[8,256,288]{1,2,0:T(8,128)}), f32[8,256,288]{1,2,0:T(8,128)}, u32[]{:S(2)}, u32[]{:S(2)}) %all-to-all-start.2) | async-done | bytes 2359328 | tf_op jit(solution)/shard_map/all_to_all | solution.py:105
  106.6 1.9 %copy.83 = f32[8,36,8,256]{3,2,0,1:T(8,128)S(1)} copy(f32[8,36,8,256]{3,2,1,0:T(8,128)} %bitcast.29) | data formatting | bytes 4718592 | tf_op jit(solution)/shard_map/all_to_all | solution.py:105
  109.1 3.5 %fusion.2 = f32[512,256]{1,0:T(8,128)S(1)} fusion(f32[2048,512]{0,1:T(8,128)S(1)} %bitcast.55, f32[2048,288]{0,1:T(8,128)S(1)} %bitcast.58), kind=kOutput, calls=%fused_computation.4 | convolution fusion | flops 3221225472 | bytes 6815744 | tf_op jit(solution)/shard_map/dot_general | solution.py:119
  112.6 7.4 %collective-permute-start.5 = (f32[32,256]{1,0:T(8,128)S(1)}, f32[32,256]{1,0:T(8,128)S(1)}, u32[]{:S(2)}, u32[]{:S(2)}) collective-permute-start(f32[32,256]{1,0:T(8,128)S(1)} %slice.81), channel_id=1, source_target_pairs={{0,8},{8,16},{16,24},{24,32},{32,40},{40,48},{48,56},{56,64},{64,7... | collective-permute-start | bytes 98312 | tf_op jit(solution)/shard_map/ppermute | solution.py:16
  120.0 8.5 %multiply_convert_fusion = bf16[256,32,256]{2,1,0:T(8,128)(2,1)} fusion(f32[32,256]{1,0:T(8,128)S(1)} %copy-done.4, f32[256,8,32]{2,1,0:T(8,128)S(1)} %fusion.6, f32[256,8,256]{2,1,0:T(8,128)S(1)} %copy-done.1), kind=kOutput, calls=%fused_computation | convolution fusion | flops 205520896 | bytes 6586368 | tf_op jit(solution)/shard_map/qti,qtj->qij/dot_general | solution.py:97
  129.8 6.6 %fusion = f32[256,16,1]{1,0,2:T(8,128)S(1)} fusion(bf16[256,32,256]{2,1,0:T(8,128)(2,1)} %multiply_convert_fusion, f32[16,32,256]{2,0,1:T(8,128)S(1)} %scatter-mul.4), kind=kOutput, calls=%fused_computation.1 | convolution fusion | flops 67239936 | bytes 4734976 | tf_op jit(solution)/shard_map/dot_general | solution.py:133
  137.8 3.4 %collective-permute-done.6 = f32[16,257]{1,0:T(8,128)S(1)} collective-permute-done((f32[16,257]{1,0:T(8,128)S(1)}, f32[16,257]{1,0:T(8,128)S(1)}, u32[]{:S(2)}, u32[]{:S(2)}) %collective-permute-start.6) | collective-permute-done | bytes 16480 | tf_op jit(solution)/shard_map/ppermute | solution.py:23
  141.2 2.7 %collective-permute-done.7 = f32[16,257]{1,0:T(8,128)S(1)} collective-permute-done((f32[16,257]{1,0:T(8,128)S(1)}, f32[16,257]{1,0:T(8,128)S(1)}, u32[]{:S(2)}, u32[]{:S(2)}) %collective-permute-start.7) | collective-permute-done | bytes 16480 | tf_op jit(solution)/shard_map/ppermute | solution.py:23
  144.4 3.6 %collective-permute-done.8 = f32[16,257]{1,0:T(8,128)S(1)} collective-permute-done((f32[16,257]{1,0:T(8,128)S(1)}, f32[16,257]{1,0:T(8,128)S(1)}, u32[]{:S(2)}, u32[]{:S(2)}) %collective-permute-start.8) | collective-permute-done | bytes 16480 | tf_op jit(solution)/shard_map/ppermute | solution.py:23
  148.2 6.6 %collective-permute-start.9 = (f32[16,256]{1,0:T(8,128)S(1)}, f32[16,256]{1,0:T(8,128)S(1)}, u32[]{:S(2)}, u32[]{:S(2)}) collective-permute-start(f32[16,256]{1,0:T(8,128)S(1)} %slice_divide_fusion), channel_id=1, source_target_pairs={{0,128},{8,136},{16,144},{24,152},{32,160},{40,168},{48,176},{56,1... | collective-permute-start | bytes 49160 | tf_op jit(solution)/shard_map/ppermute | solution.py:33
  156.0 1.8 %collective-permute-start.10 = (f32[32,256]{1,0:T(8,128)S(1)}, f32[32,256]{1,0:T(8,128)S(1)}, u32[]{:S(2)}, u32[]{:S(2)}) collective-permute-start(f32[32,256]{1,0:T(8,128)S(1)} %maximum_select_fusion.10), channel_id=1, source_target_pairs={{0,64},{8,72},{16,80},{24,88},{32,96},{40,104},{48,112},{56,120},{... | collective-permute-start | bytes 98312 | tf_op jit(solution)/shard_map/ppermute | solution.py:33
  157.8 1.9 %collective-permute-done.10 = f32[32,256]{1,0:T(8,128)S(1)} collective-permute-done((f32[32,256]{1,0:T(8,128)S(1)}, f32[32,256]{1,0:T(8,128)S(1)}, u32[]{:S(2)}, u32[]{:S(2)}) %collective-permute-start.10) | collective-permute-done | bytes 32800 | tf_op jit(solution)/shard_map/ppermute | solution.py:33
  160.8 2.1 %collective-permute-done.11 = f32[64,256]{1,0:T(8,128)S(1)} collective-permute-done((f32[64,256]{1,0:T(8,128)S(1)}, f32[64,256]{1,0:T(8,128)S(1)}, u32[]{:S(2)}, u32[]{:S(2)}) %collective-permute-start.11) | collective-permute-done | bytes 65568 | tf_op jit(solution)/shard_map/ppermute | solution.py:33
  162.9 3.0 %collective-permute-start.12 = (f32[128,256]{1,0:T(8,128)S(1)}, f32[128,256]{1,0:T(8,128)S(1)}, u32[]{:S(2)}, u32[]{:S(2)}) collective-permute-start(f32[128,256]{1,0:T(8,128)S(1)} %maximum_select_fusion.8), channel_id=1, source_target_pairs={{0,16},{8,24},{16,0},{24,8},{32,48},{40,56},{48,32},{56,40},{64,80... | collective-permute-start | bytes 393224 | tf_op jit(solution)/shard_map/ppermute | solution.py:33
  165.9 2.7 %collective-permute-done.12 = f32[128,256]{1,0:T(8,128)S(1)} collective-permute-done((f32[128,256]{1,0:T(8,128)S(1)}, f32[128,256]{1,0:T(8,128)S(1)}, u32[]{:S(2)}, u32[]{:S(2)}) %collective-permute-start.12) | collective-permute-done | bytes 131104 | tf_op jit(solution)/shard_map/ppermute | solution.py:33
  168.6 5.9 %collective-permute-start.13 = (f32[256,256]{1,0:T(8,128)S(1)}, f32[256,256]{1,0:T(8,128)S(1)}, u32[]{:S(2)}, u32[]{:S(2)}) collective-permute-start(f32[256,256]{1,0:T(8,128)S(1)} %maximum_select_fusion.6), channel_id=1, source_target_pairs={{0,8},{8,0},{16,24},{24,16},{32,40},{40,32},{48,56},{56,48},{64,72... | collective-permute-start | bytes 786440 | tf_op jit(solution)/shard_map/ppermute | solution.py:33
  (89 shorter events, 18.1 us)
Async XLA Ops:
  0.0 1.6 copy-start
  4.6 7.6 %copy-start.12 = (bf16[1792,256]{1,0:T(8,128)(2,1)S(1)}, bf16[1792,256]{1,0:T(8,128)(2,1)}, u32[]{:S(2)}) copy-start(bf16[1792,256]{1,0:T(8,128)(2,1)} %param.18) | copy-start | bytes 2752516
  4.6 35.3 %all-to-all-start.1 = ((f32[8,256,256]{2,1,0:T(8,128)}), f32[8,256,256]{2,1,0:T(8,128)}, u32[]{:S(2)}, u32[]{:S(2)}) async-start(f32[8,256,256]{2,1,0:T(8,128)} %bitcast.56), calls=%async_computation.1 | async-start | bytes 4194304 | tf_op jit(solution)/shard_map/all_to_all | solution.py:85
  39.9 4.5 %copy-start.6 = (bf16[8,8,256]{2,1,0:T(8,128)(2,1)S(1)}, bf16[8,8,256]{2,1,0:T(8,128)(2,1)}, u32[]{:S(2)}) copy-start(bf16[8,8,256]{2,1,0:T(8,128)(2,1)} %param.23) | copy-start | bytes 98308
  39.9 4.5 %copy-start.7 = (bf16[8,8,256]{2,1,0:T(8,128)(2,1)S(1)}, bf16[8,8,256]{2,1,0:T(8,128)(2,1)}, u32[]{:S(2)}) copy-start(bf16[8,8,256]{2,1,0:T(8,128)(2,1)} %param.24) | copy-start | bytes 98308
  39.9 20.6 %copy-start.5 = (bf16[256,256]{1,0:T(8,128)(2,1)S(1)}, bf16[256,256]{1,0:T(8,128)(2,1)}, u32[]{:S(2)}) copy-start(bf16[256,256]{1,0:T(8,128)(2,1)} %param.21) | copy-start | bytes 393220
  39.9 31.2 %all-to-all-start = ((f32[8,256,256]{2,1,0:T(8,128)}), f32[8,256,256]{2,1,0:T(8,128)}, u32[]{:S(2)}, u32[]{:S(2)}) async-start(f32[8,256,256]{2,1,0:T(8,128)} %bitcast.60), calls=%async_computation | async-start | bytes 4194304 | tf_op jit(solution)/shard_map/all_to_all | solution.py:88
  44.4 8.7 %collective-permute-start = (bf16[8,8,512]{2,1,0:T(8,128)(2,1)S(1)}, bf16[8,8,512]{2,1,0:T(8,128)(2,1)S(1)}, u32[]{:S(2)}, u32[]{:S(2)}) collective-permute-start(bf16[8,8,512]{2,1,0:T(8,128)(2,1)S(1)} %constant_dynamic-update-slice_fusion), channel_id=1, source_target_pairs={{0,128},{8,136},{16,144},{24,152},{32,160},{40,168},{48,176},{56,1... | collective-permute-start | bytes 196616 | tf_op jit(solution)/shard_map/ppermute | solution.py:33
  53.1 7.1 %collective-permute-start.1 = (bf16[16,8,512]{2,1,0:T(8,128)(2,1)S(1)}, bf16[16,8,512]{2,1,0:T(8,128)(2,1)S(1)}, u32[]{:S(2)}, u32[]{:S(2)}) collective-permute-start(bf16[16,8,512]{2,1,0:T(8,128)(2,1)S(1)} %maximum_select_fusion.7), channel_id=1, source_target_pairs={{0,64},{8,72},{16,80},{24,88},{32,96},{40,104},{48,112},{56,120},{... | collective-permute-start | bytes 393224 | tf_op jit(solution)/shard_map/ppermute | solution.py:33
  60.3 5.7 %collective-permute-start.2 = (bf16[32,8,512]{2,1,0:T(8,128)(2,1)S(1)}, bf16[32,8,512]{2,1,0:T(8,128)(2,1)S(1)}, u32[]{:S(2)}, u32[]{:S(2)}) collective-permute-start(bf16[32,8,512]{2,1,0:T(8,128)(2,1)S(1)} %maximum_select_fusion.5), channel_id=1, source_target_pairs={{0,32},{8,40},{16,48},{24,56},{32,0},{40,8},{48,16},{56,24},{64,96... | collective-permute-start | bytes 786440 | tf_op jit(solution)/shard_map/ppermute | solution.py:33
  66.1 6.7 %copy-start.2 = (bf16[64,8,512]{2,1,0:T(8,128)(2,1)}, bf16[64,8,512]{2,1,0:T(8,128)(2,1)S(1)}, u32[]{:S(2)}) copy-start(bf16[64,8,512]{2,1,0:T(8,128)(2,1)S(1)} %maximum_select_fusion.2) | copy-start | bytes 1572868
  66.1 13.8 %collective-permute-start.3 = (bf16[64,8,512]{2,1,0:T(8,128)(2,1)S(1)}, bf16[64,8,512]{2,1,0:T(8,128)(2,1)}, u32[]{:S(2)}, u32[]{:S(2)}) collective-permute-start(bf16[64,8,512]{2,1,0:T(8,128)(2,1)S(1)} %maximum_select_fusion.2), channel_id=1, source_target_pairs={{0,16},{8,24},{16,0},{24,8},{32,48},{40,56},{48,32},{56,40},{64,80... | collective-permute-start | bytes 1572872 | tf_op jit(solution)/shard_map/ppermute | solution.py:33
  68.3 4.6 %copy-start.3 = (bf16[256,256]{1,0:T(8,128)(2,1)S(1)}, bf16[256,256]{1,0:T(8,128)(2,1)}, u32[]{:S(2)}) copy-start(bf16[256,256]{1,0:T(8,128)(2,1)} %param.20) | copy-start | bytes 393220
  74.9 31.7 %all-to-all-start.2 = ((f32[8,256,288]{1,2,0:T(8,128)}), f32[8,256,288]{1,2,0:T(8,128)}, u32[]{:S(2)}, u32[]{:S(2)}) async-start(f32[8,256,288]{1,2,0:T(8,128)} %pad_maximum_fusion), calls=%async_computation.2 | async-start | bytes 4718592 | tf_op jit(solution)/shard_map/all_to_all | solution.py:105
  79.8 6.5 %copy-start.11 = (s32[1,16]{1,0:T(1,128)S(1)}, s32[1,16]{1,0:T(1,128)}, u32[]{:S(2)}) copy-start(s32[1,16]{1,0:T(1,128)} %param.25) | copy-start | bytes 196
  79.8 6.7 %copy-start.10 = (s32[32]{0:T(128)S(1)}, s32[32]{0:T(128)}, u32[]{:S(2)}) copy-start(s32[32]{0:T(128)} %param.26) | copy-start | bytes 388
  79.9 8.6 %copy-start.8 = (f32[32,256]{1,0:T(8,128)S(1)}, f32[32,256]{1,0:T(8,128)}, u32[]{:S(2)}) copy-start(f32[32,256]{1,0:T(8,128)} %param.22) | copy-start | bytes 98308
  81.6 7.6 %collective-permute-start.4 = (bf16[128,8,512]{2,1,0:T(8,128)(2,1)S(1)}, bf16[128,8,512]{2,1,0:T(8,128)(2,1)}, u32[]{:S(2)}, u32[]{:S(2)}) collective-permute-start(bf16[128,8,512]{2,1,0:T(8,128)(2,1)S(1)} %maximum_select_fusion.1), channel_id=1, source_target_pairs={{0,8},{8,0},{16,24},{24,16},{32,40},{40,32},{48,56},{56,48},{64,72... | collective-permute-start | bytes 3145736 | tf_op jit(solution)/shard_map/ppermute | solution.py:33
  109.1 10.9 %copy-start.1 = (f32[256,8,256]{2,1,0:T(8,128)S(1)}, f32[256,8,256]{2,1,0:T(8,128)}, u32[]{:S(2)}) copy-start(f32[256,8,256]{2,1,0:T(8,128)} %fusion.4) | copy-start | bytes 6291460
  109.1 10.9 %copy-start.4 = (f32[32,256]{1,0:T(8,128)S(1)}, f32[32,256]{1,0:T(8,128)}, u32[]{:S(2)}) copy-start(f32[32,256]{1,0:T(8,128)} %add_divide_fusion) | copy-start | bytes 98308
  112.6 16.3 %collective-permute-start.5 = (f32[32,256]{1,0:T(8,128)S(1)}, f32[32,256]{1,0:T(8,128)S(1)}, u32[]{:S(2)}, u32[]{:S(2)}) collective-permute-start(f32[32,256]{1,0:T(8,128)S(1)} %slice.81), channel_id=1, source_target_pairs={{0,8},{8,16},{16,24},{24,32},{32,40},{40,48},{48,56},{56,64},{64,7... | collective-permute-start | bytes 98312 | tf_op jit(solution)/shard_map/ppermute | solution.py:16
  129.8 44.6 %copy-start.9 = (s32[512,1]{0,1:T(1,128)S(1)}, s32[512,1]{0,1:T(1,128)}, u32[]{:S(2)}) copy-start(s32[512,1]{0,1:T(1,128)} %param.27) | copy-start | bytes 6148
  136.6 4.6 %collective-permute-start.6 = (f32[16,257]{1,0:T(8,128)S(1)}, f32[16,257]{1,0:T(8,128)S(1)}, u32[]{:S(2)}, u32[]{:S(2)}) collective-permute-start(f32[16,257]{1,0:T(8,128)S(1)} %pad_maximum_fusion.1), channel_id=1, source_target_pairs={{0,1},{1,0},{2,3},{3,2},{4,5},{5,4},{6,7},{7,6},{8,9},{9,8},{10,11... | collective-permute-start | bytes 49352 | tf_op jit(solution)/shard_map/ppermute | solution.py:23
  141.2 2.7 %collective-permute-start.7 = (f32[16,257]{1,0:T(8,128)S(1)}, f32[16,257]{1,0:T(8,128)S(1)}, u32[]{:S(2)}, u32[]{:S(2)}) collective-permute-start(f32[16,257]{1,0:T(8,128)S(1)} %fusion.33), channel_id=1, source_target_pairs={{0,2},{1,3},{2,0},{3,1},{4,6},{5,7},{6,4},{7,5},{8,10},{9,11},{10,... | collective-permute-start | bytes 49352 | tf_op jit(solution)/shard_map/ppermute | solution.py:23
  143.9 4.2 %collective-permute-start.8 = (f32[16,257]{1,0:T(8,128)S(1)}, f32[16,257]{1,0:T(8,128)S(1)}, u32[]{:S(2)}, u32[]{:S(2)}) collective-permute-start(f32[16,257]{1,0:T(8,128)S(1)} %add.76), channel_id=1, source_target_pairs={{0,4},{1,5},{2,6},{3,7},{4,0},{5,1},{6,2},{7,3},{8,12},{9,13},{10,... | collective-permute-start | bytes 49352 | tf_op jit(solution)/shard_map/ppermute | solution.py:23
  148.2 7.7 %collective-permute-start.9 = (f32[16,256]{1,0:T(8,128)S(1)}, f32[16,256]{1,0:T(8,128)S(1)}, u32[]{:S(2)}, u32[]{:S(2)}) collective-permute-start(f32[16,256]{1,0:T(8,128)S(1)} %slice_divide_fusion), channel_id=1, source_target_pairs={{0,128},{8,136},{16,144},{24,152},{32,160},{40,168},{48,176},{56,1... | collective-permute-start | bytes 49160 | tf_op jit(solution)/shard_map/ppermute | solution.py:33
  156.0 3.7 %collective-permute-start.10 = (f32[32,256]{1,0:T(8,128)S(1)}, f32[32,256]{1,0:T(8,128)S(1)}, u32[]{:S(2)}, u32[]{:S(2)}) collective-permute-start(f32[32,256]{1,0:T(8,128)S(1)} %maximum_select_fusion.10), channel_id=1, source_target_pairs={{0,64},{8,72},{16,80},{24,88},{32,96},{40,104},{48,112},{56,120},{... | collective-permute-start | bytes 98312 | tf_op jit(solution)/shard_map/ppermute | solution.py:33
  159.7 3.2 %collective-permute-start.11 = (f32[64,256]{1,0:T(8,128)S(1)}, f32[64,256]{1,0:T(8,128)S(1)}, u32[]{:S(2)}, u32[]{:S(2)}) collective-permute-start(f32[64,256]{1,0:T(8,128)S(1)} %maximum_select_fusion.9), channel_id=1, source_target_pairs={{0,32},{8,40},{16,48},{24,56},{32,0},{40,8},{48,16},{56,24},{64,96... | collective-permute-start | bytes 196616 | tf_op jit(solution)/shard_map/ppermute | solution.py:33
  162.9 5.6 %collective-permute-start.12 = (f32[128,256]{1,0:T(8,128)S(1)}, f32[128,256]{1,0:T(8,128)S(1)}, u32[]{:S(2)}, u32[]{:S(2)}) collective-permute-start(f32[128,256]{1,0:T(8,128)S(1)} %maximum_select_fusion.8), channel_id=1, source_target_pairs={{0,16},{8,24},{16,0},{24,8},{32,48},{40,56},{48,32},{56,40},{64,80... | collective-permute-start | bytes 393224 | tf_op jit(solution)/shard_map/ppermute | solution.py:33
  168.6 7.0 %collective-permute-start.13 = (f32[256,256]{1,0:T(8,128)S(1)}, f32[256,256]{1,0:T(8,128)S(1)}, u32[]{:S(2)}, u32[]{:S(2)}) collective-permute-start(f32[256,256]{1,0:T(8,128)S(1)} %maximum_select_fusion.6), channel_id=1, source_target_pairs={{0,8},{8,0},{16,24},{24,16},{32,40},{40,32},{48,56},{56,48},{64,72... | collective-permute-start | bytes 786440 | tf_op jit(solution)/shard_map/ppermute | solution.py:33

commit v11 on v7

--- a/solution.py
+++ b/solution.py
@@ -127,10 +127,10 @@
     self_part = jnp.sum(grad_rows * grad_rows * scale_block[None], axis=(1, 2))
     grad_low = grad_rows.astype(jnp.bfloat16)
 
-    part = lax.dot_general(
-        grad_low, query_grad, (((1, 2), (1, 2)), ((), ())), preferred_element_type=jnp.float32
+    part_by_query = lax.dot_general(
+        query_grad, grad_low, (((1, 2), (1, 2)), ((), ())), preferred_element_type=jnp.float32
     )
-    part = bit_reversed(part.T, data_count).T
+    part = bit_reversed(part_by_query, data_count).T
 
     totals = butterfly_sum(jnp.concatenate([part, self_part[:, None]], axis=1), "factor")
     relative = totals[:, :-1] / jnp.sqrt(totals[:, -1:] + EPSILON)

time: 176 us -> 176 us (level)
  no operation moved by 1% of the time
where the time goes in v11:
time: 176 us; the launch traced here: 175 us
  waiting for transfers between devices  74.3 us (42%)
  starting transfers between devices  50.9 us (29%)
  matrix products  30.3 us (17%)
  other arithmetic  9.76 us (6%)
  local copies, waits for them, and re-layouts  8.2 us (5%)
  between operations  1.78 us (1%)
    ppermute x10, starting transfers between devices, butterfly_gather(): other = lax.ppermute(block, axis, [(i, i ^ step) for i in range(size)])  30.6 us
    all_to_all x1, waiting for transfers between devices, per_device(): gathered_parts = lax.all_to_all(stacked_parts, 'factor', 0, 0, tiled=True)  27.9 us
    ppermute x10, waiting for transfers between devices, butterfly_gather(): other = lax.ppermute(block, axis, [(i, i ^ step) for i in range(size)])  22 us
    all_to_all x1, waiting for transfers between devices, per_device(): received = lax.all_to_all(sending, 'factor', 0, 0, tiled=True)  15 us
    ppermute x3, waiting for transfers between devices, butterfly_sum(): lax.ppermute(block, axis, [(i, i ^ step) for i in range(size)])  9.32 us
    dot_general x1, matrix products, per_device(): outer = jnp.einsum('qti,qtj->qij', q_out, q_in, precision=highest)  8.55 us
    all_to_all x1, starting transfers between devices, per_device(): gathered_parts = lax.all_to_all(stacked_parts, 'factor', 0, 0, tiled=True)  7.6 us
    dot_general x1, matrix products, per_device(): lax.dot_general(query_grad, grad_low, (((1, 2), (1, 2)), ((), ())), prefe...  6.64 us
  transfers between devices with their start and end apart: 16, of which 14 were waited for; matrix products, arithmetic and copies ran while one was open for 13% of the time, Pallas kernels for 0%

profile of v11, /device:TPU:1, one launch (start us, length us, event | category | flops | bytes accessed | tf_op | source)
XLA Modules:
  0.0 175.2 jit_solution(5587162217992293762)
XLA Ops:
  0.0 1.6 copy-done
  1.6 1.7 fusion.39
  3.3 5.2 %fusion.38 = f32[2048,256]{0,1:T(8,128)S(1)} fusion(bf16[2048,1792]{1,0:T(8,128)(2,1)} %param.16, bf16[1792,256]{1,0:T(8,128)(2,1)S(1)} %copy-done.11), kind=kOutput, calls=%fused_computation.69 | convolution fusion | flops 1879048192 | bytes 10354688 | tf_op jit(solution)/shard_map/dot_general | solution.py:82
  8.8 2.3 %copy.93 = f32[64,8,8,256]{3,2,0,1:T(8,128)} copy(f32[64,8,8,256]{3,2,1,0:T(8,128)S(1)} %bitcast.53) | data formatting | bytes 8388608 | tf_op jit(solution)/shard_map/all_to_all | solution.py:85
  11.1 7.6 %all-to-all-start = ((f32[8,256,512]{1,2,0:T(8,128)}), f32[8,256,512]{1,2,0:T(8,128)}, u32[]{:S(2)}, u32[]{:S(2)}) async-start(f32[8,256,512]{1,2,0:T(8,128)} %bitcast.52), calls=%async_computation | async-start | bytes 8388608 | tf_op jit(solution)/shard_map/all_to_all | solution.py:85
  18.8 7.0 %collective-permute-start = (bf16[8,8,512]{2,1,0:T(8,128)(2,1)S(1)}, bf16[8,8,512]{2,1,0:T(8,128)(2,1)S(1)}, u32[]{:S(2)}, u32[]{:S(2)}) collective-permute-start(bf16[8,8,512]{2,1,0:T(8,128)(2,1)S(1)} %constant_dynamic-update-slice_fusion), channel_id=1, source_target_pairs={{0,128},{8,136},{16,144},{24,152},{32,160},{40,168},{48,176},{56,1... | collective-permute-start | bytes 196616 | tf_op jit(solution)/shard_map/ppermute | solution.py:33
  25.8 1.7 collective-permute-done
  29.0 5.7 %collective-permute-done.1 = bf16[16,8,512]{2,1,0:T(8,128)(2,1)S(1)} collective-permute-done((bf16[16,8,512]{2,1,0:T(8,128)(2,1)S(1)}, bf16[16,8,512]{2,1,0:T(8,128)(2,1)S(1)}, u32[]{:S(2)}, u32[]{:S(2)}) %collective-permute-start.1) | collective-permute-done | bytes 131104 | tf_op jit(solution)/shard_map/ppermute | solution.py:33
  34.9 5.6 %collective-permute-done.2 = bf16[32,8,512]{2,1,0:T(8,128)(2,1)S(1)} collective-permute-done((bf16[32,8,512]{2,1,0:T(8,128)(2,1)S(1)}, bf16[32,8,512]{2,1,0:T(8,128)(2,1)S(1)}, u32[]{:S(2)}, u32[]{:S(2)}) %collective-permute-start.2) | collective-permute-done | bytes 262176 | tf_op jit(solution)/shard_map/ppermute | solution.py:33
  41.0 27.9 %all-to-all-done = f32[8,256,512]{1,2,0:T(8,128)} async-done(((f32[8,256,512]{1,2,0:T(8,128)}), f32[8,256,512]{1,2,0:T(8,128)}, u32[]{:S(2)}, u32[]{:S(2)}) %all-to-all-start) | async-done | bytes 4194336 | tf_op jit(solution)/shard_map/all_to_all | solution.py:85
  68.9 2.5 %reduce_sum.28 = f32[256,512]{0,1:T(8,128)S(1)} reduce(f32[8,256,512]{1,2,0:T(8,128)} %all-to-all-done, f32[]{:T(128)} %constant.180.clone.1), dimensions={0}, to_apply=%region_2.3 | reduce | flops 917504 | bytes 4718596 | tf_op jit(solution)/shard_map/reduce_sum | solution.py:95
  72.3 1.6 pad_maximum_fusion.1
  73.8 4.5 %all-to-all-start.1 = ((f32[8,256,288]{1,2,0:T(8,128)}), f32[8,256,288]{1,2,0:T(8,128)}, u32[]{:S(2)}, u32[]{:S(2)}) async-start(f32[8,256,288]{1,2,0:T(8,128)} %pad_maximum_fusion.1), calls=%async_computation.1 | async-start | bytes 4718592 | tf_op jit(solution)/shard_map/all_to_all | solution.py:102
  78.4 1.8 %maximum_select_fusion.1 = bf16[128,8,512]{2,1,0:T(8,128)(2,1)S(1)} fusion(bf16[64,8,512]{2,1,0:T(8,128)(2,1)} %copy-done.2, bf16[64,8,512]{2,1,0:T(8,128)(2,1)} %collective-permute-done.3, pred[]{:T(512)S(6)} %eq.95), kind=kLoop, calls=%fused_computation.14 | loop fusion | flops 1572864 | bytes 2097153 | tf_op jit(solution)/shard_map/jit(_where)/select_n | solution.py:35
  80.2 3.5 %collective-permute-start.4 = (bf16[128,8,512]{2,1,0:T(8,128)(2,1)S(1)}, bf16[128,8,512]{2,1,0:T(8,128)(2,1)}, u32[]{:S(2)}, u32[]{:S(2)}) collective-permute-start(bf16[128,8,512]{2,1,0:T(8,128)(2,1)S(1)} %maximum_select_fusion.1), channel_id=1, source_target_pairs={{0,8},{8,0},{16,24},{24,16},{32,40},{40,32},{48,56},{56,48},{64,72... | collective-permute-start | bytes 3145736 | tf_op jit(solution)/shard_map/ppermute | solution.py:33
  86.1 1.9 %maximum_select_fusion = bf16[256,8,512]{2,1,0:T(8,128)(2,1)S(1)} fusion(bf16[128,8,512]{2,1,0:T(8,128)(2,1)S(1)} %maximum_select_fusion.1, bf16[128,8,512]{2,1,0:T(8,128)(2,1)} %collective-permute-done.4, pred[]{:T(512)S(6)} %eq.94), kind=kLoop, calls=%fused_computation.8 | loop fusion | flops 3145728 | bytes 4194305 | tf_op jit(solution)/shard_map/jit(_where)/select_n | solution.py:35
  89.3 1.8 %fusion.4 = f32[256,8,256]{2,1,0:T(8,128)} fusion(bf16[256,8,512]{2,1,0:T(8,128)(2,1)S(1)} %maximum_select_fusion, bf16[256,256]{1,0:T(8,128)(2,1)S(1)} %copy-done.3), kind=kOutput, calls=%fused_computation.10 | convolution fusion | flops 268435456 | bytes 3276800 | tf_op jit(solution)/shard_map/qtk,kl->qtl/dot_general | solution.py:87
  91.2 15.0 %all-to-all-done.1 = f32[8,256,288]{1,2,0:T(8,128)} async-done(((f32[8,256,288]{1,2,0:T(8,128)}), f32[8,256,288]{1,2,0:T(8,128)}, u32[]{:S(2)}, u32[]{:S(2)}) %all-to-all-start.1) | async-done | bytes 2359328 | tf_op jit(solution)/shard_map/all_to_all | solution.py:102
  106.2 1.9 %copy.88 = f32[8,36,8,256]{3,2,0,1:T(8,128)S(1)} copy(f32[8,36,8,256]{3,2,1,0:T(8,128)} %bitcast.28) | data formatting | bytes 4718592 | tf_op jit(solution)/shard_map/all_to_all | solution.py:102
  108.7 3.5 %fusion.2 = f32[512,256]{1,0:T(8,128)S(1)} fusion(f32[2048,512]{0,1:T(8,128)S(1)} %bitcast.54, f32[2048,288]{0,1:T(8,128)S(1)} %bitcast.56), kind=kOutput, calls=%fused_computation.6 | convolution fusion | flops 3221225472 | bytes 6815744 | tf_op jit(solution)/shard_map/dot_general | solution.py:116
  112.2 6.5 %collective-permute-start.5 = (f32[32,256]{1,0:T(8,128)S(1)}, f32[32,256]{1,0:T(8,128)S(1)}, u32[]{:S(2)}, u32[]{:S(2)}) collective-permute-start(f32[32,256]{1,0:T(8,128)S(1)} %slice.91), channel_id=1, source_target_pairs={{0,8},{8,16},{16,24},{24,32},{32,40},{40,48},{48,56},{56,64},{64,7... | collective-permute-start | bytes 98312 | tf_op jit(solution)/shard_map/ppermute | solution.py:16
  118.6 8.6 %multiply_convert_fusion = bf16[256,32,256]{2,1,0:T(8,128)(2,1)} fusion(f32[32,256]{1,0:T(8,128)S(1)} %add_divide_fusion, f32[256,8,32]{2,1,0:T(8,128)S(1)} %fusion.6, f32[256,8,256]{2,1,0:T(8,128)S(1)} %copy-done.1), kind=kOutput, calls=%fused_computation | convolution fusion | flops 205520896 | bytes 6586368 | tf_op jit(solution)/shard_map/qti,qtj->qij/dot_general | solution.py:93
  128.5 6.6 %fusion = f32[256,16,1]{1,0,2:T(8,128)S(1)} fusion(bf16[256,32,256]{2,1,0:T(8,128)(2,1)} %multiply_convert_fusion, f32[16,32,256]{2,0,1:T(8,128)S(1)} %scatter-mul.4), kind=kOutput, calls=%fused_computation.3 | convolution fusion | flops 67239936 | bytes 4734976 | tf_op jit(solution)/shard_map/dot_general | solution.py:130
  136.4 3.0 %collective-permute-done.6 = f32[16,257]{1,0:T(8,128)S(1)} collective-permute-done((f32[16,257]{1,0:T(8,128)S(1)}, f32[16,257]{1,0:T(8,128)S(1)}, u32[]{:S(2)}, u32[]{:S(2)}) %collective-permute-start.6) | collective-permute-done | bytes 16480 | tf_op jit(solution)/shard_map/ppermute | solution.py:23
  139.5 2.7 %collective-permute-done.7 = f32[16,257]{1,0:T(8,128)S(1)} collective-permute-done((f32[16,257]{1,0:T(8,128)S(1)}, f32[16,257]{1,0:T(8,128)S(1)}, u32[]{:S(2)}, u32[]{:S(2)}) %collective-permute-start.7) | collective-permute-done | bytes 16480 | tf_op jit(solution)/shard_map/ppermute | solution.py:23
  142.7 3.6 %collective-permute-done.8 = f32[16,257]{1,0:T(8,128)S(1)} collective-permute-done((f32[16,257]{1,0:T(8,128)S(1)}, f32[16,257]{1,0:T(8,128)S(1)}, u32[]{:S(2)}, u32[]{:S(2)}) %collective-permute-start.8) | collective-permute-done | bytes 16480 | tf_op jit(solution)/shard_map/ppermute | solution.py:23
  146.5 6.9 %collective-permute-start.9 = (f32[16,256]{1,0:T(8,128)S(1)}, f32[16,256]{1,0:T(8,128)S(1)}, u32[]{:S(2)}, u32[]{:S(2)}) collective-permute-start(f32[16,256]{1,0:T(8,128)S(1)} %slice_divide_fusion), channel_id=1, source_target_pairs={{0,128},{8,136},{16,144},{24,152},{32,160},{40,168},{48,176},{56,1... | collective-permute-start | bytes 49160 | tf_op jit(solution)/shard_map/ppermute | solution.py:33
  156.0 2.3 %collective-permute-done.10 = f32[32,256]{1,0:T(8,128)S(1)} collective-permute-done((f32[32,256]{1,0:T(8,128)S(1)}, f32[32,256]{1,0:T(8,128)S(1)}, u32[]{:S(2)}, u32[]{:S(2)}) %collective-permute-start.10) | collective-permute-done | bytes 32800 | tf_op jit(solution)/shard_map/ppermute | solution.py:33
  159.2 2.3 %collective-permute-done.11 = f32[64,256]{1,0:T(8,128)S(1)} collective-permute-done((f32[64,256]{1,0:T(8,128)S(1)}, f32[64,256]{1,0:T(8,128)S(1)}, u32[]{:S(2)}, u32[]{:S(2)}) %collective-permute-start.11) | collective-permute-done | bytes 65568 | tf_op jit(solution)/shard_map/ppermute | solution.py:33
  161.6 3.0 %collective-permute-start.12 = (f32[128,256]{1,0:T(8,128)S(1)}, f32[128,256]{1,0:T(8,128)S(1)}, u32[]{:S(2)}, u32[]{:S(2)}) collective-permute-start(f32[128,256]{1,0:T(8,128)S(1)} %maximum_select_fusion.8), channel_id=1, source_target_pairs={{0,16},{8,24},{16,0},{24,8},{32,48},{40,56},{48,32},{56,40},{64,80... | collective-permute-start | bytes 393224 | tf_op jit(solution)/shard_map/ppermute | solution.py:33
  164.6 2.7 %collective-permute-done.12 = f32[128,256]{1,0:T(8,128)S(1)} collective-permute-done((f32[128,256]{1,0:T(8,128)S(1)}, f32[128,256]{1,0:T(8,128)S(1)}, u32[]{:S(2)}, u32[]{:S(2)}) %collective-permute-start.12) | collective-permute-done | bytes 131104 | tf_op jit(solution)/shard_map/ppermute | solution.py:33
  167.2 5.9 %collective-permute-start.13 = (f32[256,256]{1,0:T(8,128)S(1)}, f32[256,256]{1,0:T(8,128)S(1)}, u32[]{:S(2)}, u32[]{:S(2)}) collective-permute-start(f32[256,256]{1,0:T(8,128)S(1)} %maximum_select_fusion.6), channel_id=1, source_target_pairs={{0,8},{8,0},{16,24},{24,16},{32,40},{40,32},{48,56},{56,48},{64,72... | collective-permute-start | bytes 786440 | tf_op jit(solution)/shard_map/ppermute | solution.py:33
  (85 shorter events, 15.0 us)
Async XLA Ops:
  0.0 1.6 copy-start
  0.0 3.3 %copy-start.11 = (bf16[1792,256]{1,0:T(8,128)(2,1)S(1)}, bf16[1792,256]{1,0:T(8,128)(2,1)}, u32[]{:S(2)}) copy-start(bf16[1792,256]{1,0:T(8,128)(2,1)} %param.18) | copy-start | bytes 2752516
  11.1 7.6 %copy-start.5 = (bf16[8,8,256]{2,1,0:T(8,128)(2,1)S(1)}, bf16[8,8,256]{2,1,0:T(8,128)(2,1)}, u32[]{:S(2)}) copy-start(bf16[8,8,256]{2,1,0:T(8,128)(2,1)} %param.23) | copy-start | bytes 98308
  11.1 7.6 %copy-start.6 = (bf16[8,8,256]{2,1,0:T(8,128)(2,1)S(1)}, bf16[8,8,256]{2,1,0:T(8,128)(2,1)}, u32[]{:S(2)}) copy-start(bf16[8,8,256]{2,1,0:T(8,128)(2,1)} %param.24) | copy-start | bytes 98308
  11.1 57.8 %all-to-all-start = ((f32[8,256,512]{1,2,0:T(8,128)}), f32[8,256,512]{1,2,0:T(8,128)}, u32[]{:S(2)}, u32[]{:S(2)}) async-start(f32[8,256,512]{1,2,0:T(8,128)} %bitcast.52), calls=%async_computation | async-start | bytes 8388608 | tf_op jit(solution)/shard_map/all_to_all | solution.py:85
  18.8 8.7 %collective-permute-start = (bf16[8,8,512]{2,1,0:T(8,128)(2,1)S(1)}, bf16[8,8,512]{2,1,0:T(8,128)(2,1)S(1)}, u32[]{:S(2)}, u32[]{:S(2)}) collective-permute-start(bf16[8,8,512]{2,1,0:T(8,128)(2,1)S(1)} %constant_dynamic-update-slice_fusion), channel_id=1, source_target_pairs={{0,128},{8,136},{16,144},{24,152},{32,160},{40,168},{48,176},{56,1... | collective-permute-start | bytes 196616 | tf_op jit(solution)/shard_map/ppermute | solution.py:33
  27.5 7.2 %collective-permute-start.1 = (bf16[16,8,512]{2,1,0:T(8,128)(2,1)S(1)}, bf16[16,8,512]{2,1,0:T(8,128)(2,1)S(1)}, u32[]{:S(2)}, u32[]{:S(2)}) collective-permute-start(bf16[16,8,512]{2,1,0:T(8,128)(2,1)S(1)} %maximum_select_fusion.7), channel_id=1, source_target_pairs={{0,64},{8,72},{16,80},{24,88},{32,96},{40,104},{48,112},{56,120},{... | collective-permute-start | bytes 393224 | tf_op jit(solution)/shard_map/ppermute | solution.py:33
  34.7 5.7 %collective-permute-start.2 = (bf16[32,8,512]{2,1,0:T(8,128)(2,1)S(1)}, bf16[32,8,512]{2,1,0:T(8,128)(2,1)S(1)}, u32[]{:S(2)}, u32[]{:S(2)}) collective-permute-start(bf16[32,8,512]{2,1,0:T(8,128)(2,1)S(1)} %maximum_select_fusion.5), channel_id=1, source_target_pairs={{0,32},{8,40},{16,48},{24,56},{32,0},{40,8},{48,16},{56,24},{64,96... | collective-permute-start | bytes 786440 | tf_op jit(solution)/shard_map/ppermute | solution.py:33
  40.5 30.9 %copy-start.2 = (bf16[64,8,512]{2,1,0:T(8,128)(2,1)}, bf16[64,8,512]{2,1,0:T(8,128)(2,1)S(1)}, u32[]{:S(2)}) copy-start(bf16[64,8,512]{2,1,0:T(8,128)(2,1)S(1)} %maximum_select_fusion.2) | copy-start | bytes 1572868
  40.5 30.9 %copy-start.4 = (bf16[256,256]{1,0:T(8,128)(2,1)S(1)}, bf16[256,256]{1,0:T(8,128)(2,1)}, u32[]{:S(2)}) copy-start(bf16[256,256]{1,0:T(8,128)(2,1)} %param.21) | copy-start | bytes 393220
  40.5 31.2 %copy-start.3 = (bf16[256,256]{1,0:T(8,128)(2,1)S(1)}, bf16[256,256]{1,0:T(8,128)(2,1)}, u32[]{:S(2)}) copy-start(bf16[256,256]{1,0:T(8,128)(2,1)} %param.20) | copy-start | bytes 393220
  40.6 37.8 %collective-permute-start.3 = (bf16[64,8,512]{2,1,0:T(8,128)(2,1)S(1)}, bf16[64,8,512]{2,1,0:T(8,128)(2,1)}, u32[]{:S(2)}, u32[]{:S(2)}) collective-permute-start(bf16[64,8,512]{2,1,0:T(8,128)(2,1)S(1)} %maximum_select_fusion.2), channel_id=1, source_target_pairs={{0,16},{8,24},{16,0},{24,8},{32,48},{40,56},{48,32},{56,40},{64,80... | collective-permute-start | bytes 1572872 | tf_op jit(solution)/shard_map/ppermute | solution.py:33
  73.8 9.8 %copy-start.10 = (s32[1,16]{1,0:T(1,128)S(1)}, s32[1,16]{1,0:T(1,128)}, u32[]{:S(2)}) copy-start(s32[1,16]{1,0:T(1,128)} %param.25) | copy-start | bytes 196
  73.8 10.1 %copy-start.9 = (s32[32]{0:T(128)S(1)}, s32[32]{0:T(128)}, u32[]{:S(2)}) copy-start(s32[32]{0:T(128)} %param.26) | copy-start | bytes 388
  73.8 12.0 %copy-start.7 = (f32[32,256]{1,0:T(8,128)S(1)}, f32[32,256]{1,0:T(8,128)}, u32[]{:S(2)}) copy-start(f32[32,256]{1,0:T(8,128)} %param.22) | copy-start | bytes 98308
  73.8 32.4 %all-to-all-start.1 = ((f32[8,256,288]{1,2,0:T(8,128)}), f32[8,256,288]{1,2,0:T(8,128)}, u32[]{:S(2)}, u32[]{:S(2)}) async-start(f32[8,256,288]{1,2,0:T(8,128)} %pad_maximum_fusion.1), calls=%async_computation.1 | async-start | bytes 4718592 | tf_op jit(solution)/shard_map/all_to_all | solution.py:102
  80.2 5.9 %collective-permute-start.4 = (bf16[128,8,512]{2,1,0:T(8,128)(2,1)S(1)}, bf16[128,8,512]{2,1,0:T(8,128)(2,1)}, u32[]{:S(2)}, u32[]{:S(2)}) collective-permute-start(bf16[128,8,512]{2,1,0:T(8,128)(2,1)S(1)} %maximum_select_fusion.1), channel_id=1, source_target_pairs={{0,8},{8,0},{16,24},{24,16},{32,40},{40,32},{48,56},{56,48},{64,72... | collective-permute-start | bytes 3145736 | tf_op jit(solution)/shard_map/ppermute | solution.py:33
  108.7 10.0 %copy-start.1 = (f32[256,8,256]{2,1,0:T(8,128)S(1)}, f32[256,8,256]{2,1,0:T(8,128)}, u32[]{:S(2)}) copy-start(f32[256,8,256]{2,1,0:T(8,128)} %fusion.4) | copy-start | bytes 6291460
  112.2 15.3 %collective-permute-start.5 = (f32[32,256]{1,0:T(8,128)S(1)}, f32[32,256]{1,0:T(8,128)S(1)}, u32[]{:S(2)}, u32[]{:S(2)}) collective-permute-start(f32[32,256]{1,0:T(8,128)S(1)} %slice.91), channel_id=1, source_target_pairs={{0,8},{8,16},{16,24},{24,32},{32,40},{40,48},{48,56},{56,64},{64,7... | collective-permute-start | bytes 98312 | tf_op jit(solution)/shard_map/ppermute | solution.py:16
  128.5 44.6 %copy-start.8 = (s32[512,1]{0,1:T(1,128)S(1)}, s32[512,1]{0,1:T(1,128)}, u32[]{:S(2)}) copy-start(s32[512,1]{0,1:T(1,128)} %param.27) | copy-start | bytes 6148
  135.2 4.3 %collective-permute-start.6 = (f32[16,257]{1,0:T(8,128)S(1)}, f32[16,257]{1,0:T(8,128)S(1)}, u32[]{:S(2)}, u32[]{:S(2)}) collective-permute-start(f32[16,257]{1,0:T(8,128)S(1)} %pad_maximum_fusion.2), channel_id=1, source_target_pairs={{0,1},{1,0},{2,3},{3,2},{4,5},{5,4},{6,7},{7,6},{8,9},{9,8},{10,11... | collective-permute-start | bytes 49352 | tf_op jit(solution)/shard_map/ppermute | solution.py:23
  139.5 2.7 %collective-permute-start.7 = (f32[16,257]{1,0:T(8,128)S(1)}, f32[16,257]{1,0:T(8,128)S(1)}, u32[]{:S(2)}, u32[]{:S(2)}) collective-permute-start(f32[16,257]{1,0:T(8,128)S(1)} %fusion.36), channel_id=1, source_target_pairs={{0,2},{1,3},{2,0},{3,1},{4,6},{5,7},{6,4},{7,5},{8,10},{9,11},{10,... | collective-permute-start | bytes 49352 | tf_op jit(solution)/shard_map/ppermute | solution.py:23
  142.1 4.2 %collective-permute-start.8 = (f32[16,257]{1,0:T(8,128)S(1)}, f32[16,257]{1,0:T(8,128)S(1)}, u32[]{:S(2)}, u32[]{:S(2)}) collective-permute-start(f32[16,257]{1,0:T(8,128)S(1)} %add.76), channel_id=1, source_target_pairs={{0,4},{1,5},{2,6},{3,7},{4,0},{5,1},{6,2},{7,3},{8,12},{9,13},{10,... | collective-permute-start | bytes 49352 | tf_op jit(solution)/shard_map/ppermute | solution.py:23
  146.5 8.1 %collective-permute-start.9 = (f32[16,256]{1,0:T(8,128)S(1)}, f32[16,256]{1,0:T(8,128)S(1)}, u32[]{:S(2)}, u32[]{:S(2)}) collective-permute-start(f32[16,256]{1,0:T(8,128)S(1)} %slice_divide_fusion), channel_id=1, source_target_pairs={{0,128},{8,136},{16,144},{24,152},{32,160},{40,168},{48,176},{56,1... | collective-permute-start | bytes 49160 | tf_op jit(solution)/shard_map/ppermute | solution.py:33
  154.6 3.7 %collective-permute-start.10 = (f32[32,256]{1,0:T(8,128)S(1)}, f32[32,256]{1,0:T(8,128)S(1)}, u32[]{:S(2)}, u32[]{:S(2)}) collective-permute-start(f32[32,256]{1,0:T(8,128)S(1)} %maximum_select_fusion.10), channel_id=1, source_target_pairs={{0,64},{8,72},{16,80},{24,88},{32,96},{40,104},{48,112},{56,120},{... | collective-permute-start | bytes 98312 | tf_op jit(solution)/shard_map/ppermute | solution.py:33
  158.3 3.2 %collective-permute-start.11 = (f32[64,256]{1,0:T(8,128)S(1)}, f32[64,256]{1,0:T(8,128)S(1)}, u32[]{:S(2)}, u32[]{:S(2)}) collective-permute-start(f32[64,256]{1,0:T(8,128)S(1)} %maximum_select_fusion.9), channel_id=1, source_target_pairs={{0,32},{8,40},{16,48},{24,56},{32,0},{40,8},{48,16},{56,24},{64,96... | collective-permute-start | bytes 196616 | tf_op jit(solution)/shard_map/ppermute | solution.py:33
  161.6 5.7 %collective-permute-start.12 = (f32[128,256]{1,0:T(8,128)S(1)}, f32[128,256]{1,0:T(8,128)S(1)}, u32[]{:S(2)}, u32[]{:S(2)}) collective-permute-start(f32[128,256]{1,0:T(8,128)S(1)} %maximum_select_fusion.8), channel_id=1, source_target_pairs={{0,16},{8,24},{16,0},{24,8},{32,48},{40,56},{48,32},{56,40},{64,80... | collective-permute-start | bytes 393224 | tf_op jit(solution)/shard_map/ppermute | solution.py:33
  167.2 7.0 %collective-permute-start.13 = (f32[256,256]{1,0:T(8,128)S(1)}, f32[256,256]{1,0:T(8,128)S(1)}, u32[]{:S(2)}, u32[]{:S(2)}) collective-permute-start(f32[256,256]{1,0:T(8,128)S(1)} %maximum_select_fusion.6), channel_id=1, source_target_pairs={{0,8},{8,0},{16,24},{24,16},{32,40},{40,32},{48,56},{56,48},{64,72... | collective-permute-start | bytes 786440 | tf_op jit(solution)/shard_map/ppermute | solution.py:33

commit v12 on v7

--- a/solution.py
+++ b/solution.py
@@ -95,13 +95,13 @@
     chunk_sums = jnp.sum(gathered_parts.reshape(factor_count, chunk, rank_in + rank_out), axis=0)
     rot_in_chunk = jnp.dot(chunk_sums[:, :rank_in], basis_in_wide, precision=highest)
     rot_out_chunk = jnp.dot(chunk_sums[:, rank_in:], basis_out_wide, precision=highest)
-    out_blocks = rot_out_chunk.reshape(chunk, factor_count, rank_slice).transpose(1, 0, 2)
+    out_blocks = rot_out_chunk.reshape(chunk, factor_count, rank_slice).transpose(1, 2, 0)
     sending = jnp.concatenate(
-        [jnp.broadcast_to(rot_in_chunk[None], (factor_count, chunk, rank_in)), out_blocks], axis=2
-    ).reshape(factor_count * chunk, rank_in + rank_slice)
+        [jnp.broadcast_to(rot_in_chunk[None], (factor_count, chunk, rank_in)), out_blocks], axis=1
+    )
     received = lax.all_to_all(sending, "factor", 0, 0, tiled=True)
-    rot_in = received[:, :rank_in]
-    rot_out_rows = received[:, rank_in:]
+    rot_in = received[:, :chunk, :].reshape(tokens_here, rank_in)
+    rot_out_cols = received[:, chunk:, :].transpose(1, 0, 2).reshape(rank_slice, tokens_here)
 
     piece_lengths = lengths[0]
     piece_ends = jnp.cumsum(piece_lengths)
@@ -110,10 +110,10 @@
     member = ((position >= piece_starts[None, :]) & (position < piece_ends[None, :])).astype(
         jnp.float32
     )
-    stacked = (member[:, :, None] * rot_out_rows[:, None, :]).reshape(
-        tokens_here, pieces * rank_slice
+    stacked = (member.T[:, None, :] * rot_out_cols[None, :, :]).reshape(
+        pieces * rank_slice, tokens_here
     )
-    grad_rows = lax.dot_general(stacked, rot_in, (((0,), (0,)), ((), ())), precision=highest)
+    grad_rows = jnp.dot(stacked, rot_in, precision=highest)
     grad_rows = grad_rows.reshape(pieces, rank_slice, rank_in)
     preceding = from_behind(grad_rows[pieces - 1], "dp", 1)
     joined_next = jnp.where(data_index < data_count - 1, continues[data_index], 0).astype(

time: 176 us -> 176 us (level)
    all_to_all x1 -> x0, local copies, waits for them, and re-layouts: 1.92 us -> none  [per_device(): received = lax.all_to_all(sending, 'factor', 0, 0, tiled=True)]
  transfers between devices with their start and end apart: 16 -> 16, of which waited for: 14 -> 13; matrix products, arithmetic and copies ran while one was open for 13% -> 12% of each run, Pallas kernels for 0% -> 0%
where the time goes in v12:
time: 176 us
  waiting for transfers between devices  74.9 us (43%)
  starting transfers between devices  50.8 us (29%)
  matrix products  29.5 us (17%)
  other arithmetic  9.71 us (6%)
  local copies, waits for them, and re-layouts  9.04 us (5%)
  between operations  1.88 us (1%)
    ppermute x10, starting transfers between devices, butterfly_gather(): other = lax.ppermute(block, axis, [(i, i ^ step) for i in range(size)])  30.6 us
    all_to_all x1, waiting for transfers between devices, per_device(): gathered_parts = lax.all_to_all(stacked_parts, 'factor', 0, 0, tiled=True)  27.9 us
    ppermute x10, waiting for transfers between devices, butterfly_gather(): other = lax.ppermute(block, axis, [(i, i ^ step) for i in range(size)])  21.9 us
    all_to_all x1, waiting for transfers between devices, per_device(): received = lax.all_to_all(sending, 'factor', 0, 0, tiled=True)  15.8 us
    ppermute x3, waiting for transfers between devices, butterfly_sum(): lax.ppermute(block, axis, [(i, i ^ step) for i in range(size)])  9.32 us
    dot_general x1, matrix products, per_device(): outer = jnp.einsum('qti,qtj->qij', q_out, q_in, precision=highest)  8.55 us
    all_to_all x1, starting transfers between devices, per_device(): gathered_parts = lax.all_to_all(stacked_parts, 'factor', 0, 0, tiled=True)  7.6 us
    dot_general x1, matrix products, per_device(): lax.dot_general(grad_low, query_grad, (((1, 2), (1, 2)), ((), ())), prefe...  6.64 us
  transfers between devices with their start and end apart: 16, of which 13 were waited for; matrix products, arithmetic and copies ran while one was open for 12% of the time, Pallas kernels for 0%

profile of v12, /device:TPU:1, one launch (start us, length us, event | category | flops | bytes accessed | tf_op | source)
XLA Modules:
  0.0 175.9 jit_solution(7346961247546568795)
XLA Ops:
  0.0 1.6 copy-done
  1.6 1.7 fusion.37
  3.3 5.2 %fusion.36 = f32[2048,256]{0,1:T(8,128)S(1)} fusion(bf16[2048,1792]{1,0:T(8,128)(2,1)} %param.16, bf16[1792,256]{1,0:T(8,128)(2,1)S(1)} %copy-done.12), kind=kOutput, calls=%fused_computation.68 | convolution fusion | flops 1879048192 | bytes 10354688 | tf_op jit(solution)/shard_map/dot_general | solution.py:82
  8.8 2.3 %copy.87 = f32[64,8,8,256]{3,2,0,1:T(8,128)} copy(f32[64,8,8,256]{3,2,1,0:T(8,128)S(1)} %bitcast.57) | data formatting | bytes 8388608 | tf_op jit(solution)/shard_map/all_to_all | solution.py:85
  11.1 7.6 %all-to-all-start = ((f32[8,256,512]{1,2,0:T(8,128)}), f32[8,256,512]{1,2,0:T(8,128)}, u32[]{:S(2)}, u32[]{:S(2)}) async-start(f32[8,256,512]{1,2,0:T(8,128)} %bitcast.56), calls=%async_computation | async-start | bytes 8388608 | tf_op jit(solution)/shard_map/all_to_all | solution.py:85
  18.8 7.0 %collective-permute-start = (bf16[8,8,512]{2,1,0:T(8,128)(2,1)S(1)}, bf16[8,8,512]{2,1,0:T(8,128)(2,1)S(1)}, u32[]{:S(2)}, u32[]{:S(2)}) collective-permute-start(bf16[8,8,512]{2,1,0:T(8,128)(2,1)S(1)} %constant_dynamic-update-slice_fusion), channel_id=1, source_target_pairs={{0,128},{8,136},{16,144},{24,152},{32,160},{40,168},{48,176},{56,1... | collective-permute-start | bytes 196616 | tf_op jit(solution)/shard_map/ppermute | solution.py:33
  25.8 1.7 collective-permute-done
  29.0 5.7 %collective-permute-done.1 = bf16[16,8,512]{2,1,0:T(8,128)(2,1)S(1)} collective-permute-done((bf16[16,8,512]{2,1,0:T(8,128)(2,1)S(1)}, bf16[16,8,512]{2,1,0:T(8,128)(2,1)S(1)}, u32[]{:S(2)}, u32[]{:S(2)}) %collective-permute-start.1) | collective-permute-done | bytes 131104 | tf_op jit(solution)/shard_map/ppermute | solution.py:33
  34.9 5.6 %collective-permute-done.2 = bf16[32,8,512]{2,1,0:T(8,128)(2,1)S(1)} collective-permute-done((bf16[32,8,512]{2,1,0:T(8,128)(2,1)S(1)}, bf16[32,8,512]{2,1,0:T(8,128)(2,1)S(1)}, u32[]{:S(2)}, u32[]{:S(2)}) %collective-permute-start.2) | collective-permute-done | bytes 262176 | tf_op jit(solution)/shard_map/ppermute | solution.py:33
  41.0 27.9 %all-to-all-done = f32[8,256,512]{1,2,0:T(8,128)} async-done(((f32[8,256,512]{1,2,0:T(8,128)}), f32[8,256,512]{1,2,0:T(8,128)}, u32[]{:S(2)}, u32[]{:S(2)}) %all-to-all-start) | async-done | bytes 4194336 | tf_op jit(solution)/shard_map/all_to_all | solution.py:85
  68.9 2.5 %reduce_sum.28 = f32[256,512]{0,1:T(8,128)S(1)} reduce(f32[8,256,512]{1,2,0:T(8,128)} %all-to-all-done, f32[]{:T(128)} %constant.180.clone.1), dimensions={0}, to_apply=%region_2.3 | reduce | flops 917504 | bytes 4718596 | tf_op jit(solution)/shard_map/reduce_sum | solution.py:95
  72.3 1.6 pad_maximum_fusion.1
  73.9 4.4 %all-to-all-start.1 = ((f32[8,288,256]{2,1,0:T(8,128)}), f32[8,288,256]{2,1,0:T(8,128)}, u32[]{:S(2)}, u32[]{:S(2)}) async-start(f32[8,288,256]{2,1,0:T(8,128)} %pad_maximum_fusion.1), calls=%async_computation.1 | async-start | bytes 4718592 | tf_op jit(solution)/shard_map/all_to_all | solution.py:102
  78.3 1.8 %maximum_select_fusion.1 = bf16[128,8,512]{2,1,0:T(8,128)(2,1)S(1)} fusion(bf16[64,8,512]{2,1,0:T(8,128)(2,1)} %copy-done.2, bf16[64,8,512]{2,1,0:T(8,128)(2,1)} %collective-permute-done.3, pred[]{:T(512)S(6)} %eq.95), kind=kLoop, calls=%fused_computation.12 | loop fusion | flops 1572864 | bytes 2097153 | tf_op jit(solution)/shard_map/jit(_where)/select_n | solution.py:35
  80.1 3.5 %collective-permute-start.4 = (bf16[128,8,512]{2,1,0:T(8,128)(2,1)S(1)}, bf16[128,8,512]{2,1,0:T(8,128)(2,1)}, u32[]{:S(2)}, u32[]{:S(2)}) collective-permute-start(bf16[128,8,512]{2,1,0:T(8,128)(2,1)S(1)} %maximum_select_fusion.1), channel_id=1, source_target_pairs={{0,8},{8,0},{16,24},{24,16},{32,40},{40,32},{48,56},{56,48},{64,72... | collective-permute-start | bytes 3145736 | tf_op jit(solution)/shard_map/ppermute | solution.py:33
  86.0 1.9 %maximum_select_fusion = bf16[256,8,512]{2,1,0:T(8,128)(2,1)S(1)} fusion(bf16[128,8,512]{2,1,0:T(8,128)(2,1)S(1)} %maximum_select_fusion.1, bf16[128,8,512]{2,1,0:T(8,128)(2,1)} %collective-permute-done.4, pred[]{:T(512)S(6)} %eq.94), kind=kLoop, calls=%fused_computation.6 | loop fusion | flops 3145728 | bytes 4194305 | tf_op jit(solution)/shard_map/jit(_where)/select_n | solution.py:35
  88.4 1.8 %fusion.2 = f32[256,8,256]{2,1,0:T(8,128)} fusion(bf16[256,8,512]{2,1,0:T(8,128)(2,1)S(1)} %maximum_select_fusion, bf16[256,256]{1,0:T(8,128)(2,1)S(1)} %copy-done.3), kind=kOutput, calls=%fused_computation.8 | convolution fusion | flops 268435456 | bytes 3276800 | tf_op jit(solution)/shard_map/qtk,kl->qtl/dot_general | solution.py:87
  90.3 15.8 %all-to-all-done.1 = f32[8,288,256]{2,1,0:T(8,128)} async-done(((f32[8,288,256]{2,1,0:T(8,128)}), f32[8,288,256]{2,1,0:T(8,128)}, u32[]{:S(2)}, u32[]{:S(2)}) %all-to-all-start.1) | async-done | bytes 2359328 | tf_op jit(solution)/shard_map/all_to_all | solution.py:102
  107.6 1.7 slice.89
  109.4 3.4 %fusion.38 = f32[512,256]{1,0:T(8,128)S(1)} fusion(f32[512,2048]{1,0:T(8,128)S(1)} %bitcast.58, f32[2048,256]{1,0:T(8,128)S(1)} %bitcast.59), kind=kOutput, calls=%fused_computation.70 | convolution fusion | flops 3221225472 | bytes 6815744 | tf_op jit(solution)/shard_map/dot_general | solution.py:116
  112.8 6.5 %collective-permute-start.5 = (f32[32,256]{1,0:T(8,128)S(1)}, f32[32,256]{1,0:T(8,128)S(1)}, u32[]{:S(2)}, u32[]{:S(2)}) collective-permute-start(f32[32,256]{1,0:T(8,128)S(1)} %slice.91), channel_id=1, source_target_pairs={{0,8},{8,16},{16,24},{24,32},{32,40},{40,48},{48,56},{56,64},{64,7... | collective-permute-start | bytes 98312 | tf_op jit(solution)/shard_map/ppermute | solution.py:16
  119.3 8.5 %multiply_convert_fusion = bf16[256,32,256]{2,1,0:T(8,128)(2,1)} fusion(f32[32,256]{1,0:T(8,128)S(1)} %add_divide_fusion, f32[256,8,32]{2,1,0:T(8,128)S(1)} %fusion.4, f32[256,8,256]{2,1,0:T(8,128)S(1)} %copy-done.1), kind=kOutput, calls=%fused_computation | convolution fusion | flops 205520896 | bytes 6586368 | tf_op jit(solution)/shard_map/qti,qtj->qij/dot_general | solution.py:93
  129.1 6.6 %fusion = f32[256,16,1]{1,0,2:T(8,128)S(1)} fusion(bf16[256,32,256]{2,1,0:T(8,128)(2,1)} %multiply_convert_fusion, f32[16,32,256]{2,0,1:T(8,128)S(1)} %scatter-mul.4), kind=kOutput, calls=%fused_computation.3 | convolution fusion | flops 67239936 | bytes 4734976 | tf_op jit(solution)/shard_map/dot_general | solution.py:130
  137.1 3.0 %collective-permute-done.6 = f32[16,257]{1,0:T(8,128)S(1)} collective-permute-done((f32[16,257]{1,0:T(8,128)S(1)}, f32[16,257]{1,0:T(8,128)S(1)}, u32[]{:S(2)}, u32[]{:S(2)}) %collective-permute-start.6) | collective-permute-done | bytes 16480 | tf_op jit(solution)/shard_map/ppermute | solution.py:23
  140.1 2.7 %collective-permute-done.7 = f32[16,257]{1,0:T(8,128)S(1)} collective-permute-done((f32[16,257]{1,0:T(8,128)S(1)}, f32[16,257]{1,0:T(8,128)S(1)}, u32[]{:S(2)}, u32[]{:S(2)}) %collective-permute-start.7) | collective-permute-done | bytes 16480 | tf_op jit(solution)/shard_map/ppermute | solution.py:23
  143.4 3.6 %collective-permute-done.8 = f32[16,257]{1,0:T(8,128)S(1)} collective-permute-done((f32[16,257]{1,0:T(8,128)S(1)}, f32[16,257]{1,0:T(8,128)S(1)}, u32[]{:S(2)}, u32[]{:S(2)}) %collective-permute-start.8) | collective-permute-done | bytes 16480 | tf_op jit(solution)/shard_map/ppermute | solution.py:23
  147.2 6.9 %collective-permute-start.9 = (f32[16,256]{1,0:T(8,128)S(1)}, f32[16,256]{1,0:T(8,128)S(1)}, u32[]{:S(2)}, u32[]{:S(2)}) collective-permute-start(f32[16,256]{1,0:T(8,128)S(1)} %slice_divide_fusion), channel_id=1, source_target_pairs={{0,128},{8,136},{16,144},{24,152},{32,160},{40,168},{48,176},{56,1... | collective-permute-start | bytes 49160 | tf_op jit(solution)/shard_map/ppermute | solution.py:33
  156.7 2.3 %collective-permute-done.10 = f32[32,256]{1,0:T(8,128)S(1)} collective-permute-done((f32[32,256]{1,0:T(8,128)S(1)}, f32[32,256]{1,0:T(8,128)S(1)}, u32[]{:S(2)}, u32[]{:S(2)}) %collective-permute-start.10) | collective-permute-done | bytes 32800 | tf_op jit(solution)/shard_map/ppermute | solution.py:33
  159.9 2.3 %collective-permute-done.11 = f32[64,256]{1,0:T(8,128)S(1)} collective-permute-done((f32[64,256]{1,0:T(8,128)S(1)}, f32[64,256]{1,0:T(8,128)S(1)}, u32[]{:S(2)}, u32[]{:S(2)}) %collective-permute-start.11) | collective-permute-done | bytes 65568 | tf_op jit(solution)/shard_map/ppermute | solution.py:33
  162.2 3.0 %collective-permute-start.12 = (f32[128,256]{1,0:T(8,128)S(1)}, f32[128,256]{1,0:T(8,128)S(1)}, u32[]{:S(2)}, u32[]{:S(2)}) collective-permute-start(f32[128,256]{1,0:T(8,128)S(1)} %maximum_select_fusion.8), channel_id=1, source_target_pairs={{0,16},{8,24},{16,0},{24,8},{32,48},{40,56},{48,32},{56,40},{64,80... | collective-permute-start | bytes 393224 | tf_op jit(solution)/shard_map/ppermute | solution.py:33
  165.2 2.7 %collective-permute-done.12 = f32[128,256]{1,0:T(8,128)S(1)} collective-permute-done((f32[128,256]{1,0:T(8,128)S(1)}, f32[128,256]{1,0:T(8,128)S(1)}, u32[]{:S(2)}, u32[]{:S(2)}) %collective-permute-start.12) | collective-permute-done | bytes 131104 | tf_op jit(solution)/shard_map/ppermute | solution.py:33
  167.9 5.9 %collective-permute-start.13 = (f32[256,256]{1,0:T(8,128)S(1)}, f32[256,256]{1,0:T(8,128)S(1)}, u32[]{:S(2)}, u32[]{:S(2)}) collective-permute-start(f32[256,256]{1,0:T(8,128)S(1)} %maximum_select_fusion.6), channel_id=1, source_target_pairs={{0,8},{8,0},{16,24},{24,16},{32,40},{40,32},{48,56},{56,48},{64,72... | collective-permute-start | bytes 786440 | tf_op jit(solution)/shard_map/ppermute | solution.py:33
  (88 shorter events, 15.2 us)
Async XLA Ops:
  0.0 1.6 copy-start
  0.0 3.3 %copy-start.12 = (bf16[1792,256]{1,0:T(8,128)(2,1)S(1)}, bf16[1792,256]{1,0:T(8,128)(2,1)}, u32[]{:S(2)}) copy-start(bf16[1792,256]{1,0:T(8,128)(2,1)} %param.18) | copy-start | bytes 2752516
  11.1 7.6 %copy-start.6 = (bf16[8,8,256]{2,1,0:T(8,128)(2,1)S(1)}, bf16[8,8,256]{2,1,0:T(8,128)(2,1)}, u32[]{:S(2)}) copy-start(bf16[8,8,256]{2,1,0:T(8,128)(2,1)} %param.23) | copy-start | bytes 98308
  11.1 7.6 %copy-start.7 = (bf16[8,8,256]{2,1,0:T(8,128)(2,1)S(1)}, bf16[8,8,256]{2,1,0:T(8,128)(2,1)}, u32[]{:S(2)}) copy-start(bf16[8,8,256]{2,1,0:T(8,128)(2,1)} %param.24) | copy-start | bytes 98308
  11.1 57.8 %all-to-all-start = ((f32[8,256,512]{1,2,0:T(8,128)}), f32[8,256,512]{1,2,0:T(8,128)}, u32[]{:S(2)}, u32[]{:S(2)}) async-start(f32[8,256,512]{1,2,0:T(8,128)} %bitcast.56), calls=%async_computation | async-start | bytes 8388608 | tf_op jit(solution)/shard_map/all_to_all | solution.py:85
  18.8 8.7 %collective-permute-start = (bf16[8,8,512]{2,1,0:T(8,128)(2,1)S(1)}, bf16[8,8,512]{2,1,0:T(8,128)(2,1)S(1)}, u32[]{:S(2)}, u32[]{:S(2)}) collective-permute-start(bf16[8,8,512]{2,1,0:T(8,128)(2,1)S(1)} %constant_dynamic-update-slice_fusion), channel_id=1, source_target_pairs={{0,128},{8,136},{16,144},{24,152},{32,160},{40,168},{48,176},{56,1... | collective-permute-start | bytes 196616 | tf_op jit(solution)/shard_map/ppermute | solution.py:33
  27.5 7.2 %collective-permute-start.1 = (bf16[16,8,512]{2,1,0:T(8,128)(2,1)S(1)}, bf16[16,8,512]{2,1,0:T(8,128)(2,1)S(1)}, u32[]{:S(2)}, u32[]{:S(2)}) collective-permute-start(bf16[16,8,512]{2,1,0:T(8,128)(2,1)S(1)} %maximum_select_fusion.7), channel_id=1, source_target_pairs={{0,64},{8,72},{16,80},{24,88},{32,96},{40,104},{48,112},{56,120},{... | collective-permute-start | bytes 393224 | tf_op jit(solution)/shard_map/ppermute | solution.py:33
  34.7 5.7 %collective-permute-start.2 = (bf16[32,8,512]{2,1,0:T(8,128)(2,1)S(1)}, bf16[32,8,512]{2,1,0:T(8,128)(2,1)S(1)}, u32[]{:S(2)}, u32[]{:S(2)}) collective-permute-start(bf16[32,8,512]{2,1,0:T(8,128)(2,1)S(1)} %maximum_select_fusion.5), channel_id=1, source_target_pairs={{0,32},{8,40},{16,48},{24,56},{32,0},{40,8},{48,16},{56,24},{64,96... | collective-permute-start | bytes 786440 | tf_op jit(solution)/shard_map/ppermute | solution.py:33
  40.5 30.9 %copy-start.2 = (bf16[64,8,512]{2,1,0:T(8,128)(2,1)}, bf16[64,8,512]{2,1,0:T(8,128)(2,1)S(1)}, u32[]{:S(2)}) copy-start(bf16[64,8,512]{2,1,0:T(8,128)(2,1)S(1)} %maximum_select_fusion.2) | copy-start | bytes 1572868
  40.5 30.9 %copy-start.4 = (bf16[256,256]{1,0:T(8,128)(2,1)S(1)}, bf16[256,256]{1,0:T(8,128)(2,1)}, u32[]{:S(2)}) copy-start(bf16[256,256]{1,0:T(8,128)(2,1)} %param.21) | copy-start | bytes 393220
  40.5 31.2 %copy-start.3 = (bf16[256,256]{1,0:T(8,128)(2,1)S(1)}, bf16[256,256]{1,0:T(8,128)(2,1)}, u32[]{:S(2)}) copy-start(bf16[256,256]{1,0:T(8,128)(2,1)} %param.20) | copy-start | bytes 393220
  40.6 37.8 %collective-permute-start.3 = (bf16[64,8,512]{2,1,0:T(8,128)(2,1)S(1)}, bf16[64,8,512]{2,1,0:T(8,128)(2,1)}, u32[]{:S(2)}, u32[]{:S(2)}) collective-permute-start(bf16[64,8,512]{2,1,0:T(8,128)(2,1)S(1)} %maximum_select_fusion.2), channel_id=1, source_target_pairs={{0,16},{8,24},{16,0},{24,8},{32,48},{40,56},{48,32},{56,40},{64,80... | collective-permute-start | bytes 1572872 | tf_op jit(solution)/shard_map/ppermute | solution.py:33
  73.9 32.2 %all-to-all-start.1 = ((f32[8,288,256]{2,1,0:T(8,128)}), f32[8,288,256]{2,1,0:T(8,128)}, u32[]{:S(2)}, u32[]{:S(2)}) async-start(f32[8,288,256]{2,1,0:T(8,128)} %pad_maximum_fusion.1), calls=%async_computation.1 | async-start | bytes 4718592 | tf_op jit(solution)/shard_map/all_to_all | solution.py:102
  78.3 5.3 %copy-start.11 = (s32[1,16]{1,0:T(1,128)S(1)}, s32[1,16]{1,0:T(1,128)}, u32[]{:S(2)}) copy-start(s32[1,16]{1,0:T(1,128)} %param.25) | copy-start | bytes 196
  78.3 5.6 %copy-start.10 = (s32[32]{0:T(128)S(1)}, s32[32]{0:T(128)}, u32[]{:S(2)}) copy-start(s32[32]{0:T(128)} %param.26) | copy-start | bytes 388
  78.3 7.6 %copy-start.8 = (f32[32,256]{1,0:T(8,128)S(1)}, f32[32,256]{1,0:T(8,128)}, u32[]{:S(2)}) copy-start(f32[32,256]{1,0:T(8,128)} %param.22) | copy-start | bytes 98308
  80.1 5.9 %collective-permute-start.4 = (bf16[128,8,512]{2,1,0:T(8,128)(2,1)S(1)}, bf16[128,8,512]{2,1,0:T(8,128)(2,1)}, u32[]{:S(2)}, u32[]{:S(2)}) collective-permute-start(bf16[128,8,512]{2,1,0:T(8,128)(2,1)S(1)} %maximum_select_fusion.1), channel_id=1, source_target_pairs={{0,8},{8,0},{16,24},{24,16},{32,40},{40,32},{48,56},{56,48},{64,72... | collective-permute-start | bytes 3145736 | tf_op jit(solution)/shard_map/ppermute | solution.py:33
  86.0 1.9 %copy-start.5 = (bf16[256,256]{1,0:T(8,128)(2,1)S(1)}, bf16[256,256]{1,0:T(8,128)(2,1)}, u32[]{:S(2)}) copy-start(bf16[256,256]{1,0:T(8,128)(2,1)} %param.21) | copy-start | bytes 393220
  109.4 9.9 %copy-start.1 = (f32[256,8,256]{2,1,0:T(8,128)S(1)}, f32[256,8,256]{2,1,0:T(8,128)}, u32[]{:S(2)}) copy-start(f32[256,8,256]{2,1,0:T(8,128)} %fusion.2) | copy-start | bytes 6291460
  112.8 15.3 %collective-permute-start.5 = (f32[32,256]{1,0:T(8,128)S(1)}, f32[32,256]{1,0:T(8,128)S(1)}, u32[]{:S(2)}, u32[]{:S(2)}) collective-permute-start(f32[32,256]{1,0:T(8,128)S(1)} %slice.91), channel_id=1, source_target_pairs={{0,8},{8,16},{16,24},{24,32},{32,40},{40,48},{48,56},{56,64},{64,7... | collective-permute-start | bytes 98312 | tf_op jit(solution)/shard_map/ppermute | solution.py:16
  129.1 44.6 %copy-start.9 = (s32[512,1]{0,1:T(1,128)S(1)}, s32[512,1]{0,1:T(1,128)}, u32[]{:S(2)}) copy-start(s32[512,1]{0,1:T(1,128)} %param.27) | copy-start | bytes 6148
  135.9 4.3 %collective-permute-start.6 = (f32[16,257]{1,0:T(8,128)S(1)}, f32[16,257]{1,0:T(8,128)S(1)}, u32[]{:S(2)}, u32[]{:S(2)}) collective-permute-start(f32[16,257]{1,0:T(8,128)S(1)} %pad_maximum_fusion.2), channel_id=1, source_target_pairs={{0,1},{1,0},{2,3},{3,2},{4,5},{5,4},{6,7},{7,6},{8,9},{9,8},{10,11... | collective-permute-start | bytes 49352 | tf_op jit(solution)/shard_map/ppermute | solution.py:23
  140.1 2.7 %collective-permute-start.7 = (f32[16,257]{1,0:T(8,128)S(1)}, f32[16,257]{1,0:T(8,128)S(1)}, u32[]{:S(2)}, u32[]{:S(2)}) collective-permute-start(f32[16,257]{1,0:T(8,128)S(1)} %fusion.34), channel_id=1, source_target_pairs={{0,2},{1,3},{2,0},{3,1},{4,6},{5,7},{6,4},{7,5},{8,10},{9,11},{10,... | collective-permute-start | bytes 49352 | tf_op jit(solution)/shard_map/ppermute | solution.py:23
  142.8 4.2 %collective-permute-start.8 = (f32[16,257]{1,0:T(8,128)S(1)}, f32[16,257]{1,0:T(8,128)S(1)}, u32[]{:S(2)}, u32[]{:S(2)}) collective-permute-start(f32[16,257]{1,0:T(8,128)S(1)} %add.76), channel_id=1, source_target_pairs={{0,4},{1,5},{2,6},{3,7},{4,0},{5,1},{6,2},{7,3},{8,12},{9,13},{10,... | collective-permute-start | bytes 49352 | tf_op jit(solution)/shard_map/ppermute | solution.py:23
  147.2 8.1 %collective-permute-start.9 = (f32[16,256]{1,0:T(8,128)S(1)}, f32[16,256]{1,0:T(8,128)S(1)}, u32[]{:S(2)}, u32[]{:S(2)}) collective-permute-start(f32[16,256]{1,0:T(8,128)S(1)} %slice_divide_fusion), channel_id=1, source_target_pairs={{0,128},{8,136},{16,144},{24,152},{32,160},{40,168},{48,176},{56,1... | collective-permute-start | bytes 49160 | tf_op jit(solution)/shard_map/ppermute | solution.py:33
  155.3 3.7 %collective-permute-start.10 = (f32[32,256]{1,0:T(8,128)S(1)}, f32[32,256]{1,0:T(8,128)S(1)}, u32[]{:S(2)}, u32[]{:S(2)}) collective-permute-start(f32[32,256]{1,0:T(8,128)S(1)} %maximum_select_fusion.10), channel_id=1, source_target_pairs={{0,64},{8,72},{16,80},{24,88},{32,96},{40,104},{48,112},{56,120},{... | collective-permute-start | bytes 98312 | tf_op jit(solution)/shard_map/ppermute | solution.py:33
  159.0 3.2 %collective-permute-start.11 = (f32[64,256]{1,0:T(8,128)S(1)}, f32[64,256]{1,0:T(8,128)S(1)}, u32[]{:S(2)}, u32[]{:S(2)}) collective-permute-start(f32[64,256]{1,0:T(8,128)S(1)} %maximum_select_fusion.9), channel_id=1, source_target_pairs={{0,32},{8,40},{16,48},{24,56},{32,0},{40,8},{48,16},{56,24},{64,96... | collective-permute-start | bytes 196616 | tf_op jit(solution)/shard_map/ppermute | solution.py:33
  162.2 5.7 %collective-permute-start.12 = (f32[128,256]{1,0:T(8,128)S(1)}, f32[128,256]{1,0:T(8,128)S(1)}, u32[]{:S(2)}, u32[]{:S(2)}) collective-permute-start(f32[128,256]{1,0:T(8,128)S(1)} %maximum_select_fusion.8), channel_id=1, source_target_pairs={{0,16},{8,24},{16,0},{24,8},{32,48},{40,56},{48,32},{56,40},{64,80... | collective-permute-start | bytes 393224 | tf_op jit(solution)/shard_map/ppermute | solution.py:33
  167.9 7.0 %collective-permute-start.13 = (f32[256,256]{1,0:T(8,128)S(1)}, f32[256,256]{1,0:T(8,128)S(1)}, u32[]{:S(2)}, u32[]{:S(2)}) collective-permute-start(f32[256,256]{1,0:T(8,128)S(1)} %maximum_select_fusion.6), channel_id=1, source_target_pairs={{0,8},{8,0},{16,24},{24,16},{32,40},{40,32},{48,56},{56,48},{64,72... | collective-permute-start | bytes 786440 | tf_op jit(solution)/shard_map/ppermute | solution.py:33
